TPU v7x, 32 devices: a whole 2x2x4 slice. The times are simulated.
32 devices in a mesh: hel: 4 (over y, x), rad: 8 (over z, core).
Axes of the slice: x: 2, y: 2, z: 4, core: 2. Of those that a mesh axis runs over, the one named last changes fastest.
Arguments:
- prev_vector: float32 [16, 256, 16, 512], P('hel', 'rad'), may hold values from -6 to 6
- curr_vector: float32 [16, 256, 16, 512], P('hel', 'rad'), may hold values from -6 to 6
- kinetic_matrix: float32 [256, 256], replicated, may hold values from -0.1875 to 0.1875
- basis_first: float32 [512, 32], replicated, may hold values from -3 to 3
- basis_second: float32 [512, 32], replicated, may hold values from -3 to 3
- chan_table: int32 [512], replicated, may hold values from 0 to 1023, as said below
- potential: float32 [256, 512], P('rad'), may hold values from -0.6 to 0.6
- vib_coupling: float32 [16, 16], replicated, may hold values from -1.5 to 1.5
- vib_energy: float32 [16], replicated, may hold values from -0.4 to 0.4
- coriolis: float32 [16, 512], P('hel'), may hold values from 0.05 to 0.3
- radial_factor: float32 [256], replicated, may hold values from 0.5 to 2
- damping: float32 [256], replicated, may hold values from 0.6 to 1
- stencil: int32 [256], replicated, may hold values from 0 to 252, as said below
- interp_weights: float32 [256, 4], replicated, may hold values from -4 to 4
- frame_rotation: float32 [16, 16], replicated, may hold values from -1.5 to 1.5
Outputs:
- final_vector: float32 [16, 256, 16, 512], P('hel', 'rad')
- product_amp: float32 [16, 256, 16, 512], P('hel', None, None, 'rad')
Inputs may be any that keep to these rules, and one draw needn't show every extreme that they name: Values are distinct; channel c pairs level chan_table[c] // 32 of the first diatom with level chan_table[c] % 32 of the second. `stencil`: non-decreasing along the product points, first value 0, last value 256 - 4.
All inputs are finite; a program needn't handle non-finite values.
Results may differ from a plain program's by a relative error of at most 0.0001.
Values sent between devices are 32-bit elements; how exact they have to be, the bound alone decides.
No kernel may reach another device: no remote copies, remote signals or barrier semaphores. Data moves between devices by JAX's collectives and lax.ppermute only.
A program may use at most 128 MiB of HBM per device.

v0:
```python
import jax
import jax.numpy as jnp
from jax import lax
from jax.sharding import PartitionSpec as P

R = 256
STEPS = 2


PRECISE = lax.Precision.HIGHEST


def shifted(block, axis, distance):
    devices = range(lax.axis_size(axis))
    route = [(i - distance, i) for i in devices if i - distance in devices]
    return lax.ppermute(block, axis, route)


def angular_matrix(basis_first, basis_second, chan_table):
    levels = basis_first.shape[1]
    level_grid = jnp.arange(levels, dtype=jnp.int32)
    first_hot = (chan_table[None, :] // levels == level_grid[:, None]).astype(jnp.float32)
    second_hot = (chan_table[None, :] % levels == level_grid[:, None]).astype(jnp.float32)
    first_part = jnp.dot(
        basis_first, first_hot, precision=PRECISE, preferred_element_type=jnp.float32
    )
    second_part = jnp.dot(
        basis_second, second_hot, precision=PRECISE, preferred_element_type=jnp.float32
    )
    return first_part * second_part


def interp_matrix(stencil, interp_weights, radial_count):
    offsets = jnp.arange(4, dtype=jnp.int32)
    points = jnp.arange(radial_count, dtype=jnp.int32)
    matches = (points[None, None, :] == (stencil[:, None] + offsets[None, :])[:, :, None]).astype(
        jnp.float32
    )
    return jnp.sum(matches * interp_weights[:, :, None], axis=1)


def shards(
    prev_vector,
    curr_vector,
    kinetic_matrix,
    basis_first,
    basis_second,
    chan_table,
    potential,
    vib_coupling,
    vib_energy,
    coriolis,
    radial_factor,
    damping,
    stencil,
    interp_weights,
    frame_rotation,
):
    heli_local, rad_local, vib_count, chan_count = curr_vector.shape
    chan_local = chan_count // lax.axis_size("rad")
    rad_index = lax.axis_index("rad")
    radial_local = lax.dynamic_slice_in_dim(radial_factor, rad_index * rad_local, rad_local)
    damping_local = lax.dynamic_slice_in_dim(damping, rad_index * rad_local, rad_local)
    damp_full = damping_local[None, :, None, None]
    transform = angular_matrix(basis_first, basis_second, chan_table)
    earlier = prev_vector
    current = curr_vector
    for iteration in range(STEPS):
        kinetic_radial_block = lax.all_to_all(
            current, "rad", split_axis=3, concat_axis=1, tiled=True
        )
        kinetic_merged = kinetic_radial_block.reshape(
            kinetic_radial_block.shape[0], kinetic_radial_block.shape[1], -1
        )
        applied = jnp.einsum(
            "rs,ksm->krm",
            kinetic_matrix,
            kinetic_merged,
            precision=PRECISE,
            preferred_element_type=jnp.float32,
        )
        kinetic_image = lax.all_to_all(
            applied.reshape(kinetic_radial_block.shape),
            "rad",
            split_axis=1,
            concat_axis=3,
            tiled=True,
        )
        flattened = current.reshape(-1, chan_count)
        angles = jnp.dot(
            flattened, transform.T, precision=PRECISE, preferred_element_type=jnp.float32
        )
        angles = angles.reshape(heli_local, rad_local, vib_count, -1)
        angles = jnp.einsum(
            "uv,krva->krua",
            vib_coupling,
            angles,
            precision=PRECISE,
            preferred_element_type=jnp.float32,
        )
        angles = angles * potential[None, :, None, :]
        angular = jnp.dot(
            angles.reshape(-1, angles.shape[3]),
            transform,
            precision=PRECISE,
            preferred_element_type=jnp.float32,
        )
        weighted = coriolis[:, None, None, :] * current
        from_above = shifted(current[:1], "hel", -1)
        from_below = shifted(weighted[-1:], "hel", 1)
        upper_side = jnp.concatenate([current[1:], from_above], axis=0)
        lower_side = jnp.concatenate([from_below, weighted[:-1]], axis=0)
        image = (
            kinetic_image
            + (angular.reshape(current.shape) + vib_energy[None, None, :, None] * current)
            + radial_local[None, :, None, None]
            * (coriolis[:, None, None, :] * upper_side + lower_side)
        )
        following = damp_full * (2.0 * image - damp_full * earlier)
        earlier = current
        current = following
    interp = interp_matrix(stencil, interp_weights, R)
    radial_block = lax.all_to_all(current, "rad", split_axis=3, concat_axis=1, tiled=True)
    merged = radial_block.reshape(radial_block.shape[0], radial_block.shape[1], -1)
    placed = jnp.einsum(
        "qr,krm->kqm", interp, merged, precision=PRECISE, preferred_element_type=jnp.float32
    )
    turned = jnp.einsum(
        "jk,kqm->jqm",
        frame_rotation,
        lax.all_to_all(placed, "hel", split_axis=1, concat_axis=0, tiled=True),
        precision=PRECISE,
        preferred_element_type=jnp.float32,
    )
    rotated = lax.all_to_all(turned, "hel", split_axis=0, concat_axis=1, tiled=True)
    product_amp = rotated.reshape(heli_local, rotated.shape[1], vib_count, chan_local)
    return (current, product_amp)


def solution(mesh):
    in_specs = (
        P("hel", "rad", None, None),
        P("hel", "rad", None, None),
        P(),
        P(),
        P(),
        P(),
        P("rad", None),
        P(),
        P(),
        P("hel", None),
        P(),
        P(),
        P(),
        P(),
        P(),
    )
    out_specs = (P("hel", "rad", None, None), P("hel", None, None, "rad"))
    return jax.shard_map(shards, mesh=mesh, in_specs=in_specs, out_specs=out_specs, check_vma=False)
```

profile of v0, /device:TPU:0, one launch (start us, length us, event | category | flops | bytes accessed | tf_op | source)
XLA Modules:
  0.0 1054.5 jit_solution(1805130596638117278)
XLA Ops:
  0.6 14.4 %copy.86 = f32[4,32,16,512]{1,2,0,3:T(8,128)} copy(f32[4,32,16,512]{3,2,1,0:T(8,128)} %param.16) | data formatting | bytes 8388608 | tf_op args[1]
  27.9 100.5 %all_to_all.114 = f32[8,1,131072]{2,1,0:T(1,128)} all-to-all(f32[8,1,131072]{2,1,0:T(1,128)} %reshape.110), channel_id=1, replica_groups=mesh['hel'=4,'rad'=8] {'rad'}, dimensions={0} | all-to-all | bytes 8388608 | tf_op jit(solution)/shard_map/all_to_all | solution.py:69
  128.9 13.7 %reduce = f32[8,131072]{1,0:T(8,128)} reduce(f32[8,1,131072]{2,1,0:T(1,128)} %all_to_all.114, f32[]{:T(128)} %broadcast.70), dimensions={1}, to_apply=%all_to_all.83.reduce_sub_computation | reduce | bytes 8388612 | tf_op jit(solution)/shard_map/all_to_all | solution.py:69
  142.6 13.4 %reshape.111 = f32[512,4,16,32]{3,2,1,0:T(8,128)} reshape(f32[8,131072]{1,0:T(8,128)} %reduce) | data formatting | bytes 8388608
  156.0 13.9 %copy.87 = f32[4,32,16,8,64]{4,2,1,3,0:T(8,128)} copy(f32[4,32,16,8,64]{1,2,0,4,3:T(8,128)} %bitcast.110) | data formatting | bytes 8388608 | tf_op jit(solution)/shard_map/all_to_all | solution.py:69
  227.9 16.5 %convolution_bitcast_fusion = f32[2048,512]{0,1:T(8,128)} fusion(f32[512,512]{1,0:T(8,128)S(1)} %convolution_multiply_fusion, f32[2048,512]{1,0:T(8,128)} %bitcast.109), kind=kOutput, calls=%fused_computation.21 | convolution fusion | flops 6442450944 | bytes 9437184 | tf_op jit(solution)/shard_map/dot_general | solution.py:90
  258.3 48.3 %all-to-all-done.1 = f32[8,1,131072]{2,1,0:T(1,128)} async-done(((f32[8,1,131072]{2,1,0:T(1,128)}), f32[8,1,131072]{2,1,0:T(1,128)}, u32[]{:S(2)}, u32[]{:S(2)}) %all-to-all-start.1) | async-done | bytes 4194336 | tf_op jit(solution)/shard_map/all_to_all | solution.py:82
  306.6 13.9 %reduce.1 = f32[8,131072]{1,0:T(8,128)} reduce(f32[8,1,131072]{2,1,0:T(1,128)} %all-to-all-done.1, f32[]{:T(128)} %broadcast.70), dimensions={1}, to_apply=%all_to_all.86.reduce_sub_computation | reduce | bytes 8388612 | tf_op jit(solution)/shard_map/all_to_all | solution.py:82
  348.4 15.8 %broadcast_multiply_fusion = (f32[4,32,16,512]{3,2,1,0:T(8,128)}, f32[4,32,16,512]{3,2,1,0:T(8,128)}) fusion(f32[4,512]{1,0:T(4,128)S(1)} %copy-done.6, f32[4,32,16,512]{3,2,1,0:T(8,128)} %param.15, f32[3,32,16,512]{3,2,1,0:T(8,128)} %slice.33, f32[1,32,16,512]{3,2,1,0:T(8,128)S(1)} %collective-permute-done.1, ...), kind=kOutput, calls=%fused_computation.24 | convolution fusion | flops 6458179584 | bytes 34677056 | tf_op jit(solution)/shard_map/dot_general | solution.py:102
  364.2 14.4 %copy.93 = f32[4,32,16,512]{1,2,0,3:T(8,128)} copy(f32[4,32,16,512]{3,2,1,0:T(8,128)} %get-tuple-element.13) | data formatting | bytes 8388608 | tf_op jit(solution)/shard_map/mul | solution.py:119
  391.4 98.7 %all_to_all.115 = f32[8,1,131072]{2,1,0:T(1,128)} all-to-all(f32[8,1,131072]{2,1,0:T(1,128)} %reshape.114), channel_id=1, replica_groups=mesh['hel'=4,'rad'=8] {'rad'}, dimensions={0} | all-to-all | bytes 8388608 | tf_op jit(solution)/shard_map/all_to_all | solution.py:69
  490.1 13.7 %reduce.2 = f32[8,131072]{1,0:T(8,128)} reduce(f32[8,1,131072]{2,1,0:T(1,128)} %all_to_all.115, f32[]{:T(128)} %broadcast.70), dimensions={1}, to_apply=%all_to_all.90.reduce_sub_computation | reduce | bytes 8388612 | tf_op jit(solution)/shard_map/all_to_all | solution.py:69
  503.8 13.3 %reshape.115 = f32[512,4,16,32]{3,2,1,0:T(8,128)} reshape(f32[8,131072]{1,0:T(8,128)} %reduce.2) | data formatting | bytes 8388608
  517.1 13.9 %copy.94 = f32[4,32,16,8,64]{4,2,1,3,0:T(8,128)} copy(f32[4,32,16,8,64]{1,2,0,4,3:T(8,128)} %bitcast.111) | data formatting | bytes 8388608 | tf_op jit(solution)/shard_map/all_to_all | solution.py:69
  601.2 66.1 %all-to-all-done.3 = f32[8,1,131072]{2,1,0:T(1,128)} async-done(((f32[8,1,131072]{2,1,0:T(1,128)}), f32[8,1,131072]{2,1,0:T(1,128)}, u32[]{:S(2)}, u32[]{:S(2)}) %all-to-all-start.3) | async-done | bytes 4194336 | tf_op jit(solution)/shard_map/all_to_all | solution.py:82
  667.2 13.9 %reduce.3 = f32[8,131072]{1,0:T(8,128)} reduce(f32[8,1,131072]{2,1,0:T(1,128)} %all-to-all-done.3, f32[]{:T(128)} %broadcast.70), dimensions={1}, to_apply=%all_to_all.93.reduce_sub_computation | reduce | bytes 8388612 | tf_op jit(solution)/shard_map/all_to_all | solution.py:82
  708.7 14.7 %fusion.11 = f32[4,32,16,512]{3,2,1,0:T(8,128)} fusion(f32[1,32,16,512]{3,2,1,0:T(8,128)S(1)} %collective-permute-done.2, f32[3,32,16,512]{3,2,1,0:T(8,128)} %slice.34, f32[3,32,16,512]{3,2,1,0:T(8,128)} %slice.37, f32[1,32,16,512]{3,2,1,0:T(8,128)S(1)} %collective-permute-done.3, f32[4,32,16,512]{3,2,1,0:T(8,128)} %param.16, ...), kind=kOutput, calls=%fused_computation.13 | convolution fusion | flops 6457131008 | bytes 30482752 | tf_op jit(solution)/shard_map/dot_general | solution.py:102
  723.4 14.4 %copy.99 = f32[4,32,16,512]{1,2,0,3:T(8,128)} copy(f32[4,32,16,512]{3,2,1,0:T(8,128)} %fusion.11) | data formatting | bytes 8388608 | tf_op jit(solution)/shard_map/mul | solution.py:119
  756.0 93.6 %all-to-all-done.4 = f32[8,1,131072]{2,1,0:T(1,128)} async-done(((f32[8,1,131072]{2,1,0:T(1,128)}), f32[8,1,131072]{2,1,0:T(1,128)}, u32[]{:S(2)}, u32[]{:S(2)}) %all-to-all-start.4) | async-done | bytes 4194336 | tf_op jit(solution)/shard_map/all_to_all | solution.py:123
  849.6 13.7 %reduce.4 = f32[8,131072]{1,0:T(8,128)} reduce(f32[8,1,131072]{2,1,0:T(1,128)} %all-to-all-done.4, f32[]{:T(128)} %broadcast.70), dimensions={1}, to_apply=%all_to_all.97.reduce_sub_computation | reduce | bytes 8388612 | tf_op jit(solution)/shard_map/all_to_all | solution.py:123
  863.4 13.4 %reshape.119 = f32[512,4,16,32]{3,2,1,0:T(8,128)} reshape(f32[8,131072]{1,0:T(8,128)} %reduce.4) | data formatting | bytes 8388608
  876.7 13.9 %copy.100 = f32[4,32,16,8,64]{4,2,1,3,0:T(8,128)} copy(f32[4,32,16,8,64]{1,2,0,4,3:T(8,128)} %bitcast.112) | data formatting | bytes 8388608 | tf_op jit(solution)/shard_map/all_to_all | solution.py:123
  915.1 51.9 %all_to_all.116 = f32[4,256,1024]{2,0,1:T(4,128)S(1)} all-to-all(f32[4,256,1024]{2,0,1:T(4,128)} %copy.102), channel_id=1, replica_groups=mesh['hel'=4,'rad'=8] {'hel'}, dimensions={1} | all-to-all | bytes 8388608 | tf_op jit(solution)/shard_map/all_to_all | solution.py:131
  987.9 49.2 %all_to_all.117 = f32[16,64,1024]{2,1,0:T(8,128)S(1)} all-to-all(f32[16,64,1024]{2,1,0:T(8,128)S(1)} %copy.105), channel_id=1, replica_groups=mesh['hel'=4,'rad'=8] {'hel'}, dimensions={0} | all-to-all | bytes 8388608 | tf_op jit(solution)/shard_map/all_to_all | solution.py:135
  (94 shorter events, 304.1 us)
Async XLA Ops:
  0.6 177.4 %copy-start = (f32[256,256]{1,0:T(8,128)S(1)}, f32[256,256]{1,0:T(8,128)}, u32[]{:S(2)}) copy-start(f32[256,256]{1,0:T(8,128)} %param.17) | copy-start | bytes 786436
  207.9 4.7 copy-start.6
  207.9 98.7 %all-to-all-start.1 = ((f32[8,1,131072]{2,1,0:T(1,128)}), f32[8,1,131072]{2,1,0:T(1,128)}, u32[]{:S(2)}, u32[]{:S(2)}) async-start(f32[8,1,131072]{2,1,0:T(1,128)} %reshape.112), calls=%async_computation.1 | async-start | bytes 8388608 | tf_op jit(solution)/shard_map/all_to_all | solution.py:82
  212.6 7.4 copy-start.2
  216.5 131.8 %collective-permute-start.1 = (f32[1,32,16,512]{3,2,1,0:T(8,128)}, f32[1,32,16,512]{3,2,1,0:T(8,128)S(1)}, u32[]{:S(2)}, u32[]{:S(2)}) collective-permute-start(f32[1,32,16,512]{3,2,1,0:T(8,128)} %slice.32), channel_id=1, source_target_pairs={{0,8},{8,16},{16,24},{1,9},{9,17},{17,25},{2,10},{10,18},{18,26},{... | collective-permute-start | bytes 3145736 | tf_op jit(solution)/shard_map/ppermute | solution.py:16
  221.1 127.3 %collective-permute-start = (f32[1,32,16,512]{3,2,1,0:T(8,128)}, f32[1,32,16,512]{3,2,1,0:T(8,128)S(1)}, u32[]{:S(2)}, u32[]{:S(2)}) collective-permute-start(f32[1,32,16,512]{3,2,1,0:T(8,128)} %slice.25), channel_id=1, source_target_pairs={{8,0},{16,8},{24,16},{9,1},{17,9},{25,17},{10,2},{18,10},{26,18},{... | collective-permute-start | bytes 3145736 | tf_op jit(solution)/shard_map/ppermute | solution.py:16
  224.4 2.1 copy-start.15
  224.4 2.1 copy-start.16
  224.4 2.2 copy-start.12
  224.4 2.2 copy-start.7
  224.4 2.9 copy-start.8
  244.5 5.4 copy-start.9
  340.9 7.5 copy-start.5
  340.9 7.5 copy-start.13
  568.6 98.6 %all-to-all-start.3 = ((f32[8,1,131072]{2,1,0:T(1,128)}), f32[8,1,131072]{2,1,0:T(1,128)}, u32[]{:S(2)}, u32[]{:S(2)}) async-start(f32[8,1,131072]{2,1,0:T(1,128)} %reshape.116), calls=%async_computation.3 | async-start | bytes 8388608 | tf_op jit(solution)/shard_map/all_to_all | solution.py:82
  573.2 11.3 %copy-start.3 = (f32[4,32,16,512]{3,2,1,0:T(8,128)S(1)}, f32[4,32,16,512]{3,2,1,0:T(8,128)}, u32[]{:S(2)}) copy-start(f32[4,32,16,512]{3,2,1,0:T(8,128)} %get-tuple-element.13) | copy-start | bytes 12582916
  575.7 133.0 %collective-permute-start.2 = (f32[1,32,16,512]{3,2,1,0:T(8,128)}, f32[1,32,16,512]{3,2,1,0:T(8,128)S(1)}, u32[]{:S(2)}, u32[]{:S(2)}) collective-permute-start(f32[1,32,16,512]{3,2,1,0:T(8,128)} %slice.35), channel_id=1, source_target_pairs={{8,0},{16,8},{24,16},{9,1},{17,9},{25,17},{10,2},{18,10},{26,18},{... | collective-permute-start | bytes 3145736 | tf_op jit(solution)/shard_map/ppermute | solution.py:16
  577.0 9.5 copy-start.4
  579.5 129.3 %collective-permute-start.3 = (f32[1,32,16,512]{3,2,1,0:T(8,128)}, f32[1,32,16,512]{3,2,1,0:T(8,128)S(1)}, u32[]{:S(2)}, u32[]{:S(2)}) collective-permute-start(f32[1,32,16,512]{3,2,1,0:T(8,128)} %slice.36), channel_id=1, source_target_pairs={{0,8},{8,16},{16,24},{1,9},{9,17},{17,25},{2,10},{10,18},{18,26},{... | collective-permute-start | bytes 3145736 | tf_op jit(solution)/shard_map/ppermute | solution.py:16
  750.7 5.0 copy-start.14
  750.7 5.0 copy-start.11
  750.7 99.0 %all-to-all-start.4 = ((f32[8,1,131072]{2,1,0:T(1,128)}), f32[8,1,131072]{2,1,0:T(1,128)}, u32[]{:S(2)}, u32[]{:S(2)}) async-start(f32[8,1,131072]{2,1,0:T(1,128)} %reshape.118), calls=%async_computation.4 | async-start | bytes 8388608 | tf_op jit(solution)/shard_map/all_to_all | solution.py:123
  974.1 5.3 copy-start.10
  1039.4 15.0 %copy-start.1 = (f32[256,256]{1,0:T(8,128)S(1)}, f32[256,256]{1,0:T(8,128)}, u32[]{:S(2)}) copy-start(f32[256,256]{1,0:T(8,128)} %param.17) | copy-start | bytes 786436
where the time goes:
time: 1070 us; the launch traced here: 1050 us
  local copies, waits for them, and re-layouts  340 us (32%)
  blocking collectives  300 us (28%)
  waiting for transfers between devices  208 us (19%)
  matrix products  108 us (10%)
  other arithmetic  72.3 us (7%)
  starting transfers between devices  25.3 us (2%)
    all_to_all x2, blocking collectives, shards(): lax.all_to_all(current, 'rad', split_axis=3, concat_axis=1, tiled=True)  199 us
    unnamed x46, local copies, waits for them, and re-layouts  138 us
    all_to_all x2, waiting for transfers between devices, shards(): lax.all_to_all(applied.reshape(kinetic_radial_block.shape), 'rad', split_...  114 us
    all_to_all x1, waiting for transfers between devices, shards(): lax.all_to_all(current, 'rad', split_axis=3, concat_axis=1, tiled=True)  93.6 us
    all_to_all x1, blocking collectives, shards(): lax.all_to_all(placed, 'hel', split_axis=1, concat_axis=0, tiled=True)  51.9 us
    all_to_all x1, blocking collectives, shards(): lax.all_to_all(turned, 'hel', split_axis=0, concat_axis=1, tiled=True)  49.2 us
    all_to_all x4, local copies, waits for them, and re-layouts, shards(): lax.all_to_all(current, 'rad', split_axis=3, concat_axis=1, tiled=True)  42.4 us
    all_to_all x3, other arithmetic, shards(): lax.all_to_all(current, 'rad', split_axis=3, concat_axis=1, tiled=True)  41.2 us
  transfers between devices with their start and end apart: 7, of which 3 were waited for; matrix products, arithmetic and copies ran while one was open for 12% of the time, Pallas kernels for 0%

commit v1 on v0

v1 whole, which is shorter than its diff:
```python
import jax
import jax.numpy as jnp
from jax import lax
from jax.sharding import PartitionSpec as P

STEPS = 2
PRECISE = lax.Precision.HIGHEST


def shifted(block, axis, distance):
    devices = range(lax.axis_size(axis))
    route = [(i - distance, i) for i in devices if i - distance in devices]
    return lax.ppermute(block, axis, route)


def angular_matrix(basis_first, basis_second, chan_table):
    levels = basis_first.shape[1]
    level_grid = jnp.arange(levels, dtype=jnp.int32)
    first_hot = (chan_table[None, :] // levels == level_grid[:, None]).astype(jnp.float32)
    second_hot = (chan_table[None, :] % levels == level_grid[:, None]).astype(jnp.float32)
    first_part = jnp.dot(
        basis_first, first_hot, precision=PRECISE, preferred_element_type=jnp.float32
    )
    second_part = jnp.dot(
        basis_second, second_hot, precision=PRECISE, preferred_element_type=jnp.float32
    )
    return first_part * second_part


def interp_matrix(stencil, interp_weights, radial_count):
    offsets = jnp.arange(4, dtype=jnp.int32)
    points = jnp.arange(radial_count, dtype=jnp.int32)
    matches = (points[None, None, :] == (stencil[:, None] + offsets[None, :])[:, :, None]).astype(
        jnp.float32
    )
    return jnp.sum(matches * interp_weights[:, :, None], axis=1)


def exchange(piece_for, place, out, axis):
    n = lax.axis_size(axis)
    me = lax.axis_index(axis)
    out = place(out, piece_for(me), me)
    for d in range(1, n):
        dest = lax.rem(me + d, n)
        src = lax.rem(me + n - d, n)
        got = lax.ppermute(piece_for(dest), axis, [(i, (i + d) % n) for i in range(n)])
        out = place(out, got, src)
    return out


def shards(
    prev_vector,
    curr_vector,
    kinetic_matrix,
    basis_first,
    basis_second,
    chan_table,
    potential,
    vib_coupling,
    vib_energy,
    coriolis,
    radial_factor,
    damping,
    stencil,
    interp_weights,
    frame_rotation,
):
    kl, rl, vc, cc = curr_vector.shape
    n = lax.axis_size("rad")
    nh = lax.axis_size("hel")
    radial = rl * n
    mb = vc * cc // n
    cb = cc // n
    rad_index = lax.axis_index("rad")
    radial_local = lax.dynamic_slice_in_dim(radial_factor, rad_index * rl, rl)
    damping_local = lax.dynamic_slice_in_dim(damping, rad_index * rl, rl)
    damp_full = damping_local[None, :, None, None]
    transform = angular_matrix(basis_first, basis_second, chan_table)
    vib_batched = jnp.broadcast_to(vib_coupling, (kl * rl, vc, vc))

    def to_radial_columns(x):
        blocks = x.reshape(kl, rl, n, mb)

        def piece_for(dest):
            part = lax.dynamic_index_in_dim(blocks, dest, axis=2, keepdims=False)
            return jnp.transpose(part, (1, 0, 2))

        def place(out, piece, src):
            return lax.dynamic_update_slice_in_dim(out, piece, src * rl, axis=0)

        return exchange(piece_for, place, jnp.zeros((radial, kl, mb), x.dtype), "rad")

    def to_radial_rows(y):
        def piece_for(dest):
            part = lax.dynamic_slice_in_dim(y, dest * rl, rl, axis=0)
            return jnp.transpose(part, (1, 0, 2))

        def place(out, piece, src):
            return lax.dynamic_update_slice_in_dim(out, piece[:, :, None, :], src, axis=2)

        out = exchange(piece_for, place, jnp.zeros((kl, rl, n, mb), y.dtype), "rad")
        return out.reshape(kl, rl, vc, cc)

    def hamiltonian(current):
        columns = to_radial_columns(current)
        applied = jnp.dot(
            kinetic_matrix,
            columns.reshape(radial, kl * mb),
            precision=PRECISE,
            preferred_element_type=jnp.float32,
        )
        kinetic_image = to_radial_rows(applied.reshape(radial, kl, mb))
        angles = jnp.dot(
            current.reshape(-1, cc), transform.T, precision=PRECISE,
            preferred_element_type=jnp.float32,
        )
        angles = jnp.einsum(
            "buv,bva->bua",
            vib_batched,
            angles.reshape(kl * rl, vc, -1),
            precision=PRECISE,
            preferred_element_type=jnp.float32,
        )
        angles = angles.reshape(kl, rl, vc, -1) * potential[None, :, None, :]
        angular = jnp.dot(
            angles.reshape(-1, angles.shape[3]),
            transform,
            precision=PRECISE,
            preferred_element_type=jnp.float32,
        )
        weighted = coriolis[:, None, None, :] * current
        from_above = shifted(current[:1], "hel", -1)
        from_below = shifted(weighted[-1:], "hel", 1)
        upper_side = jnp.concatenate([current[1:], from_above], axis=0)
        lower_side = jnp.concatenate([from_below, weighted[:-1]], axis=0)
        return (
            kinetic_image
            + (angular.reshape(current.shape) + vib_energy[None, None, :, None] * current)
            + radial_local[None, :, None, None]
            * (coriolis[:, None, None, :] * upper_side + lower_side)
        )

    earlier = prev_vector
    current = curr_vector
    for iteration in range(STEPS):
        image = hamiltonian(current)
        following = damp_full * (2.0 * image - damp_full * earlier)
        earlier = current
        current = following

    chans = current.reshape(kl, rl, vc, n, cb)

    def chan_piece(dest):
        part = lax.dynamic_index_in_dim(chans, dest, axis=3, keepdims=False)
        return jnp.transpose(part, (1, 0, 2, 3))

    def chan_place(out, piece, src):
        return lax.dynamic_update_slice_in_dim(out, piece, src * rl, axis=0)

    radial_block = exchange(
        chan_piece, chan_place, jnp.zeros((radial, kl, vc, cb), current.dtype), "rad"
    )
    interp = interp_matrix(stencil, interp_weights, radial)
    qq = interp.shape[0]
    qb = qq // nh
    width = vc * cb
    placed = jnp.dot(
        interp,
        radial_block.reshape(radial, kl * width),
        precision=PRECISE,
        preferred_element_type=jnp.float32,
    ).reshape(qq, kl, width)

    def hel_piece(dest):
        part = lax.dynamic_slice_in_dim(placed, dest * qb, qb, axis=0)
        return jnp.transpose(part, (1, 0, 2))

    def hel_place(out, piece, src):
        return lax.dynamic_update_slice_in_dim(out, piece, src * kl, axis=0)

    gathered = exchange(
        hel_piece, hel_place, jnp.zeros((kl * nh, qb, width), placed.dtype), "hel"
    )
    turned = jnp.dot(
        frame_rotation,
        gathered.reshape(kl * nh, qb * width),
        precision=PRECISE,
        preferred_element_type=jnp.float32,
    ).reshape(kl * nh, qb, width)

    def back_piece(dest):
        return lax.dynamic_slice_in_dim(turned, dest * kl, kl, axis=0)

    def back_place(out, piece, src):
        return lax.dynamic_update_slice_in_dim(out, piece, src * qb, axis=1)

    rotated = exchange(back_piece, back_place, jnp.zeros((kl, qq, width), turned.dtype), "hel")
    product_amp = rotated.reshape(kl, qq, vc, cb)
    return (current, product_amp)


def solution(mesh):
    in_specs = (
        P("hel", "rad", None, None),
        P("hel", "rad", None, None),
        P(),
        P(),
        P(),
        P(),
        P("rad", None),
        P(),
        P(),
        P("hel", None),
        P(),
        P(),
        P(),
        P(),
        P(),
    )
    out_specs = (P("hel", "rad", None, None), P("hel", None, None, "rad"))
    return jax.shard_map(shards, mesh=mesh, in_specs=in_specs, out_specs=out_specs, check_vma=False)
```

time: 1070 us -> 1310 us (1.22)
  the two profiles are of different devices: /device:TPU:0 before, /device:TPU:17 now
where the time goes in v1:
time: 1310 us; the launch traced here: 1290 us
  local copies, waits for them, and re-layouts  795 us (61%)
  waiting for transfers between devices  282 us (22%)
  starting transfers between devices  105 us (8%)
  matrix products  75.1 us (6%)
  other arithmetic  27.8 us (2%)
    ppermute x41, waiting for transfers between devices, exchange(): lax.ppermute(piece_for(dest), axis, [(i, (i + d) % n) for i in range(n)])  282 us
    dynamic_update_slice x16, local copies, waits for them, and re-layouts, place(): return lax.dynamic_update_slice_in_dim(out, piece, src * rl, axis=0)  180 us
    dynamic_update_slice x16, local copies, waits for them, and re-layouts, place(): lax.dynamic_update_slice_in_dim(out, piece[:, :, None, :], src, axis=2)  176 us
    dynamic_update_slice x8, local copies, waits for them, and re-layouts, chan_place(): return lax.dynamic_update_slice_in_dim(out, piece, src * rl, axis=0)  116 us
    ppermute x41, starting transfers between devices, exchange(): lax.ppermute(piece_for(dest), axis, [(i, (i + d) % n) for i in range(n)])  92.5 us
    unnamed x88, local copies, waits for them, and re-layouts  67.1 us
    dynamic_update_slice x4, local copies, waits for them, and re-layouts, back_place(): return lax.dynamic_update_slice_in_dim(out, piece, src * qb, axis=1)  43.4 us
    ppermute x24, local copies, waits for them, and re-layouts, exchange(): lax.ppermute(piece_for(dest), axis, [(i, (i + d) % n) for i in range(n)])  39.3 us
  transfers between devices with their start and end apart: 45, of which 11 were waited for; matrix products, arithmetic and copies ran while one was open for 55% of the time, Pallas kernels for 0%

profile of v1, /device:TPU:17, one launch (start us, length us, event | category | flops | bytes accessed | tf_op | source)
XLA Modules:
  0.0 1286.7 jit_solution(16918266247473385818)
XLA Ops:
  5.9 17.2 %constant_dynamic-slice_fusion.35 = (f32[4,32,1,1024]{3,2,1,0:T(1,128)S(1)}, f32[4,32,1,1024]{3,2,1,0:T(1,128)S(1)}, f32[4,32,1,1024]{3,2,1,0:T(1,128)S(1)}, f32...) fusion(f32[4,32,8,1024]{3,2,1,0:T(8,128)} %reshape.126, ...), kind=kLoop, calls=%fused_computation.98 | loop fusion | bytes 8388640 | tf_op jit(solution)/shard_map/jit(dynamic_index_in_dim)/dynamic_slice | solution.py:85
  81.1 12.0 dynamic_update_slice.146
  102.2 12.0 dynamic_update_slice.147
  209.8 14.8 %convolution_bitcast_fusion = f32[2048,512]{0,1:T(8,128)} fusion(f32[512,512]{1,0:T(8,128)S(1)} %convolution_multiply_fusion, f32[2048,512]{1,0:T(8,128)S(1)} %bitcast.217), kind=kOutput, calls=%fused_computation.18 | convolution fusion | flops 6442450944 | bytes 9437184 | tf_op jit(solution)/shard_map/dot_general | solution.py:113
  371.1 13.3 %broadcast_multiply_fusion = (f32[4,32,16,512]{3,2,1,0:T(8,128)}, f32[4,32,16,512]{3,2,1,0:T(8,128)}) fusion(f32[4,512]{1,0:T(4,128)S(1)} %copy-done.17, f32[4,32,16,512]{3,2,1,0:T(8,128)} %param.15, f32[3,32,16,512]{3,2,1,0:T(8,128)} %slice.33, f32[1,32,16,512]{3,2,1,0:T(8,128)} %collective-permute-done.15, f32[1,32,16,512]{3,2,1,0:T(8,128)} %collective-permute-done.14, ...), kind=kLoop, calls=%fused_computation.19 | loop fusion | flops 14680064 | bytes 33562944 | tf_op jit(solution)/shard_map/mul | solution.py:131
  389.7 17.4 %constant_dynamic-slice_fusion.20 = (f32[4,32,1,1024]{3,2,1,0:T(1,128)S(1)}, f32[4,32,1,1024]{3,2,1,0:T(1,128)S(1)}, f32[4,32,1,1024]{3,2,1,0:T(1,128)S(1)}, f32...) fusion(f32[4,32,8,1024]{3,2,1,0:T(8,128)} %reshape.133, ...), kind=kLoop, calls=%fused_computation.83 | loop fusion | bytes 8388640 | tf_op jit(solution)/shard_map/jit(dynamic_index_in_dim)/dynamic_slice | solution.py:85
  409.3 28.4 %collective-permute-start.17 = (f32[32,4,1024]{2,0,1:T(8,128)S(1)}, f32[32,4,1024]{2,0,1:T(8,128)S(1)}, u32[]{:S(2)}, u32[]{:S(2)}) collective-permute-start(f32[32,4,1024]{2,0,1:T(8,128)S(1)} %bitcast.248), channel_id=1, source_target_pairs={{0,2},{1,3},{2,4},{3,5},{4,6},{5,7},{6,0},{7,1},{8,10},{9,11},{10,... | collective-permute-start | bytes 1572872 | tf_op jit(solution)/shard_map/ppermute | solution.py:46
  445.5 56.3 %collective-permute-done.17 = f32[32,4,1024]{2,0,1:T(8,128)S(1)} collective-permute-done((f32[32,4,1024]{2,0,1:T(8,128)S(1)}, f32[32,4,1024]{2,0,1:T(8,128)S(1)}, u32[]{:S(2)}, u32[]{:S(2)}) %collective-permute-start.17) | collective-permute-done | bytes 524320 | tf_op jit(solution)/shard_map/ppermute | solution.py:46
  530.8 12.0 dynamic_update_slice.162
  544.5 12.0 dynamic_update_slice.163
  558.2 12.0 dynamic_update_slice.164
  666.5 20.5 %collective-permute-done.25 = f32[4,32,1024]{2,1,0:T(8,128)} collective-permute-done((f32[4,32,1024]{2,1,0:T(8,128)}, f32[4,32,1024]{2,1,0:T(8,128)}, u32[]{:S(2)}, u32[]{:S(2)}) %collective-permute-start.25) | collective-permute-done | bytes 524320 | tf_op jit(solution)/shard_map/ppermute | solution.py:46
  831.9 26.8 %constant_dynamic-slice_fusion.4 = (f32[4,32,16,1,64]{4,3,2,1,0:T(1,128)}, f32[4,32,16,1,64]{4,3,2,1,0:T(1,128)}, f32[4,32,16,1,64]{4,3,2,1,0:T(1,128)}, f32[4,3...) fusion(f32[4,32,16,8,64]{4,3,2,1,0:T(8,128)} %reshape.138, ...), kind=kLoop, calls=%fused_computation.67 | loop fusion | bytes 8388640 | tf_op jit(solution)/shard_map/jit(dynamic_index_in_dim)/dynamic_slice | solution.py:154
  858.7 17.8 %collective-permute-start.32 = (f32[32,4,16,64]{3,2,0,1:T(8,128)S(1)}, f32[32,4,16,64]{3,2,0,1:T(8,128)}, u32[]{:S(2)}, u32[]{:S(2)}) collective-permute-start(f32[32,4,16,64]{3,2,0,1:T(8,128)S(1)} %bitcast.237), channel_id=1, source_target_pairs={{0,1},{1,2},{2,3},{3,4},{4,5},{5,6},{6,7},{7,0},{8,9},{9,10},{10,1... | collective-permute-start | bytes 1572872 | tf_op jit(solution)/shard_map/ppermute | solution.py:46
  882.4 15.2 %collective-permute-done.32 = f32[32,4,16,64]{3,2,0,1:T(8,128)} collective-permute-done((f32[32,4,16,64]{3,2,0,1:T(8,128)S(1)}, f32[32,4,16,64]{3,2,0,1:T(8,128)}, u32[]{:S(2)}, u32[]{:S(2)}) %collective-permute-start.32) | collective-permute-done | bytes 524320 | tf_op jit(solution)/shard_map/ppermute | solution.py:46
  899.5 112.9 %collective-permute-done.33 = f32[32,4,16,64]{3,2,0,1:T(8,128)} collective-permute-done((f32[32,4,16,64]{3,2,0,1:T(8,128)S(1)}, f32[32,4,16,64]{3,2,0,1:T(8,128)}, u32[]{:S(2)}, u32[]{:S(2)}) %collective-permute-start.33) | collective-permute-done | bytes 524320 | tf_op jit(solution)/shard_map/ppermute | solution.py:46
  1016.0 15.8 %dynamic_update_slice.176 = f32[256,4,16,64]{0,3,2,1:T(8,128)} dynamic-update-slice(f32[256,4,16,64]{0,3,2,1:T(8,128)} %broadcast_in_dim.99, f32[32,4,16,64]{0,3,2,1:T(8,128)S(1)} %copy.255, s32[]{:T(128)S(6)} %select_n.162, s32[]{:T(128)} %constant.162.clone.1, s32[]{:T(128)} %constant.162.clone.1, s32[]{:T(128)} %constant.162.clone.1) | dynamic-update-slice | bytes 1048580 | tf_op jit(solution)/shard_map/dynamic_update_slice | solution.py:158
  1045.3 16.2 %dynamic_update_slice.178 = f32[256,4,16,64]{0,3,2,1:T(8,128)} dynamic-update-slice(f32[256,4,16,64]{0,3,2,1:T(8,128)} %dynamic_update_slice.177, f32[32,4,16,64]{0,3,2,1:T(8,128)S(1)} %copy.259, s32[]{:T(128)S(6)} %select_n.167, s32[]{:T(128)} %constant.162.clone.1, s32[]{:T(128)} %constant.162.clone.1, s32[]{:T(128)} %constant.162.clone.1) | dynamic-update-slice | bytes 1048580 | tf_op jit(solution)/shard_map/dynamic_update_slice | solution.py:158
  1063.4 16.2 %dynamic_update_slice.179 = f32[256,4,16,64]{0,3,2,1:T(8,128)} dynamic-update-slice(f32[256,4,16,64]{0,3,2,1:T(8,128)} %dynamic_update_slice.178, f32[32,4,16,64]{0,3,2,1:T(8,128)S(1)} %copy.261, s32[]{:T(128)S(6)} %select_n.169, s32[]{:T(128)} %constant.162.clone.1, s32[]{:T(128)} %constant.162.clone.1, s32[]{:T(128)} %constant.162.clone.1) | dynamic-update-slice | bytes 1048580 | tf_op jit(solution)/shard_map/dynamic_update_slice | solution.py:158
  1081.5 16.2 %dynamic_update_slice.180 = f32[256,4,16,64]{0,3,2,1:T(8,128)} dynamic-update-slice(f32[256,4,16,64]{0,3,2,1:T(8,128)} %dynamic_update_slice.179, f32[32,4,16,64]{0,3,2,1:T(8,128)S(1)} %copy.263, s32[]{:T(128)S(6)} %select_n.171, s32[]{:T(128)} %constant.162.clone.1, s32[]{:T(128)} %constant.162.clone.1, s32[]{:T(128)} %constant.162.clone.1) | dynamic-update-slice | bytes 1048580 | tf_op jit(solution)/shard_map/dynamic_update_slice | solution.py:158
  1112.0 15.4 %dynamic_update_slice.182 = f32[256,4,16,64]{0,3,2,1:T(8,128)} dynamic-update-slice(f32[256,4,16,64]{0,3,2,1:T(8,128)} %dynamic_update_slice.181, f32[32,4,16,64]{0,3,2,1:T(8,128)S(1)} %copy.267, s32[]{:T(128)S(6)} %select_n.175, s32[]{:T(128)} %constant.162.clone.1, s32[]{:T(128)} %constant.162.clone.1, s32[]{:T(128)} %constant.162.clone.1) | dynamic-update-slice | bytes 1048580 | tf_op jit(solution)/shard_map/dynamic_update_slice | solution.py:158
  1129.3 15.4 %dynamic_update_slice.183 = f32[256,4,16,64]{0,3,2,1:T(8,128)} dynamic-update-slice(f32[256,4,16,64]{0,3,2,1:T(8,128)} %dynamic_update_slice.182, f32[32,4,16,64]{0,3,2,1:T(8,128)S(1)} %copy.269, s32[]{:T(128)S(6)} %select_n.177, s32[]{:T(128)} %constant.162.clone.1, s32[]{:T(128)} %constant.162.clone.1, s32[]{:T(128)} %constant.162.clone.1) | dynamic-update-slice | bytes 1048580 | tf_op jit(solution)/shard_map/dynamic_update_slice | solution.py:158
  1158.4 21.8 %collective-permute-done.39 = f32[4,64,1024]{2,1,0:T(8,128)S(1)} collective-permute-done((f32[4,64,1024]{2,1,0:T(8,128)}, f32[4,64,1024]{2,1,0:T(8,128)S(1)}, u32[]{:S(2)}, u32[]{:S(2)}) %collective-permute-start.39) | collective-permute-done | bytes 1048608 | tf_op jit(solution)/shard_map/ppermute | solution.py:46
  1180.3 21.4 %collective-permute-done.40 = f32[4,64,1024]{2,1,0:T(8,128)S(1)} collective-permute-done((f32[4,64,1024]{2,1,0:T(8,128)}, f32[4,64,1024]{2,1,0:T(8,128)S(1)}, u32[]{:S(2)}, u32[]{:S(2)}) %collective-permute-start.40) | collective-permute-done | bytes 1048608 | tf_op jit(solution)/shard_map/ppermute | solution.py:46
  (293 shorter events, 745.9 us)
Async XLA Ops:
  27.7 68.6 %collective-permute-start.2 = (f32[32,4,1024]{2,0,1:T(8,128)}, f32[32,4,1024]{2,0,1:T(8,128)}, u32[]{:S(2)}, u32[]{:S(2)}) collective-permute-start(f32[32,4,1024]{2,0,1:T(8,128)} %bitcast.207), channel_id=1, source_target_pairs={{0,3},{1,4},{2,5},{3,6},{4,7},{5,0},{6,1},{7,2},{8,11},{9,12},{10,... | collective-permute-start | bytes 1572872 | tf_op jit(solution)/shard_map/ppermute | solution.py:46
  28.9 85.3 %collective-permute-start.3 = (f32[32,4,1024]{2,0,1:T(8,128)}, f32[32,4,1024]{2,0,1:T(8,128)}, u32[]{:S(2)}, u32[]{:S(2)}) collective-permute-start(f32[32,4,1024]{2,0,1:T(8,128)} %bitcast.206), channel_id=1, source_target_pairs={{0,4},{1,5},{2,6},{3,7},{4,0},{5,1},{6,2},{7,3},{8,12},{9,13},{10,... | collective-permute-start | bytes 1572872 | tf_op jit(solution)/shard_map/ppermute | solution.py:46
  32.1 95.7 %collective-permute-start.4 = (f32[32,4,1024]{2,0,1:T(8,128)}, f32[32,4,1024]{2,0,1:T(8,128)}, u32[]{:S(2)}, u32[]{:S(2)}) collective-permute-start(f32[32,4,1024]{2,0,1:T(8,128)} %bitcast.205), channel_id=1, source_target_pairs={{0,5},{1,6},{2,7},{3,0},{4,1},{5,2},{6,3},{7,4},{8,13},{9,14},{10,... | collective-permute-start | bytes 1572872 | tf_op jit(solution)/shard_map/ppermute | solution.py:46
  37.4 102.6 %collective-permute-start.5 = (f32[32,4,1024]{2,0,1:T(8,128)}, f32[32,4,1024]{2,0,1:T(8,128)S(1)}, u32[]{:S(2)}, u32[]{:S(2)}) collective-permute-start(f32[32,4,1024]{2,0,1:T(8,128)} %bitcast.204), channel_id=1, source_target_pairs={{0,6},{1,7},{2,0},{3,1},{4,2},{5,3},{6,4},{7,5},{8,14},{9,15},{10,... | collective-permute-start | bytes 1572872 | tf_op jit(solution)/shard_map/ppermute | solution.py:46
  48.7 103.2 %collective-permute-start.6 = (f32[32,4,1024]{2,0,1:T(8,128)}, f32[32,4,1024]{2,0,1:T(8,128)S(1)}, u32[]{:S(2)}, u32[]{:S(2)}) collective-permute-start(f32[32,4,1024]{2,0,1:T(8,128)} %bitcast.203), channel_id=1, source_target_pairs={{0,7},{1,0},{2,1},{3,2},{4,3},{5,4},{6,5},{7,6},{8,15},{9,8},{10,9... | collective-permute-start | bytes 1572872 | tf_op jit(solution)/shard_map/ppermute | solution.py:46
  96.3 274.8 %collective-permute-start.15 = (f32[1,32,16,512]{3,2,1,0:T(8,128)}, f32[1,32,16,512]{3,2,1,0:T(8,128)}, u32[]{:S(2)}, u32[]{:S(2)}) collective-permute-start(f32[1,32,16,512]{3,2,1,0:T(8,128)} %slice.32), channel_id=1, source_target_pairs={{0,8},{8,16},{16,24},{1,9},{9,17},{17,25},{2,10},{10,18},{18,26},{... | collective-permute-start | bytes 3145736 | tf_op jit(solution)/shard_map/ppermute | solution.py:13
  208.1 162.9 %collective-permute-start.14 = (f32[1,32,16,512]{3,2,1,0:T(8,128)}, f32[1,32,16,512]{3,2,1,0:T(8,128)}, u32[]{:S(2)}, u32[]{:S(2)}) collective-permute-start(f32[1,32,16,512]{3,2,1,0:T(8,128)} %slice.25), channel_id=1, source_target_pairs={{8,0},{16,8},{24,16},{9,1},{17,9},{25,17},{10,2},{18,10},{26,18},{... | collective-permute-start | bytes 3145736 | tf_op jit(solution)/shard_map/ppermute | solution.py:13
  409.3 92.5 %collective-permute-start.17 = (f32[32,4,1024]{2,0,1:T(8,128)S(1)}, f32[32,4,1024]{2,0,1:T(8,128)S(1)}, u32[]{:S(2)}, u32[]{:S(2)}) collective-permute-start(f32[32,4,1024]{2,0,1:T(8,128)S(1)} %bitcast.248), channel_id=1, source_target_pairs={{0,2},{1,3},{2,4},{3,5},{4,6},{5,7},{6,0},{7,1},{8,10},{9,11},{10,... | collective-permute-start | bytes 1572872 | tf_op jit(solution)/shard_map/ppermute | solution.py:46
  438.6 104.3 %collective-permute-start.18 = (f32[32,4,1024]{2,0,1:T(8,128)}, f32[32,4,1024]{2,0,1:T(8,128)}, u32[]{:S(2)}, u32[]{:S(2)}) collective-permute-start(f32[32,4,1024]{2,0,1:T(8,128)} %bitcast.214), channel_id=1, source_target_pairs={{0,3},{1,4},{2,5},{3,6},{4,7},{5,0},{6,1},{7,2},{8,11},{9,12},{10,... | collective-permute-start | bytes 1572872 | tf_op jit(solution)/shard_map/ppermute | solution.py:46
  439.5 117.0 %collective-permute-start.19 = (f32[32,4,1024]{2,0,1:T(8,128)}, f32[32,4,1024]{2,0,1:T(8,128)}, u32[]{:S(2)}, u32[]{:S(2)}) collective-permute-start(f32[32,4,1024]{2,0,1:T(8,128)} %bitcast.213), channel_id=1, source_target_pairs={{0,4},{1,5},{2,6},{3,7},{4,0},{5,1},{6,2},{7,3},{8,12},{9,13},{10,... | collective-permute-start | bytes 1572872 | tf_op jit(solution)/shard_map/ppermute | solution.py:46
  440.4 129.8 %collective-permute-start.20 = (f32[32,4,1024]{2,0,1:T(8,128)}, f32[32,4,1024]{2,0,1:T(8,128)}, u32[]{:S(2)}, u32[]{:S(2)}) collective-permute-start(f32[32,4,1024]{2,0,1:T(8,128)} %bitcast.212), channel_id=1, source_target_pairs={{0,5},{1,6},{2,7},{3,0},{4,1},{5,2},{6,3},{7,4},{8,13},{9,14},{10,... | collective-permute-start | bytes 1572872 | tf_op jit(solution)/shard_map/ppermute | solution.py:46
  444.0 138.4 %collective-permute-start.21 = (f32[32,4,1024]{2,0,1:T(8,128)}, f32[32,4,1024]{2,0,1:T(8,128)}, u32[]{:S(2)}, u32[]{:S(2)}) collective-permute-start(f32[32,4,1024]{2,0,1:T(8,128)} %bitcast.211), channel_id=1, source_target_pairs={{0,6},{1,7},{2,0},{3,1},{4,2},{5,3},{6,4},{7,5},{8,14},{9,15},{10,... | collective-permute-start | bytes 1572872 | tf_op jit(solution)/shard_map/ppermute | solution.py:46
  501.8 93.6 %collective-permute-start.22 = (f32[32,4,1024]{2,0,1:T(8,128)}, f32[32,4,1024]{2,0,1:T(8,128)}, u32[]{:S(2)}, u32[]{:S(2)}) collective-permute-start(f32[32,4,1024]{2,0,1:T(8,128)} %bitcast.210), channel_id=1, source_target_pairs={{0,7},{1,0},{2,1},{3,2},{4,3},{5,4},{6,5},{7,6},{8,15},{9,8},{10,9... | collective-permute-start | bytes 1572872 | tf_op jit(solution)/shard_map/ppermute | solution.py:46
  639.0 174.4 %collective-permute-start.30 = (f32[1,32,16,512]{3,2,1,0:T(8,128)}, f32[1,32,16,512]{3,2,1,0:T(8,128)}, u32[]{:S(2)}, u32[]{:S(2)}) collective-permute-start(f32[1,32,16,512]{3,2,1,0:T(8,128)} %slice.35), channel_id=1, source_target_pairs={{8,0},{16,8},{24,16},{9,1},{17,9},{25,17},{10,2},{18,10},{26,18},{... | collective-permute-start | bytes 3145736 | tf_op jit(solution)/shard_map/ppermute | solution.py:13
  642.6 170.8 %collective-permute-start.31 = (f32[1,32,16,512]{3,2,1,0:T(8,128)}, f32[1,32,16,512]{3,2,1,0:T(8,128)}, u32[]{:S(2)}, u32[]{:S(2)}) collective-permute-start(f32[1,32,16,512]{3,2,1,0:T(8,128)} %slice.36), channel_id=1, source_target_pairs={{0,8},{8,16},{16,24},{1,9},{9,17},{17,25},{2,10},{10,18},{18,26},{... | collective-permute-start | bytes 3145736 | tf_op jit(solution)/shard_map/ppermute | solution.py:13
  664.9 106.2 %collective-permute-start.27 = (f32[4,32,1024]{2,1,0:T(8,128)}, f32[4,32,1024]{2,1,0:T(8,128)}, u32[]{:S(2)}, u32[]{:S(2)}) collective-permute-start(f32[4,32,1024]{2,1,0:T(8,128)} %bitcast.240), channel_id=1, source_target_pairs={{0,5},{1,6},{2,7},{3,0},{4,1},{5,2},{6,3},{7,4},{8,13},{9,14},{10,... | collective-permute-start | bytes 1572872 | tf_op jit(solution)/shard_map/ppermute | solution.py:46
  687.0 96.4 %collective-permute-start.28 = (f32[4,32,1024]{2,1,0:T(8,128)}, f32[4,32,1024]{2,1,0:T(8,128)}, u32[]{:S(2)}, u32[]{:S(2)}) collective-permute-start(f32[4,32,1024]{2,1,0:T(8,128)} %bitcast.239), channel_id=1, source_target_pairs={{0,6},{1,7},{2,0},{3,1},{4,2},{5,3},{6,4},{7,5},{8,14},{9,15},{10,... | collective-permute-start | bytes 1572872 | tf_op jit(solution)/shard_map/ppermute | solution.py:46
  687.9 107.9 %collective-permute-start.29 = (f32[4,32,1024]{2,1,0:T(8,128)}, f32[4,32,1024]{2,1,0:T(8,128)}, u32[]{:S(2)}, u32[]{:S(2)}) collective-permute-start(f32[4,32,1024]{2,1,0:T(8,128)} %bitcast.238), channel_id=1, source_target_pairs={{0,7},{1,0},{2,1},{3,2},{4,3},{5,4},{6,5},{7,6},{8,15},{9,8},{10,9... | collective-permute-start | bytes 1572872 | tf_op jit(solution)/shard_map/ppermute | solution.py:46
  876.4 136.0 %collective-permute-start.33 = (f32[32,4,16,64]{3,2,0,1:T(8,128)S(1)}, f32[32,4,16,64]{3,2,0,1:T(8,128)}, u32[]{:S(2)}, u32[]{:S(2)}) collective-permute-start(f32[32,4,16,64]{3,2,0,1:T(8,128)S(1)} %bitcast.236), channel_id=1, source_target_pairs={{0,2},{1,3},{2,4},{3,5},{4,6},{5,7},{6,0},{7,1},{8,10},{9,11},{10,... | collective-permute-start | bytes 1572872 | tf_op jit(solution)/shard_map/ppermute | solution.py:46
  880.6 181.0 %collective-permute-start.34 = (f32[32,4,16,64]{3,2,0,1:T(8,128)}, f32[32,4,16,64]{3,2,0,1:T(8,128)}, u32[]{:S(2)}, u32[]{:S(2)}) collective-permute-start(f32[32,4,16,64]{3,2,0,1:T(8,128)} %bitcast.77), channel_id=1, source_target_pairs={{0,3},{1,4},{2,5},{3,6},{4,7},{5,0},{6,1},{7,2},{8,11},{9,12},{10,... | collective-permute-start | bytes 1572872 | tf_op jit(solution)/shard_map/ppermute | solution.py:46
  880.6 199.1 %collective-permute-start.35 = (f32[32,4,16,64]{3,2,0,1:T(8,128)}, f32[32,4,16,64]{3,2,0,1:T(8,128)}, u32[]{:S(2)}, u32[]{:S(2)}) collective-permute-start(f32[32,4,16,64]{3,2,0,1:T(8,128)} %bitcast.79), channel_id=1, source_target_pairs={{0,4},{1,5},{2,6},{3,7},{4,0},{5,1},{6,2},{7,3},{8,12},{9,13},{10,... | collective-permute-start | bytes 1572872 | tf_op jit(solution)/shard_map/ppermute | solution.py:46
  880.6 217.2 %collective-permute-start.36 = (f32[32,4,16,64]{3,2,0,1:T(8,128)}, f32[32,4,16,64]{3,2,0,1:T(8,128)}, u32[]{:S(2)}, u32[]{:S(2)}) collective-permute-start(f32[32,4,16,64]{3,2,0,1:T(8,128)} %bitcast.81), channel_id=1, source_target_pairs={{0,5},{1,6},{2,7},{3,0},{4,1},{5,2},{6,3},{7,4},{8,13},{9,14},{10,... | collective-permute-start | bytes 1572872 | tf_op jit(solution)/shard_map/ppermute | solution.py:46
  897.6 212.5 %collective-permute-start.37 = (f32[32,4,16,64]{3,2,0,1:T(8,128)}, f32[32,4,16,64]{3,2,0,1:T(8,128)}, u32[]{:S(2)}, u32[]{:S(2)}) collective-permute-start(f32[32,4,16,64]{3,2,0,1:T(8,128)} %bitcast.83), channel_id=1, source_target_pairs={{0,6},{1,7},{2,0},{3,1},{4,2},{5,3},{6,4},{7,5},{8,14},{9,15},{10,... | collective-permute-start | bytes 1572872 | tf_op jit(solution)/shard_map/ppermute | solution.py:46
  1012.4 115.0 %collective-permute-start.38 = (f32[32,4,16,64]{3,2,0,1:T(8,128)}, f32[32,4,16,64]{3,2,0,1:T(8,128)}, u32[]{:S(2)}, u32[]{:S(2)}) collective-permute-start(f32[32,4,16,64]{3,2,0,1:T(8,128)} %bitcast.85), channel_id=1, source_target_pairs={{0,7},{1,0},{2,1},{3,2},{4,3},{5,4},{6,5},{7,6},{8,15},{9,8},{10,9... | collective-permute-start | bytes 1572872 | tf_op jit(solution)/shard_map/ppermute | solution.py:46
  (49 other events, 1654.0 us)

commit v2 on v1

--- a/solution.py
+++ b/solution.py
@@ -36,18 +36,6 @@
     return jnp.sum(matches * interp_weights[:, :, None], axis=1)
 
 
-def exchange(piece_for, place, out, axis):
-    n = lax.axis_size(axis)
-    me = lax.axis_index(axis)
-    out = place(out, piece_for(me), me)
-    for d in range(1, n):
-        dest = lax.rem(me + d, n)
-        src = lax.rem(me + n - d, n)
-        got = lax.ppermute(piece_for(dest), axis, [(i, (i + d) % n) for i in range(n)])
-        out = place(out, got, src)
-    return out
-
-
 def shards(
     prev_vector,
     curr_vector,
@@ -78,38 +66,28 @@
     transform = angular_matrix(basis_first, basis_second, chan_table)
     vib_batched = jnp.broadcast_to(vib_coupling, (kl * rl, vc, vc))
 
+    kinetic_batched = jnp.broadcast_to(kinetic_matrix, (kl, radial, radial))
+
     def to_radial_columns(x):
-        blocks = x.reshape(kl, rl, n, mb)
-
-        def piece_for(dest):
-            part = lax.dynamic_index_in_dim(blocks, dest, axis=2, keepdims=False)
-            return jnp.transpose(part, (1, 0, 2))
-
-        def place(out, piece, src):
-            return lax.dynamic_update_slice_in_dim(out, piece, src * rl, axis=0)
-
-        return exchange(piece_for, place, jnp.zeros((radial, kl, mb), x.dtype), "rad")
+        blocks = jnp.transpose(x.reshape(kl, rl, n, mb), (2, 0, 1, 3))
+        got = lax.all_to_all(blocks, "rad", 0, 0, tiled=True).reshape(n, kl, rl, mb)
+        return jnp.transpose(got, (1, 0, 2, 3)).reshape(kl, radial, mb)
 
     def to_radial_rows(y):
-        def piece_for(dest):
-            part = lax.dynamic_slice_in_dim(y, dest * rl, rl, axis=0)
-            return jnp.transpose(part, (1, 0, 2))
-
-        def place(out, piece, src):
-            return lax.dynamic_update_slice_in_dim(out, piece[:, :, None, :], src, axis=2)
-
-        out = exchange(piece_for, place, jnp.zeros((kl, rl, n, mb), y.dtype), "rad")
-        return out.reshape(kl, rl, vc, cc)
+        blocks = jnp.transpose(y.reshape(kl, n, rl, mb), (1, 0, 2, 3))
+        got = lax.all_to_all(blocks, "rad", 0, 0, tiled=True).reshape(n, kl, rl, mb)
+        return jnp.transpose(got, (1, 2, 0, 3)).reshape(kl, rl, vc, cc)
 
     def hamiltonian(current):
         columns = to_radial_columns(current)
-        applied = jnp.dot(
-            kinetic_matrix,
-            columns.reshape(radial, kl * mb),
+        applied = jnp.einsum(
+            "krs,ksm->krm",
+            kinetic_batched,
+            columns,
             precision=PRECISE,
             preferred_element_type=jnp.float32,
         )
-        kinetic_image = to_radial_rows(applied.reshape(radial, kl, mb))
+        kinetic_image = to_radial_rows(applied)
         angles = jnp.dot(
             current.reshape(-1, cc), transform.T, precision=PRECISE,
             preferred_element_type=jnp.float32,
@@ -148,53 +126,32 @@
         earlier = current
         current = following
 
-    chans = current.reshape(kl, rl, vc, n, cb)
-
-    def chan_piece(dest):
-        part = lax.dynamic_index_in_dim(chans, dest, axis=3, keepdims=False)
-        return jnp.transpose(part, (1, 0, 2, 3))
-
-    def chan_place(out, piece, src):
-        return lax.dynamic_update_slice_in_dim(out, piece, src * rl, axis=0)
-
-    radial_block = exchange(
-        chan_piece, chan_place, jnp.zeros((radial, kl, vc, cb), current.dtype), "rad"
+    width = vc * cb
+    chans = jnp.transpose(current.reshape(kl, rl, vc, n, cb), (3, 0, 1, 2, 4))
+    got = lax.all_to_all(chans.reshape(n, kl, rl, width), "rad", 0, 0, tiled=True)
+    radial_block = jnp.transpose(got.reshape(n, kl, rl, width), (1, 0, 2, 3)).reshape(
+        kl, radial, width
     )
     interp = interp_matrix(stencil, interp_weights, radial)
     qq = interp.shape[0]
     qb = qq // nh
-    width = vc * cb
-    placed = jnp.dot(
-        interp,
-        radial_block.reshape(radial, kl * width),
+    placed = jnp.einsum(
+        "kqr,krm->kqm",
+        jnp.broadcast_to(interp, (kl, qq, radial)),
+        radial_block,
         precision=PRECISE,
         preferred_element_type=jnp.float32,
-    ).reshape(qq, kl, width)
-
-    def hel_piece(dest):
-        part = lax.dynamic_slice_in_dim(placed, dest * qb, qb, axis=0)
-        return jnp.transpose(part, (1, 0, 2))
-
-    def hel_place(out, piece, src):
-        return lax.dynamic_update_slice_in_dim(out, piece, src * kl, axis=0)
-
-    gathered = exchange(
-        hel_piece, hel_place, jnp.zeros((kl * nh, qb, width), placed.dtype), "hel"
     )
+    pieces = jnp.transpose(placed.reshape(kl, nh, qb, width), (1, 0, 2, 3))
+    gathered = lax.all_to_all(pieces, "hel", 0, 0, tiled=True)
     turned = jnp.dot(
         frame_rotation,
-        gathered.reshape(kl * nh, qb * width),
+        gathered.reshape(nh * kl, qb * width),
         precision=PRECISE,
         preferred_element_type=jnp.float32,
-    ).reshape(kl * nh, qb, width)
-
-    def back_piece(dest):
-        return lax.dynamic_slice_in_dim(turned, dest * kl, kl, axis=0)
-
-    def back_place(out, piece, src):
-        return lax.dynamic_update_slice_in_dim(out, piece, src * qb, axis=1)
-
-    rotated = exchange(back_piece, back_place, jnp.zeros((kl, qq, width), turned.dtype), "hel")
+    )
+    back = lax.all_to_all(turned.reshape(nh, kl, qb, width), "hel", 0, 0, tiled=True)
+    rotated = jnp.transpose(back.reshape(nh, kl, qb, width), (1, 0, 2, 3))
     product_amp = rotated.reshape(kl, qq, vc, cb)
     return (current, product_amp)
 

time: 1310 us -> 746 us (0.57)
  the two profiles are of different devices: /device:TPU:17 before, /device:TPU:0 now
where the time goes in v2:
time: 746 us; the launch traced here: 737 us
  blocking collectives  298 us (40%)
  waiting for transfers between devices  209 us (28%)
  local copies, waits for them, and re-layouts  118 us (16%)
  matrix products  83.1 us (11%)
  starting transfers between devices  24.8 us (3%)
    all_to_all x2, blocking collectives, to_radial_columns(): got = lax.all_to_all(blocks, 'rad', 0, 0, tiled=True).reshape(n, kl, rl, mb)  197 us
    all_to_all x2, waiting for transfers between devices, to_radial_rows(): got = lax.all_to_all(blocks, 'rad', 0, 0, tiled=True).reshape(n, kl, rl, mb)  115 us
    all_to_all x1, waiting for transfers between devices, shards(): lax.all_to_all(chans.reshape(n, kl, rl, width), 'rad', 0, 0, tiled=True)  93.6 us
    all_to_all x1, blocking collectives, shards(): gathered = lax.all_to_all(pieces, 'hel', 0, 0, tiled=True)  51.2 us
    all_to_all x1, blocking collectives, shards(): lax.all_to_all(turned.reshape(nh, kl, qb, width), 'hel', 0, 0, tiled=True)  49.9 us
    dot_general x2, matrix products, hamiltonian(): jnp.dot(angles.reshape(-1, angles.shape[3]), transform, precision=PRECISE...  29.9 us
    dot_general x2, matrix products, hamiltonian(): jnp.dot(current.reshape(-1, cc), transform.T, precision=PRECISE, preferre...  23.2 us
    unnamed x38, local copies, waits for them, and re-layouts  22 us
  transfers between devices with their start and end apart: 7, of which 3 were waited for; matrix products, arithmetic and copies ran while one was open for 12% of the time, Pallas kernels for 0%

profile of v2, /device:TPU:0, one launch (start us, length us, event | category | flops | bytes accessed | tf_op | source)
XLA Modules:
  0.0 737.0 jit_solution(14051700002310206018)
XLA Ops:
  0.6 5.3 reshape.130
  10.5 100.2 %all_to_all.35 = f32[8,4,32,1024]{3,2,1,0:T(8,128)S(1)} all-to-all(f32[8,4,32,1024]{3,2,1,0:T(8,128)S(1)} %copy.64), channel_id=1, replica_groups=mesh['hel'=4,'rad'=8] {'rad'}, dimensions={0} | all-to-all | bytes 8388608 | tf_op jit(solution)/shard_map/all_to_all | solution.py:73
  137.5 16.4 %convolution_bitcast_fusion = f32[2048,512]{0,1:T(8,128)} fusion(f32[512,512]{1,0:T(8,128)S(1)} %convolution_multiply_fusion, f32[2048,512]{1,0:T(8,128)} %bitcast.86), kind=kOutput, calls=%fused_computation.23 | convolution fusion | flops 6442450944 | bytes 9437184 | tf_op jit(solution)/shard_map/dot_general | solution.py:91
  153.9 5.8 copy.68
  159.7 7.9 %fusion.30 = f32[128,512,16]{1,2,0:T(8,128)} fusion(f32[128,16,512]{2,1,0:T(8,128)} %bitcast.91, f32[16,16]{1,0:T(8,128)S(1)} %copy-done.9), kind=kOutput, calls=%fused_computation.39 | convolution fusion | flops 201326592 | bytes 8389632 | tf_op jit(solution)/shard_map/buv,bva->bua/dot_general | solution.py:95
  167.6 48.5 %all-to-all-done.1 = f32[8,4,32,1024]{3,2,1,0:T(8,128)} async-done(((f32[8,4,32,1024]{3,2,1,0:T(8,128)}), f32[8,4,32,1024]{3,2,1,0:T(8,128)}, u32[]{:S(2)}, u32[]{:S(2)}) %all-to-all-start.1) | async-done | bytes 4194336 | tf_op jit(solution)/shard_map/all_to_all | solution.py:78
  216.1 6.6 copy.67
  227.7 15.3 %broadcast_multiply_fusion = (f32[4,32,16,512]{3,2,1,0:T(8,128)}, f32[4,32,16,512]{3,2,1,0:T(8,128)}) fusion(f32[4,512]{1,0:T(4,128)S(1)} %copy-done.6, f32[4,32,16,512]{3,2,1,0:T(8,128)} %param.15, f32[3,32,16,512]{3,2,1,0:T(8,128)} %slice.33, f32[1,32,16,512]{3,2,1,0:T(8,128)S(1)} %collective-permute-done.1, ...), kind=kOutput, calls=%fused_computation.24 | convolution fusion | flops 6458179584 | bytes 34677056 | tf_op jit(solution)/shard_map/dot_general | solution.py:103
  243.0 5.4 reshape.137
  253.0 96.5 %all_to_all.36 = f32[8,4,32,1024]{3,2,1,0:T(8,128)S(1)} all-to-all(f32[8,4,32,1024]{3,2,1,0:T(8,128)S(1)} %bitcast.101), channel_id=1, replica_groups=mesh['hel'=4,'rad'=8] {'rad'}, dimensions={0} | all-to-all | bytes 8388608 | tf_op jit(solution)/shard_map/all_to_all | solution.py:73
  376.0 6.9 fusion.24
  382.9 5.6 fusion.28
  388.5 66.7 %all-to-all-done.3 = f32[8,4,32,1024]{3,2,1,0:T(8,128)} async-done(((f32[8,4,32,1024]{3,2,1,0:T(8,128)}), f32[8,4,32,1024]{3,2,1,0:T(8,128)}, u32[]{:S(2)}, u32[]{:S(2)}) %all-to-all-start.3) | async-done | bytes 4194336 | tf_op jit(solution)/shard_map/all_to_all | solution.py:78
  455.2 6.6 copy.72
  461.9 5.0 reshape.140
  466.9 14.6 %fusion.11 = f32[4,32,16,512]{3,2,1,0:T(8,128)} fusion(f32[1,32,16,512]{3,2,1,0:T(8,128)S(1)} %collective-permute-done.2, f32[3,32,16,512]{3,2,1,0:T(8,128)} %slice.34, f32[3,32,16,512]{3,2,1,0:T(8,128)} %slice.37, f32[1,32,16,512]{3,2,1,0:T(8,128)S(1)} %collective-permute-done.3, f32[4,32,16,512]{3,2,1,0:T(8,128)} %param.16, ...), kind=kOutput, calls=%fused_computation.14 | convolution fusion | flops 6457131008 | bytes 30482752 | tf_op jit(solution)/shard_map/dot_general | solution.py:103
  481.5 7.1 reshape.142
  488.6 8.2 %copy.88 = f32[4,32,16,8,64]{4,2,1,0,3:T(8,128)} copy(f32[4,32,16,8,64]{4,3,2,1,0:T(8,128)} %reshape.142) | data formatting | bytes 8388608 | tf_op jit(solution)/shard_map/reshape | solution.py:130
  496.8 7.8 %reshape.143 = f32[8,4,32,1024]{3,2,1,0:T(8,128)} reshape(f32[8,4,32,16,64]{4,3,2,1,0:T(8,128)} %bitcast.88) | data formatting | bytes 8388608 | tf_op jit(solution)/shard_map/reshape | solution.py:131
  509.6 93.6 %all-to-all-done.4 = f32[8,4,32,1024]{3,2,1,0:T(8,128)} async-done(((f32[8,4,32,1024]{3,2,1,0:T(8,128)}), f32[8,4,32,1024]{3,2,1,0:T(8,128)}, u32[]{:S(2)}, u32[]{:S(2)}) %all-to-all-start.4) | async-done | bytes 4194336 | tf_op jit(solution)/shard_map/all_to_all | solution.py:131
  610.1 51.2 %all_to_all.37 = f32[4,4,64,1024]{3,2,1,0:T(8,128)S(1)} all-to-all(f32[4,4,64,1024]{3,2,1,0:T(8,128)S(1)} %bitcast.105), channel_id=1, replica_groups=mesh['hel'=4,'rad'=8] {'hel'}, dimensions={0} | all-to-all | bytes 8388608 | tf_op jit(solution)/shard_map/all_to_all | solution.py:146
  669.9 49.9 %all_to_all.38 = f32[4,4,64,1024]{3,2,1,0:T(8,128)} all-to-all(f32[4,4,64,1024]{3,2,1,0:T(8,128)S(1)} %bitcast.107), channel_id=1, replica_groups=mesh['hel'=4,'rad'=8] {'hel'}, dimensions={0} | all-to-all | bytes 8388608 | tf_op jit(solution)/shard_map/all_to_all | solution.py:153
  719.8 8.5 %copy.79 = f32[4,4,64,1024]{2,1,3,0:T(4,128)} copy(f32[4,4,64,1024]{3,2,0,1:T(8,128)} %bitcast.90) | data formatting | bytes 8388608
  728.3 8.6 %reshape.151 = f32[4,256,16,64]{1,3,2,0:T(8,128)} reshape(f32[4,4,64,1024]{2,1,3,0:T(4,128)} %copy.79) | data formatting | bytes 8388608
  (76 shorter events, 87.8 us)
Async XLA Ops:
  0.6 110.6 %copy-start = (f32[256,256]{1,0:T(8,128)S(1)}, f32[256,256]{1,0:T(8,128)}, u32[]{:S(2)}) copy-start(f32[256,256]{1,0:T(8,128)} %param.17) | copy-start | bytes 786436
  117.4 4.7 copy-start.6
  117.4 98.7 %all-to-all-start.1 = ((f32[8,4,32,1024]{3,2,1,0:T(8,128)}), f32[8,4,32,1024]{3,2,1,0:T(8,128)}, u32[]{:S(2)}, u32[]{:S(2)}) async-start(f32[8,4,32,1024]{3,2,1,0:T(8,128)} %bitcast.94), calls=%async_computation.1 | async-start | bytes 8388608 | tf_op jit(solution)/shard_map/all_to_all | solution.py:78
  122.1 7.5 %copy-start.2 = (f32[4,32,16,512]{3,2,1,0:T(8,128)S(1)}, f32[4,32,16,512]{3,2,1,0:T(8,128)}, u32[]{:S(2)}) copy-start(f32[4,32,16,512]{3,2,1,0:T(8,128)} %param.16) | copy-start | bytes 12582916
  126.1 101.6 %collective-permute-start.1 = (f32[1,32,16,512]{3,2,1,0:T(8,128)}, f32[1,32,16,512]{3,2,1,0:T(8,128)S(1)}, u32[]{:S(2)}, u32[]{:S(2)}) collective-permute-start(f32[1,32,16,512]{3,2,1,0:T(8,128)} %slice.32), channel_id=1, source_target_pairs={{0,8},{8,16},{16,24},{1,9},{9,17},{17,25},{2,10},{10,18},{18,26},{... | collective-permute-start | bytes 3145736 | tf_op jit(solution)/shard_map/ppermute | solution.py:13
  130.6 97.1 %collective-permute-start = (f32[1,32,16,512]{3,2,1,0:T(8,128)}, f32[1,32,16,512]{3,2,1,0:T(8,128)S(1)}, u32[]{:S(2)}, u32[]{:S(2)}) collective-permute-start(f32[1,32,16,512]{3,2,1,0:T(8,128)} %slice.25), channel_id=1, source_target_pairs={{8,0},{16,8},{24,16},{9,1},{17,9},{25,17},{10,2},{18,10},{26,18},{... | collective-permute-start | bytes 3145736 | tf_op jit(solution)/shard_map/ppermute | solution.py:13
  134.1 2.0 copy-start.15
  134.1 2.1 copy-start.16
  134.1 2.1 copy-start.12
  134.1 2.2 copy-start.7
  134.1 2.8 copy-start.8
  153.9 5.8 copy-start.9
  222.7 5.0 copy-start.5
  222.7 5.0 copy-start.13
  356.7 98.6 %all-to-all-start.3 = ((f32[8,4,32,1024]{3,2,1,0:T(8,128)}), f32[8,4,32,1024]{3,2,1,0:T(8,128)}, u32[]{:S(2)}, u32[]{:S(2)}) async-start(f32[8,4,32,1024]{3,2,1,0:T(8,128)} %bitcast.95), calls=%async_computation.3 | async-start | bytes 8388608 | tf_op jit(solution)/shard_map/all_to_all | solution.py:78
  361.2 10.9 %copy-start.3 = (f32[4,32,16,512]{3,2,1,0:T(8,128)S(1)}, f32[4,32,16,512]{3,2,1,0:T(8,128)}, u32[]{:S(2)}) copy-start(f32[4,32,16,512]{3,2,1,0:T(8,128)} %get-tuple-element.13) | copy-start | bytes 12582916
  363.7 103.2 %collective-permute-start.2 = (f32[1,32,16,512]{3,2,1,0:T(8,128)}, f32[1,32,16,512]{3,2,1,0:T(8,128)S(1)}, u32[]{:S(2)}, u32[]{:S(2)}) collective-permute-start(f32[1,32,16,512]{3,2,1,0:T(8,128)} %slice.35), channel_id=1, source_target_pairs={{8,0},{16,8},{24,16},{9,1},{17,9},{25,17},{10,2},{18,10},{26,18},{... | collective-permute-start | bytes 3145736 | tf_op jit(solution)/shard_map/ppermute | solution.py:13
  365.0 9.1 %copy-start.4 = (f32[4,32,16,512]{3,2,1,0:T(8,128)S(1)}, f32[4,32,16,512]{3,2,1,0:T(8,128)}, u32[]{:S(2)}) copy-start(f32[4,32,16,512]{3,2,1,0:T(8,128)} %get-tuple-element.12) | copy-start | bytes 12582916
  367.5 99.4 %collective-permute-start.3 = (f32[1,32,16,512]{3,2,1,0:T(8,128)}, f32[1,32,16,512]{3,2,1,0:T(8,128)S(1)}, u32[]{:S(2)}, u32[]{:S(2)}) collective-permute-start(f32[1,32,16,512]{3,2,1,0:T(8,128)} %slice.36), channel_id=1, source_target_pairs={{0,8},{8,16},{16,24},{1,9},{9,17},{17,25},{2,10},{10,18},{18,26},{... | collective-permute-start | bytes 3145736 | tf_op jit(solution)/shard_map/ppermute | solution.py:13
  504.6 4.7 copy-start.14
  504.6 4.7 copy-start.11
  504.6 98.7 %all-to-all-start.4 = ((f32[8,4,32,1024]{3,2,1,0:T(8,128)}), f32[8,4,32,1024]{3,2,1,0:T(8,128)}, u32[]{:S(2)}, u32[]{:S(2)}) async-start(f32[8,4,32,1024]{3,2,1,0:T(8,128)} %reshape.143), calls=%async_computation.4 | async-start | bytes 8388608 | tf_op jit(solution)/shard_map/all_to_all | solution.py:131
  661.3 2.4 copy-start.10
  719.8 17.1 %copy-start.1 = (f32[256,256]{1,0:T(8,128)S(1)}, f32[256,256]{1,0:T(8,128)}, u32[]{:S(2)}) copy-start(f32[256,256]{1,0:T(8,128)} %param.17) | copy-start | bytes 786436

commit v3 on v2

v3 whole, which is shorter than its diff:
```python
import jax
import jax.numpy as jnp
from jax import lax
from jax.sharding import PartitionSpec as P

STEPS = 2
PRECISE = lax.Precision.HIGHEST


def shifted(block, axis, distance):
    devices = range(lax.axis_size(axis))
    route = [(i - distance, i) for i in devices if i - distance in devices]
    return lax.ppermute(block, axis, route)


def angular_matrix(basis_first, basis_second, chan_table):
    levels = basis_first.shape[1]
    level_grid = jnp.arange(levels, dtype=jnp.int32)
    first_hot = (chan_table[None, :] // levels == level_grid[:, None]).astype(jnp.float32)
    second_hot = (chan_table[None, :] % levels == level_grid[:, None]).astype(jnp.float32)
    first_part = jnp.dot(
        basis_first, first_hot, precision=PRECISE, preferred_element_type=jnp.float32
    )
    second_part = jnp.dot(
        basis_second, second_hot, precision=PRECISE, preferred_element_type=jnp.float32
    )
    return first_part * second_part


def interp_matrix(stencil, interp_weights, radial_count):
    offsets = jnp.arange(4, dtype=jnp.int32)
    points = jnp.arange(radial_count, dtype=jnp.int32)
    matches = (points[None, None, :] == (stencil[:, None] + offsets[None, :])[:, :, None]).astype(
        jnp.float32
    )
    return jnp.sum(matches * interp_weights[:, :, None], axis=1)


def shards(
    prev_vector,
    curr_vector,
    kinetic_matrix,
    basis_first,
    basis_second,
    chan_table,
    potential,
    vib_coupling,
    vib_energy,
    coriolis,
    radial_factor,
    damping,
    stencil,
    interp_weights,
    frame_rotation,
):
    kl, rl, vc, cc = curr_vector.shape
    n = lax.axis_size("rad")
    nh = lax.axis_size("hel")
    radial = rl * n
    mb = vc * cc // n
    cb = cc // n
    rad_index = lax.axis_index("rad")
    radial_local = lax.dynamic_slice_in_dim(radial_factor, rad_index * rl, rl)
    damping_local = lax.dynamic_slice_in_dim(damping, rad_index * rl, rl)
    damp_full = damping_local[None, :, None, None]
    transform = angular_matrix(basis_first, basis_second, chan_table)
    vib_batched = jnp.broadcast_to(vib_coupling, (kl * rl, vc, vc))

    kinetic_batched = jnp.broadcast_to(kinetic_matrix, (kl, radial, radial))

    def to_radial_columns(x):
        ck = x.shape[0]
        blocks = jnp.transpose(x.reshape(ck, rl, n, mb), (2, 0, 1, 3))
        got = lax.all_to_all(blocks, "rad", 0, 0, tiled=True).reshape(n, ck, rl, mb)
        return jnp.transpose(got, (1, 0, 2, 3)).reshape(ck, radial, mb)

    def to_radial_rows(y):
        ck = y.shape[0]
        blocks = jnp.transpose(y.reshape(ck, n, rl, mb), (1, 0, 2, 3))
        got = lax.all_to_all(blocks, "rad", 0, 0, tiled=True).reshape(n, ck, rl, mb)
        return jnp.transpose(got, (1, 2, 0, 3)).reshape(ck, rl, vc, cc)

    def kinetic(chunk):
        columns = to_radial_columns(chunk)
        applied = jnp.einsum(
            "krs,ksm->krm",
            kinetic_batched[: chunk.shape[0]],
            columns,
            precision=PRECISE,
            preferred_element_type=jnp.float32,
        )
        return to_radial_rows(applied)

    def potential_part(chunk):
        ck = chunk.shape[0]
        angles = jnp.dot(
            chunk.reshape(-1, cc), transform.T, precision=PRECISE,
            preferred_element_type=jnp.float32,
        )
        angles = jnp.einsum(
            "buv,bva->bua",
            vib_batched[: ck * rl],
            angles.reshape(ck * rl, vc, -1),
            precision=PRECISE,
            preferred_element_type=jnp.float32,
        )
        angles = angles.reshape(ck, rl, vc, -1) * potential[None, :, None, :]
        angular = jnp.dot(
            angles.reshape(-1, angles.shape[3]),
            transform,
            precision=PRECISE,
            preferred_element_type=jnp.float32,
        )
        return angular.reshape(chunk.shape) + vib_energy[None, None, :, None] * chunk

    kchunks = 2 if kl % 2 == 0 else 1
    ks = kl // kchunks

    def step(earlier, current):
        whole = jnp.concatenate(current, axis=0)
        weighted = coriolis[:, None, None, :] * whole
        from_above = shifted(whole[:1], "hel", -1)
        from_below = shifted(weighted[-1:], "hel", 1)
        upper_side = jnp.concatenate([whole[1:], from_above], axis=0)
        lower_side = jnp.concatenate([from_below, weighted[:-1]], axis=0)
        following = []
        for i, chunk in enumerate(current):
            sl = slice(i * ks, (i + 1) * ks)
            image = (
                kinetic(chunk)
                + potential_part(chunk)
                + radial_local[None, :, None, None]
                * (coriolis[sl, None, None, :] * upper_side[sl] + lower_side[sl])
            )
            following.append(damp_full * (2.0 * image - damp_full * earlier[i]))
        return following

    def split(x):
        return [x[i * ks:(i + 1) * ks] for i in range(kchunks)]

    earlier = split(prev_vector)
    current = split(curr_vector)
    for iteration in range(STEPS):
        earlier, current = current, step(earlier, current)
    current = jnp.concatenate(current, axis=0)

    interp = interp_matrix(stencil, interp_weights, radial)
    qq = interp.shape[0]
    qb = qq // nh
    interp_batched = jnp.broadcast_to(interp, (kl, qq, radial))
    vchunks = 4 if vc % 4 == 0 else 1
    vs = vc // vchunks
    width = vs * cb
    results = []
    for i in range(vchunks):
        part = current[:, :, i * vs:(i + 1) * vs, :]
        chans = jnp.transpose(part.reshape(kl, rl, vs, n, cb), (3, 0, 1, 2, 4))
        got = lax.all_to_all(chans.reshape(n, kl, rl, width), "rad", 0, 0, tiled=True)
        radial_block = jnp.transpose(got.reshape(n, kl, rl, width), (1, 0, 2, 3)).reshape(
            kl, radial, width
        )
        placed = jnp.einsum(
            "kqr,krm->kqm",
            interp_batched,
            radial_block,
            precision=PRECISE,
            preferred_element_type=jnp.float32,
        )
        pieces = jnp.transpose(placed.reshape(kl, nh, qb, width), (1, 0, 2, 3))
        gathered = lax.all_to_all(pieces, "hel", 0, 0, tiled=True)
        turned = jnp.dot(
            frame_rotation,
            gathered.reshape(nh * kl, qb * width),
            precision=PRECISE,
            preferred_element_type=jnp.float32,
        )
        back = lax.all_to_all(turned.reshape(nh, kl, qb, width), "hel", 0, 0, tiled=True)
        rotated = jnp.transpose(back.reshape(nh, kl, qb, width), (1, 0, 2, 3))
        results.append(rotated.reshape(kl, qq, vs, cb))
    product_amp = jnp.concatenate(results, axis=2)
    return (current, product_amp)


def solution(mesh):
    in_specs = (
        P("hel", "rad", None, None),
        P("hel", "rad", None, None),
        P(),
        P(),
        P(),
        P(),
        P("rad", None),
        P(),
        P(),
        P("hel", None),
        P(),
        P(),
        P(),
        P(),
        P(),
    )
    out_specs = (P("hel", "rad", None, None), P("hel", None, None, "rad"))
    return jax.shard_map(shards, mesh=mesh, in_specs=in_specs, out_specs=out_specs, check_vma=False)
```

time: 746 us -> 762 us (1.021)
  blocking collectives: 298 us -> 0 us
  waiting for transfers between devices: 209 us -> 397 us
  starting transfers between devices: 24.8 us -> 92.6 us
  local copies, waits for them, and re-layouts: 118 us -> 151 us
  other arithmetic: 3.25 us -> 20.5 us
    all_to_all x4 -> x0, blocking collectives: 298 us -> none  [the longest x2 197 us: to_radial_columns(): got = lax.all_to_all(blocks, 'rad', 0, 0, tiled=True).reshape(n, kl, rl, mb)]
    all_to_all x2 -> x16, waiting for transfers between devices: 115 us -> 308 us  [the longest x4 135 us: to_radial_columns(): got = lax.all_to_all(blocks, 'rad', 0, 0, tiled=True).reshape(n, ck, rl, mb)]
    all_to_all x2 -> x16, starting transfers between devices: 9.25 us -> 65.1 us  [the longest x4 18.8 us: to_radial_columns(): got = lax.all_to_all(blocks, 'rad', 0, 0, tiled=True).reshape(n, ck, rl, mb)]
    reshape x9 -> x28, local copies, waits for them, and re-layouts: 45.5 us -> 62.9 us  [the longest x8 24.3 us: to_radial_columns(): blocks = jnp.transpose(x.reshape(ck, rl, n, mb), (2, 0, 1, 3))]
    concatenate x0 -> x4, other arithmetic: none -> 15.2 us  [the longest x2 6.67 us: shards(): current = jnp.concatenate(current, axis=0)]
    all_to_all x1 -> x4, starting transfers between devices: 4.69 us -> 15.8 us  [shards(): lax.all_to_all(chans.reshape(n, kl, rl, width), 'rad', 0, 0, tiled=True)]
    all_to_all x1 -> x4, waiting for transfers between devices: 93.6 us -> 82.9 us  [shards(): lax.all_to_all(chans.reshape(n, kl, rl, width), 'rad', 0, 0, tiled=True)]
    dot_general x9 -> x20, matrix products: 78.2 us -> 84.3 us  [the longest x4 34.4 us: potential_part(): jnp.dot(angles.reshape(-1, angles.shape[3]), transform, precision=PRECISE...]
  transfers between devices with their start and end apart: 7 -> 24, of which waited for: 3 -> 20; matrix products, arithmetic and copies ran while one was open for 12% -> 28% of each run, Pallas kernels for 0% -> 0%
where the time goes in v3:
time: 762 us; the launch traced here: 752 us
  waiting for transfers between devices  397 us (52%)
  local copies, waits for them, and re-layouts  151 us (20%)
  starting transfers between devices  92.6 us (12%)
  matrix products  89.6 us (12%)
  other arithmetic  20.5 us (3%)
    all_to_all x4, waiting for transfers between devices, to_radial_columns(): got = lax.all_to_all(blocks, 'rad', 0, 0, tiled=True).reshape(n, ck, rl, mb)  135 us
    all_to_all x4, waiting for transfers between devices, to_radial_rows(): got = lax.all_to_all(blocks, 'rad', 0, 0, tiled=True).reshape(n, ck, rl, mb)  103 us
    all_to_all x4, waiting for transfers between devices, shards(): lax.all_to_all(chans.reshape(n, kl, rl, width), 'rad', 0, 0, tiled=True)  82.9 us
    all_to_all x4, waiting for transfers between devices, shards(): gathered = lax.all_to_all(pieces, 'hel', 0, 0, tiled=True)  41 us
    dot_general x4, matrix products, potential_part(): jnp.dot(angles.reshape(-1, angles.shape[3]), transform, precision=PRECISE...  34.4 us
    all_to_all x4, waiting for transfers between devices, shards(): lax.all_to_all(turned.reshape(nh, kl, qb, width), 'hel', 0, 0, tiled=True)  29.6 us
    reshape x8, local copies, waits for them, and re-layouts, to_radial_columns(): blocks = jnp.transpose(x.reshape(ck, rl, n, mb), (2, 0, 1, 3))  24.3 us
    unnamed x97, local copies, waits for them, and re-layouts  22.8 us
  transfers between devices with their start and end apart: 24, of which 20 were waited for; matrix products, arithmetic and copies ran while one was open for 28% of the time, Pallas kernels for 0%

profile of v3, /device:TPU:0, one launch (start us, length us, event | category | flops | bytes accessed | tf_op | source)
XLA Modules:
  0.0 752.2 jit_solution(3994546385543508963)
XLA Ops:
  24.9 43.4 %all-to-all-done = f32[8,2,32,1024]{3,2,1,0:T(8,128)} async-done(((f32[8,2,32,1024]{3,2,1,0:T(8,128)}), f32[8,2,32,1024]{3,2,1,0:T(8,128)}, u32[]{:S(2)}, u32[]{:S(2)}) %all-to-all-start) | async-done | bytes 2097184 | tf_op jit(solution)/shard_map/all_to_all | solution.py:74
  77.0 43.9 %all-to-all-done.4 = f32[8,2,32,1024]{3,2,1,0:T(8,128)S(1)} async-done(((f32[8,2,32,1024]{3,2,1,0:T(8,128)}), f32[8,2,32,1024]{3,2,1,0:T(8,128)S(1)}, u32[]{:S(2)}, u32[]{:S(2)}) %all-to-all-start.4) | async-done | bytes 2097184 | tf_op jit(solution)/shard_map/all_to_all | solution.py:74
  131.0 43.8 %all-to-all-done.1 = f32[8,2,32,1024]{3,2,1,0:T(8,128)S(1)} async-done(((f32[8,2,32,1024]{3,2,1,0:T(8,128)}), f32[8,2,32,1024]{3,2,1,0:T(8,128)S(1)}, u32[]{:S(2)}, u32[]{:S(2)}) %all-to-all-start.1) | async-done | bytes 2097184 | tf_op jit(solution)/shard_map/all_to_all | solution.py:80
  192.3 8.1 %convolution_bitcast_fusion.1 = f32[1024,512]{0,1:T(8,128)} fusion(f32[512,512]{1,0:T(8,128)S(1)} %convolution_multiply_fusion, f32[1024,512]{1,0:T(8,128)S(1)} %bitcast.205), kind=kOutput, calls=%fused_computation.71 | convolution fusion | flops 3221225472 | bytes 5242880 | tf_op jit(solution)/shard_map/dot_general | solution.py:96
  214.2 9.0 %fusion.27 = f32[2,32,16,512]{3,2,1,0:T(8,128)S(1)} fusion(f32[3,32,16,512]{3,2,1,0:T(8,128)} %slice.128, f32[1,32,16,512]{3,2,1,0:T(8,128)} %collective-permute-done, f32[4,32,16,512]{3,2,1,0:T(8,128)} %param.15, f32[4,32,16,512]{3,2,1,0:T(8,128)} %param.16, f32[2,32,16,512]{3,2,1,0:T(8,128)} %reshape.250, f32[2,32,16,512]{3,2,1,0:T(8,128)} %bitcast.209, ...), kind=kOutput, calls=%fused_computation.48 | convolution fusion | flops 3228041216 | bytes 17895744 | tf_op jit(solution)/shard_map/dot_general | solution.py:108
  238.3 6.7 convolution_bitcast_fusion
  264.6 10.1 %fusion.20 = f32[2,32,16,512]{3,2,1,0:T(8,128)} fusion(f32[4,32,16,512]{3,2,1,0:T(8,128)} %copy-done.8, f32[1,32,16,512]{3,2,1,0:T(8,128)} %collective-permute-done.1, f32[3,32,16,512]{3,2,1,0:T(8,128)S(1)} %slice-done, f32[4,32,16,512]{3,2,1,0:T(8,128)} %param.15, f32[2,32,16,512]{3,2,1,0:T(8,128)} %reshape.262, f32[2,32,16,512]{3,2,1,0:T(8,128)} %bitcast.208, ...), kind=kOutput, calls=%fused_computation.39 | convolution fusion | flops 3228041216 | bytes 17895744 | tf_op jit(solution)/shard_map/dot_general | solution.py:108
  292.7 43.7 %all-to-all-done.6 = f32[8,2,32,1024]{3,2,1,0:T(8,128)S(1)} async-done(((f32[8,2,32,1024]{3,2,1,0:T(8,128)}), f32[8,2,32,1024]{3,2,1,0:T(8,128)S(1)}, u32[]{:S(2)}, u32[]{:S(2)}) %all-to-all-start.6) | async-done | bytes 2097184 | tf_op jit(solution)/shard_map/all_to_all | solution.py:74
  346.6 43.7 %all-to-all-done.3 = f32[8,2,32,1024]{3,2,1,0:T(8,128)S(1)} async-done(((f32[8,2,32,1024]{3,2,1,0:T(8,128)}), f32[8,2,32,1024]{3,2,1,0:T(8,128)S(1)}, u32[]{:S(2)}, u32[]{:S(2)}) %all-to-all-start.3) | async-done | bytes 2097184 | tf_op jit(solution)/shard_map/all_to_all | solution.py:80
  430.0 15.1 %all-to-all-done.7 = f32[8,2,32,1024]{3,2,1,0:T(8,128)} async-done(((f32[8,2,32,1024]{3,2,1,0:T(8,128)}), f32[8,2,32,1024]{3,2,1,0:T(8,128)}, u32[]{:S(2)}, u32[]{:S(2)}) %all-to-all-start.7) | async-done | bytes 2097184 | tf_op jit(solution)/shard_map/all_to_all | solution.py:80
  452.0 9.0 %fusion.9 = f32[2,32,16,512]{3,2,1,0:T(8,128)S(1)} fusion(f32[2,32,16,512]{3,2,1,0:T(8,128)} %copy-done.4, f32[2,32,16,512]{3,2,1,0:T(8,128)S(1)} %copy-done.3, f32[3,32,16,512]{3,2,1,0:T(8,128)} %slice.133, f32[1,32,16,512]{3,2,1,0:T(8,128)} %collective-permute-done.2, f32[2,32,16,512]{3,2,1,0:T(8,128)} %reshape.257, f32[2,32,16,512]{3,2,1,0:T(8,128)} %bitcast.207, ...), kind=kOutput, calls=%fused_computation.24 | convolution fusion | flops 3228565504 | bytes 17895744 | tf_op jit(solution)/shard_map/dot_general | solution.py:108
  486.2 19.6 %all-to-all-done.8 = f32[8,4,32,256]{3,2,1,0:T(8,128)S(1)} async-done(((f32[8,4,32,256]{3,2,1,0:T(8,128)}), f32[8,4,32,256]{3,2,1,0:T(8,128)S(1)}, u32[]{:S(2)}, u32[]{:S(2)}) %all-to-all-start.8) | async-done | bytes 1048608 | tf_op jit(solution)/shard_map/all_to_all | solution.py:158
  516.9 19.7 %all-to-all-done.11 = f32[8,4,32,256]{3,2,1,0:T(8,128)} async-done(((f32[8,4,32,256]{3,2,1,0:T(8,128)}), f32[8,4,32,256]{3,2,1,0:T(8,128)}, u32[]{:S(2)}, u32[]{:S(2)}) %all-to-all-start.11) | async-done | bytes 1048608 | tf_op jit(solution)/shard_map/all_to_all | solution.py:158
  547.8 19.7 %all-to-all-done.14 = f32[8,4,32,256]{3,2,1,0:T(8,128)} async-done(((f32[8,4,32,256]{3,2,1,0:T(8,128)}), f32[8,4,32,256]{3,2,1,0:T(8,128)}, u32[]{:S(2)}, u32[]{:S(2)}) %all-to-all-start.14) | async-done | bytes 1048608 | tf_op jit(solution)/shard_map/all_to_all | solution.py:158
  573.6 23.9 %all-to-all-done.17 = f32[8,4,32,256]{3,2,1,0:T(8,128)S(1)} async-done(((f32[8,4,32,256]{3,2,1,0:T(8,128)}), f32[8,4,32,256]{3,2,1,0:T(8,128)S(1)}, u32[]{:S(2)}, u32[]{:S(2)}) %all-to-all-start.17) | async-done | bytes 1048608 | tf_op jit(solution)/shard_map/all_to_all | solution.py:158
  604.5 10.3 %all-to-all-done.9 = f32[4,4,64,256]{3,2,1,0:T(8,128)S(1)} async-done(((f32[4,4,64,256]{3,2,1,0:T(8,128)}), f32[4,4,64,256]{3,2,1,0:T(8,128)S(1)}, u32[]{:S(2)}, u32[]{:S(2)}) %all-to-all-start.9) | async-done | bytes 1048608 | tf_op jit(solution)/shard_map/all_to_all | solution.py:170
  621.7 9.6 %all-to-all-done.12 = f32[4,4,64,256]{3,2,1,0:T(8,128)S(1)} async-done(((f32[4,4,64,256]{3,2,1,0:T(8,128)}), f32[4,4,64,256]{3,2,1,0:T(8,128)S(1)}, u32[]{:S(2)}, u32[]{:S(2)}) %all-to-all-start.12) | async-done | bytes 1048608 | tf_op jit(solution)/shard_map/all_to_all | solution.py:170
  638.2 10.9 %all-to-all-done.15 = f32[4,4,64,256]{3,2,1,0:T(8,128)} async-done(((f32[4,4,64,256]{3,2,1,0:T(8,128)}), f32[4,4,64,256]{3,2,1,0:T(8,128)}, u32[]{:S(2)}, u32[]{:S(2)}) %all-to-all-start.15) | async-done | bytes 1048608 | tf_op jit(solution)/shard_map/all_to_all | solution.py:170
  655.7 10.2 %all-to-all-done.18 = f32[4,4,64,256]{3,2,1,0:T(8,128)S(1)} async-done(((f32[4,4,64,256]{3,2,1,0:T(8,128)}), f32[4,4,64,256]{3,2,1,0:T(8,128)S(1)}, u32[]{:S(2)}, u32[]{:S(2)}) %all-to-all-start.18) | async-done | bytes 1048608 | tf_op jit(solution)/shard_map/all_to_all | solution.py:170
  673.3 10.1 %all-to-all-done.10 = f32[4,4,64,256]{3,2,1,0:T(8,128)S(1)} async-done(((f32[4,4,64,256]{3,2,1,0:T(8,128)}), f32[4,4,64,256]{3,2,1,0:T(8,128)S(1)}, u32[]{:S(2)}, u32[]{:S(2)}) %all-to-all-start.10) | async-done | bytes 1048608 | tf_op jit(solution)/shard_map/all_to_all | solution.py:177
  691.2 8.8 %all-to-all-done.13 = f32[4,4,64,256]{3,2,1,0:T(8,128)S(1)} async-done(((f32[4,4,64,256]{3,2,1,0:T(8,128)}), f32[4,4,64,256]{3,2,1,0:T(8,128)S(1)}, u32[]{:S(2)}, u32[]{:S(2)}) %all-to-all-start.13) | async-done | bytes 1048608 | tf_op jit(solution)/shard_map/all_to_all | solution.py:177
  706.5 10.1 %all-to-all-done.16 = f32[4,4,64,256]{3,2,1,0:T(8,128)S(1)} async-done(((f32[4,4,64,256]{3,2,1,0:T(8,128)}), f32[4,4,64,256]{3,2,1,0:T(8,128)S(1)}, u32[]{:S(2)}, u32[]{:S(2)}) %all-to-all-start.16) | async-done | bytes 1048608 | tf_op jit(solution)/shard_map/all_to_all | solution.py:177
  737.7 6.6 pad_maximum_fusion
  744.3 7.7 %copy.130 = f32[4,256,16,64]{1,3,2,0:T(8,128)} copy(f32[4,256,16,64]{3,2,1,0:T(8,128)} %pad_maximum_fusion) | data formatting | bytes 8388608
  (222 shorter events, 306.9 us)
Async XLA Ops:
  12.8 55.5 %all-to-all-start = ((f32[8,2,32,1024]{3,2,1,0:T(8,128)}), f32[8,2,32,1024]{3,2,1,0:T(8,128)}, u32[]{:S(2)}, u32[]{:S(2)}) async-start(f32[8,2,32,1024]{3,2,1,0:T(8,128)} %bitcast.221), calls=%async_computation | async-start | bytes 4194304 | tf_op jit(solution)/shard_map/all_to_all | solution.py:74
  68.3 52.6 %all-to-all-start.4 = ((f32[8,2,32,1024]{3,2,1,0:T(8,128)}), f32[8,2,32,1024]{3,2,1,0:T(8,128)S(1)}, u32[]{:S(2)}, u32[]{:S(2)}) async-start(f32[8,2,32,1024]{3,2,1,0:T(8,128)} %bitcast.217), calls=%async_computation.4 | async-start | bytes 4194304 | tf_op jit(solution)/shard_map/all_to_all | solution.py:74
  122.2 52.6 %all-to-all-start.1 = ((f32[8,2,32,1024]{3,2,1,0:T(8,128)}), f32[8,2,32,1024]{3,2,1,0:T(8,128)S(1)}, u32[]{:S(2)}, u32[]{:S(2)}) async-start(f32[8,2,32,1024]{3,2,1,0:T(8,128)} %bitcast.218), calls=%async_computation.1 | async-start | bytes 4194304 | tf_op jit(solution)/shard_map/all_to_all | solution.py:80
  174.8 54.6 %all-to-all-start.5 = ((f32[8,2,32,1024]{3,2,1,0:T(8,128)}), f32[8,2,32,1024]{3,2,1,0:T(8,128)}, u32[]{:S(2)}, u32[]{:S(2)}) async-start(f32[8,2,32,1024]{3,2,1,0:T(8,128)} %bitcast.192), calls=%async_computation.5 | async-start | bytes 4194304 | tf_op jit(solution)/shard_map/all_to_all | solution.py:80
  183.2 31.0 %collective-permute-start = (f32[1,32,16,512]{3,2,1,0:T(8,128)}, f32[1,32,16,512]{3,2,1,0:T(8,128)}, u32[]{:S(2)}, u32[]{:S(2)}) collective-permute-start(f32[1,32,16,512]{3,2,1,0:T(8,128)} %slice.127), channel_id=1, source_target_pairs={{0,8},{8,16},{16,24},{1,9},{9,17},{17,25},{2,10},{10,18},{18,26},{... | collective-permute-start | bytes 3145736 | tf_op jit(solution)/shard_map/ppermute | solution.py:13
  229.4 54.1 %all-to-all-start.2 = ((f32[8,2,32,1024]{3,2,1,0:T(8,128)}), f32[8,2,32,1024]{3,2,1,0:T(8,128)}, u32[]{:S(2)}, u32[]{:S(2)}) async-start(f32[8,2,32,1024]{3,2,1,0:T(8,128)} %bitcast.211), calls=%async_computation.2 | async-start | bytes 4194304 | tf_op jit(solution)/shard_map/all_to_all | solution.py:74
  236.7 27.9 %collective-permute-start.1 = (f32[1,32,16,512]{3,2,1,0:T(8,128)}, f32[1,32,16,512]{3,2,1,0:T(8,128)}, u32[]{:S(2)}, u32[]{:S(2)}) collective-permute-start(f32[1,32,16,512]{3,2,1,0:T(8,128)} %slice.111), channel_id=1, source_target_pairs={{8,0},{16,8},{24,16},{9,1},{17,9},{25,17},{10,2},{18,10},{26,18},{... | collective-permute-start | bytes 3145736 | tf_op jit(solution)/shard_map/ppermute | solution.py:13
  283.5 52.8 %all-to-all-start.6 = ((f32[8,2,32,1024]{3,2,1,0:T(8,128)}), f32[8,2,32,1024]{3,2,1,0:T(8,128)S(1)}, u32[]{:S(2)}, u32[]{:S(2)}) async-start(f32[8,2,32,1024]{3,2,1,0:T(8,128)} %bitcast.219), calls=%async_computation.6 | async-start | bytes 4194304 | tf_op jit(solution)/shard_map/all_to_all | solution.py:74
  337.7 52.6 %all-to-all-start.3 = ((f32[8,2,32,1024]{3,2,1,0:T(8,128)}), f32[8,2,32,1024]{3,2,1,0:T(8,128)S(1)}, u32[]{:S(2)}, u32[]{:S(2)}) async-start(f32[8,2,32,1024]{3,2,1,0:T(8,128)} %bitcast.220), calls=%async_computation.3 | async-start | bytes 4194304 | tf_op jit(solution)/shard_map/all_to_all | solution.py:80
  391.6 53.4 %all-to-all-start.7 = ((f32[8,2,32,1024]{3,2,1,0:T(8,128)}), f32[8,2,32,1024]{3,2,1,0:T(8,128)}, u32[]{:S(2)}, u32[]{:S(2)}) async-start(f32[8,2,32,1024]{3,2,1,0:T(8,128)} %bitcast.213), calls=%async_computation.7 | async-start | bytes 4194304 | tf_op jit(solution)/shard_map/all_to_all | solution.py:80
  401.8 50.2 %collective-permute-start.2 = (f32[1,32,16,512]{3,2,1,0:T(8,128)}, f32[1,32,16,512]{3,2,1,0:T(8,128)}, u32[]{:S(2)}, u32[]{:S(2)}) collective-permute-start(f32[1,32,16,512]{3,2,1,0:T(8,128)} %slice.132), channel_id=1, source_target_pairs={{0,8},{8,16},{16,24},{1,9},{9,17},{17,25},{2,10},{10,18},{18,26},{... | collective-permute-start | bytes 3145736 | tf_op jit(solution)/shard_map/ppermute | solution.py:13
  405.5 55.6 %collective-permute-start.3 = (f32[1,32,16,512]{3,2,1,0:T(8,128)}, f32[1,32,16,512]{3,2,1,0:T(8,128)}, u32[]{:S(2)}, u32[]{:S(2)}) collective-permute-start(f32[1,32,16,512]{3,2,1,0:T(8,128)} %slice.136), channel_id=1, source_target_pairs={{8,0},{16,8},{24,16},{9,1},{17,9},{25,17},{10,2},{18,10},{26,18},{... | collective-permute-start | bytes 3145736 | tf_op jit(solution)/shard_map/ppermute | solution.py:13
  475.5 30.3 %all-to-all-start.8 = ((f32[8,4,32,256]{3,2,1,0:T(8,128)}), f32[8,4,32,256]{3,2,1,0:T(8,128)S(1)}, u32[]{:S(2)}, u32[]{:S(2)}) async-start(f32[8,4,32,256]{3,2,1,0:T(8,128)} %reshape.272), calls=%async_computation.8 | async-start | bytes 2097152 | tf_op jit(solution)/shard_map/all_to_all | solution.py:158
  505.8 30.8 %all-to-all-start.11 = ((f32[8,4,32,256]{3,2,1,0:T(8,128)}), f32[8,4,32,256]{3,2,1,0:T(8,128)}, u32[]{:S(2)}, u32[]{:S(2)}) async-start(f32[8,4,32,256]{3,2,1,0:T(8,128)} %reshape.279), calls=%async_computation.11 | async-start | bytes 2097152 | tf_op jit(solution)/shard_map/all_to_all | solution.py:158
  536.6 30.8 %all-to-all-start.14 = ((f32[8,4,32,256]{3,2,1,0:T(8,128)}), f32[8,4,32,256]{3,2,1,0:T(8,128)}, u32[]{:S(2)}, u32[]{:S(2)}) async-start(f32[8,4,32,256]{3,2,1,0:T(8,128)} %reshape.286), calls=%async_computation.14 | async-start | bytes 2097152 | tf_op jit(solution)/shard_map/all_to_all | solution.py:158
  567.5 30.1 %all-to-all-start.17 = ((f32[8,4,32,256]{3,2,1,0:T(8,128)}), f32[8,4,32,256]{3,2,1,0:T(8,128)S(1)}, u32[]{:S(2)}, u32[]{:S(2)}) async-start(f32[8,4,32,256]{3,2,1,0:T(8,128)} %reshape.293), calls=%async_computation.17 | async-start | bytes 2097152 | tf_op jit(solution)/shard_map/all_to_all | solution.py:158
  597.5 17.2 %all-to-all-start.9 = ((f32[4,4,64,256]{3,2,1,0:T(8,128)}), f32[4,4,64,256]{3,2,1,0:T(8,128)S(1)}, u32[]{:S(2)}, u32[]{:S(2)}) async-start(f32[4,4,64,256]{3,2,1,0:T(8,128)} %bitcast.201), calls=%async_computation.9 | async-start | bytes 2097152 | tf_op jit(solution)/shard_map/all_to_all | solution.py:170
  614.7 16.6 %all-to-all-start.12 = ((f32[4,4,64,256]{3,2,1,0:T(8,128)}), f32[4,4,64,256]{3,2,1,0:T(8,128)S(1)}, u32[]{:S(2)}, u32[]{:S(2)}) async-start(f32[4,4,64,256]{3,2,1,0:T(8,128)} %bitcast.245), calls=%async_computation.12 | async-start | bytes 2097152 | tf_op jit(solution)/shard_map/all_to_all | solution.py:170
  631.3 17.8 %all-to-all-start.15 = ((f32[4,4,64,256]{3,2,1,0:T(8,128)}), f32[4,4,64,256]{3,2,1,0:T(8,128)}, u32[]{:S(2)}, u32[]{:S(2)}) async-start(f32[4,4,64,256]{3,2,1,0:T(8,128)} %bitcast.244), calls=%async_computation.15 | async-start | bytes 2097152 | tf_op jit(solution)/shard_map/all_to_all | solution.py:170
  649.1 16.8 %all-to-all-start.18 = ((f32[4,4,64,256]{3,2,1,0:T(8,128)}), f32[4,4,64,256]{3,2,1,0:T(8,128)S(1)}, u32[]{:S(2)}, u32[]{:S(2)}) async-start(f32[4,4,64,256]{3,2,1,0:T(8,128)} %bitcast.198), calls=%async_computation.18 | async-start | bytes 2097152 | tf_op jit(solution)/shard_map/all_to_all | solution.py:170
  666.9 16.6 %all-to-all-start.10 = ((f32[4,4,64,256]{3,2,1,0:T(8,128)}), f32[4,4,64,256]{3,2,1,0:T(8,128)S(1)}, u32[]{:S(2)}, u32[]{:S(2)}) async-start(f32[4,4,64,256]{3,2,1,0:T(8,128)} %bitcast.93), calls=%async_computation.10 | async-start | bytes 2097152 | tf_op jit(solution)/shard_map/all_to_all | solution.py:177
  683.4 16.6 %all-to-all-start.13 = ((f32[4,4,64,256]{3,2,1,0:T(8,128)}), f32[4,4,64,256]{3,2,1,0:T(8,128)S(1)}, u32[]{:S(2)}, u32[]{:S(2)}) async-start(f32[4,4,64,256]{3,2,1,0:T(8,128)} %bitcast.100), calls=%async_computation.13 | async-start | bytes 2097152 | tf_op jit(solution)/shard_map/all_to_all | solution.py:177
  700.0 16.6 %all-to-all-start.16 = ((f32[4,4,64,256]{3,2,1,0:T(8,128)}), f32[4,4,64,256]{3,2,1,0:T(8,128)S(1)}, u32[]{:S(2)}, u32[]{:S(2)}) async-start(f32[4,4,64,256]{3,2,1,0:T(8,128)} %bitcast.246), calls=%async_computation.16 | async-start | bytes 2097152 | tf_op jit(solution)/shard_map/all_to_all | solution.py:177
  716.6 17.6 %all-to-all-start.19 = ((f32[4,4,64,256]{3,2,1,0:T(8,128)}), f32[4,4,64,256]{3,2,1,0:T(8,128)}, u32[]{:S(2)}, u32[]{:S(2)}) async-start(f32[4,4,64,256]{3,2,1,0:T(8,128)} %bitcast.243), calls=%async_computation.19 | async-start | bytes 2097152 | tf_op jit(solution)/shard_map/all_to_all | solution.py:177
  (45 other events, 433.9 us)

commit v4 on v2

--- a/solution.py
+++ b/solution.py
@@ -126,33 +126,59 @@
         earlier = current
         current = following
 
-    width = vc * cb
-    chans = jnp.transpose(current.reshape(kl, rl, vc, n, cb), (3, 0, 1, 2, 4))
-    got = lax.all_to_all(chans.reshape(n, kl, rl, width), "rad", 0, 0, tiled=True)
-    radial_block = jnp.transpose(got.reshape(n, kl, rl, width), (1, 0, 2, 3)).reshape(
-        kl, radial, width
-    )
+    hel_index = lax.axis_index("hel")
     interp = interp_matrix(stencil, interp_weights, radial)
     qq = interp.shape[0]
     qb = qq // nh
-    placed = jnp.einsum(
-        "kqr,krm->kqm",
-        jnp.broadcast_to(interp, (kl, qq, radial)),
-        radial_block,
-        precision=PRECISE,
-        preferred_element_type=jnp.float32,
-    )
-    pieces = jnp.transpose(placed.reshape(kl, nh, qb, width), (1, 0, 2, 3))
-    gathered = lax.all_to_all(pieces, "hel", 0, 0, tiled=True)
-    turned = jnp.dot(
-        frame_rotation,
-        gathered.reshape(nh * kl, qb * width),
-        precision=PRECISE,
-        preferred_element_type=jnp.float32,
-    )
-    back = lax.all_to_all(turned.reshape(nh, kl, qb, width), "hel", 0, 0, tiled=True)
-    rotated = jnp.transpose(back.reshape(nh, kl, qb, width), (1, 0, 2, 3))
-    product_amp = rotated.reshape(kl, qq, vc, cb)
+    turn = jnp.arange(nh, dtype=jnp.int32)
+    q_rows = (lax.rem(hel_index + turn, nh)[:, None] * qb + jnp.arange(qb)[None, :]).reshape(-1)
+    interp_turned = jnp.broadcast_to(interp[q_rows], (kl, qq, radial))
+    k_cols = (lax.rem(hel_index - turn + nh, nh)[:, None] * kl + jnp.arange(kl)[None, :]).reshape(-1)
+    j_rows = (lax.rem(hel_index + turn, nh)[:, None] * kl + jnp.arange(kl)[None, :]).reshape(-1)
+    frame_turned = frame_rotation[j_rows][:, k_cols]
+
+    def hel_shift(x, d):
+        if d == 0:
+            return x
+        return lax.ppermute(x, "hel", [(i, (i + d) % nh) for i in range(nh)])
+
+    vchunks = 4 if vc % 4 == 0 else 1
+    vs = vc // vchunks
+    width = vs * cb
+    results = []
+    for i in range(vchunks):
+        part = current[:, :, i * vs:(i + 1) * vs, :]
+        chans = jnp.transpose(part.reshape(kl, rl, vs, n, cb), (3, 0, 1, 2, 4))
+        got = lax.all_to_all(chans.reshape(n, kl, rl, width), "rad", 0, 0, tiled=True)
+        radial_block = jnp.transpose(got.reshape(n, kl, rl, width), (1, 0, 2, 3)).reshape(
+            kl, radial, width
+        )
+        placed = jnp.einsum(
+            "kqr,krm->kqm",
+            interp_turned,
+            radial_block,
+            precision=PRECISE,
+            preferred_element_type=jnp.float32,
+        )
+        arrived = [hel_shift(placed[:, d * qb:(d + 1) * qb], d) for d in range(nh)]
+        gathered = jnp.stack(arrived, axis=0)
+        turned = jnp.dot(
+            frame_turned,
+            gathered.reshape(nh * kl, qb * width),
+            precision=PRECISE,
+            preferred_element_type=jnp.float32,
+        ).reshape(nh, kl, qb, width)
+        back = [hel_shift(turned[e], e) for e in range(nh)]
+        blocks = []
+        for block in range(nh):
+            source = lax.rem(hel_index - block + nh, nh)
+            pick = back[0]
+            for e in range(1, nh):
+                pick = jnp.where(source == e, back[e], pick)
+            blocks.append(pick)
+        rotated = jnp.concatenate(blocks, axis=1)
+        results.append(rotated.reshape(kl, qq, vs, cb))
+    product_amp = jnp.concatenate(results, axis=2)
     return (current, product_amp)
 
 

time: 746 us -> 712 us (0.954)
  blocking collectives: 298 us -> 197 us
  starting transfers between devices: 24.8 us -> 74.4 us
  other arithmetic: 3.25 us -> 16.1 us
    all_to_all x2 -> x0, blocking collectives: 101 us -> none  [the longest x1 51.2 us: shards(): gathered = lax.all_to_all(pieces, 'hel', 0, 0, tiled=True)]
    ppermute x0 -> x24, starting transfers between devices: none -> 39 us  [hel_shift(): return lax.ppermute(x, 'hel', [(i, (i + d) % nh) for i in range(nh)])]
    all_to_all x1 -> x4, waiting for transfers between devices: 93.6 us -> 70.3 us  [shards(): lax.all_to_all(chans.reshape(n, kl, rl, width), 'rad', 0, 0, tiled=True)]
    ppermute x0 -> x24, waiting for transfers between devices: none -> 18.8 us  [hel_shift(): return lax.ppermute(x, 'hel', [(i, (i + d) % nh) for i in range(nh)])]
    all_to_all x1 -> x4, starting transfers between devices: 4.69 us -> 15.1 us  [shards(): lax.all_to_all(chans.reshape(n, kl, rl, width), 'rad', 0, 0, tiled=True)]
    unnamed x38 -> x62, local copies, waits for them, and re-layouts: 22 us -> 11.9 us
    reshape x3 -> x8, local copies, waits for them, and re-layouts: 15.9 us -> 13.6 us  [shards(): chans = jnp.transpose(part.reshape(kl, rl, vs, n, cb), (3, 0, 1, 2, 4))]
  transfers between devices with their start and end apart: 7 -> 34, of which waited for: 3 -> 15; matrix products, arithmetic and copies ran while one was open for 12% -> 20% of each run, Pallas kernels for 0% -> 0%
where the time goes in v4:
time: 712 us; the launch traced here: 704 us
  waiting for transfers between devices  204 us (29%)
  blocking collectives  197 us (28%)
  local copies, waits for them, and re-layouts  123 us (17%)
  matrix products  87.6 us (12%)
  starting transfers between devices  74.4 us (10%)
  other arithmetic  16.1 us (2%)
    all_to_all x2, blocking collectives, to_radial_columns(): got = lax.all_to_all(blocks, 'rad', 0, 0, tiled=True).reshape(n, kl, rl, mb)  197 us
    all_to_all x2, waiting for transfers between devices, to_radial_rows(): got = lax.all_to_all(blocks, 'rad', 0, 0, tiled=True).reshape(n, kl, rl, mb)  115 us
    all_to_all x4, waiting for transfers between devices, shards(): lax.all_to_all(chans.reshape(n, kl, rl, width), 'rad', 0, 0, tiled=True)  70.3 us
    ppermute x24, starting transfers between devices, hel_shift(): return lax.ppermute(x, 'hel', [(i, (i + d) % nh) for i in range(nh)])  39 us
    dot_general x2, matrix products, hamiltonian(): jnp.dot(angles.reshape(-1, angles.shape[3]), transform, precision=PRECISE...  33.5 us
    dot_general x2, matrix products, hamiltonian(): jnp.dot(current.reshape(-1, cc), transform.T, precision=PRECISE, preferre...  23.2 us
    ppermute x24, waiting for transfers between devices, hel_shift(): return lax.ppermute(x, 'hel', [(i, (i + d) % nh) for i in range(nh)])  18.8 us
    reshape x3, local copies, waits for them, and re-layouts, to_radial_columns(): blocks = jnp.transpose(x.reshape(kl, rl, n, mb), (2, 0, 1, 3))  15.3 us
  transfers between devices with their start and end apart: 34, of which 15 were waited for; matrix products, arithmetic and copies ran while one was open for 20% of the time, Pallas kernels for 0%

profile of v4, /device:TPU:0, one launch (start us, length us, event | category | flops | bytes accessed | tf_op | source)
XLA Modules:
  0.0 703.5 jit_solution(12302073694200376326)
XLA Ops:
  0.6 5.3 reshape.324
  10.5 100.2 %all_to_all.40 = f32[8,4,32,1024]{3,2,1,0:T(8,128)S(1)} all-to-all(f32[8,4,32,1024]{3,2,1,0:T(8,128)S(1)} %copy.92), channel_id=1, replica_groups=mesh['hel'=4,'rad'=8] {'rad'}, dimensions={0} | all-to-all | bytes 8388608 | tf_op jit(solution)/shard_map/all_to_all | solution.py:73
  137.5 16.4 %convolution_bitcast_fusion = f32[2048,512]{0,1:T(8,128)} fusion(f32[512,512]{1,0:T(8,128)S(1)} %convolution_multiply_fusion, f32[2048,512]{1,0:T(8,128)} %bitcast.269), kind=kOutput, calls=%fused_computation.25 | convolution fusion | flops 6442450944 | bytes 9437184 | tf_op jit(solution)/shard_map/dot_general | solution.py:91
  153.9 5.8 copy.96
  159.7 7.9 %fusion.36 = f32[128,512,16]{1,2,0:T(8,128)} fusion(f32[128,16,512]{2,1,0:T(8,128)} %bitcast.272, f32[16,16]{1,0:T(8,128)S(1)} %copy-done.16), kind=kOutput, calls=%fused_computation.59 | convolution fusion | flops 201326592 | bytes 8389632 | tf_op jit(solution)/shard_map/buv,bva->bua/dot_general | solution.py:95
  167.6 48.5 %all-to-all-done.1 = f32[8,4,32,1024]{3,2,1,0:T(8,128)} async-done(((f32[8,4,32,1024]{3,2,1,0:T(8,128)}), f32[8,4,32,1024]{3,2,1,0:T(8,128)}, u32[]{:S(2)}, u32[]{:S(2)}) %all-to-all-start.1) | async-done | bytes 4194336 | tf_op jit(solution)/shard_map/all_to_all | solution.py:78
  216.1 6.6 copy.95
  222.7 4.9 reshape.327
  227.7 15.3 %broadcast_multiply_fusion = (f32[4,32,16,512]{3,2,1,0:T(8,128)}, f32[4,32,16,512]{3,2,1,0:T(8,128)}) fusion(f32[4,512]{1,0:T(4,128)S(1)} %copy-done.13, f32[4,32,16,512]{3,2,1,0:T(8,128)} %param.15, f32[3,32,16,512]{3,2,1,0:T(8,128)} %slice.199, f32[1,32,16,512]{3,2,1,0:T(8,128)S(1)} %collective-permute-done.1, ...), kind=kOutput, calls=%fused_computation.30 | convolution fusion | flops 6458179584 | bytes 34677056 | tf_op jit(solution)/shard_map/dot_general | solution.py:103
  243.0 5.4 reshape.331
  253.0 96.5 %all_to_all.41 = f32[8,4,32,1024]{3,2,1,0:T(8,128)S(1)} all-to-all(f32[8,4,32,1024]{3,2,1,0:T(8,128)S(1)} %bitcast.278), channel_id=1, replica_groups=mesh['hel'=4,'rad'=8] {'rad'}, dimensions={0} | all-to-all | bytes 8388608 | tf_op jit(solution)/shard_map/all_to_all | solution.py:73
  367.7 4.8 collective-permute-start.3
  376.4 6.9 fusion.24
  383.3 5.7 fusion.34
  389.0 66.5 %all-to-all-done.3 = f32[8,4,32,1024]{3,2,1,0:T(8,128)} async-done(((f32[8,4,32,1024]{3,2,1,0:T(8,128)}), f32[8,4,32,1024]{3,2,1,0:T(8,128)}, u32[]{:S(2)}, u32[]{:S(2)}) %all-to-all-start.3) | async-done | bytes 4194336 | tf_op jit(solution)/shard_map/all_to_all | solution.py:78
  455.4 6.6 copy.100
  462.1 5.0 reshape.334
  467.1 18.2 %fusion.11 = f32[4,32,16,512]{3,2,1,0:T(8,128)S(1)} fusion(f32[1,32,16,512]{3,2,1,0:T(8,128)S(1)} %collective-permute-done.2, f32[3,32,16,512]{3,2,1,0:T(8,128)} %slice.200, f32[3,32,16,512]{3,2,1,0:T(8,128)} %slice.203, f32[1,32,16,512]{3,2,1,0:T(8,128)S(1)} %collective-permute-done.3, f32[4,32,16,512]{3,2,1,0:T(8,128)} %param.16, ...), kind=kOutput, calls=%fused_computation.16 | convolution fusion | flops 6457131008 | bytes 30482752 | tf_op jit(solution)/shard_map/dot_general | solution.py:103
  504.4 19.6 %all-to-all-done.4 = f32[8,4,32,256]{3,2,1,0:T(8,128)S(1)} async-done(((f32[8,4,32,256]{3,2,1,0:T(8,128)}), f32[8,4,32,256]{3,2,1,0:T(8,128)S(1)}, u32[]{:S(2)}, u32[]{:S(2)}) %all-to-all-start.4) | async-done | bytes 1048608 | tf_op jit(solution)/shard_map/all_to_all | solution.py:152
  535.5 19.6 %all-to-all-done.5 = f32[8,4,32,256]{3,2,1,0:T(8,128)S(1)} async-done(((f32[8,4,32,256]{3,2,1,0:T(8,128)}), f32[8,4,32,256]{3,2,1,0:T(8,128)S(1)}, u32[]{:S(2)}, u32[]{:S(2)}) %all-to-all-start.5) | async-done | bytes 1048608 | tf_op jit(solution)/shard_map/all_to_all | solution.py:152
  567.0 19.1 %all-to-all-done.6 = f32[8,4,32,256]{3,2,1,0:T(8,128)S(1)} async-done(((f32[8,4,32,256]{3,2,1,0:T(8,128)}), f32[8,4,32,256]{3,2,1,0:T(8,128)S(1)}, u32[]{:S(2)}, u32[]{:S(2)}) %all-to-all-start.6) | async-done | bytes 1048608 | tf_op jit(solution)/shard_map/all_to_all | solution.py:152
  605.3 11.9 %all-to-all-done.7 = f32[8,4,32,256]{3,2,1,0:T(8,128)} async-done(((f32[8,4,32,256]{3,2,1,0:T(8,128)}), f32[8,4,32,256]{3,2,1,0:T(8,128)}, u32[]{:S(2)}, u32[]{:S(2)}) %all-to-all-start.7) | async-done | bytes 1048608 | tf_op jit(solution)/shard_map/all_to_all | solution.py:152
  670.9 6.4 collective-permute-start.25
  691.6 4.8 collective-permute-done.27
  (213 shorter events, 193.7 us)
Async XLA Ops:
  117.4 98.7 %all-to-all-start.1 = ((f32[8,4,32,1024]{3,2,1,0:T(8,128)}), f32[8,4,32,1024]{3,2,1,0:T(8,128)}, u32[]{:S(2)}, u32[]{:S(2)}) async-start(f32[8,4,32,1024]{3,2,1,0:T(8,128)} %bitcast.273), calls=%async_computation.1 | async-start | bytes 8388608 | tf_op jit(solution)/shard_map/all_to_all | solution.py:78
  126.1 101.6 %collective-permute-start.1 = (f32[1,32,16,512]{3,2,1,0:T(8,128)}, f32[1,32,16,512]{3,2,1,0:T(8,128)S(1)}, u32[]{:S(2)}, u32[]{:S(2)}) collective-permute-start(f32[1,32,16,512]{3,2,1,0:T(8,128)} %slice.198), channel_id=1, source_target_pairs={{0,8},{8,16},{16,24},{1,9},{9,17},{17,25},{2,10},{10,18},{18,26},{... | collective-permute-start | bytes 3145736 | tf_op jit(solution)/shard_map/ppermute | solution.py:13
  130.6 97.1 %collective-permute-start = (f32[1,32,16,512]{3,2,1,0:T(8,128)}, f32[1,32,16,512]{3,2,1,0:T(8,128)S(1)}, u32[]{:S(2)}, u32[]{:S(2)}) collective-permute-start(f32[1,32,16,512]{3,2,1,0:T(8,128)} %slice.149), channel_id=1, source_target_pairs={{8,0},{16,8},{24,16},{9,1},{17,9},{25,17},{10,2},{18,10},{26,18},{... | collective-permute-start | bytes 3145736 | tf_op jit(solution)/shard_map/ppermute | solution.py:13
  356.8 98.6 %all-to-all-start.3 = ((f32[8,4,32,1024]{3,2,1,0:T(8,128)}), f32[8,4,32,1024]{3,2,1,0:T(8,128)}, u32[]{:S(2)}, u32[]{:S(2)}) async-start(f32[8,4,32,1024]{3,2,1,0:T(8,128)} %bitcast.274), calls=%async_computation.3 | async-start | bytes 8388608 | tf_op jit(solution)/shard_map/all_to_all | solution.py:78
  363.9 103.1 %collective-permute-start.2 = (f32[1,32,16,512]{3,2,1,0:T(8,128)}, f32[1,32,16,512]{3,2,1,0:T(8,128)S(1)}, u32[]{:S(2)}, u32[]{:S(2)}) collective-permute-start(f32[1,32,16,512]{3,2,1,0:T(8,128)} %slice.201), channel_id=1, source_target_pairs={{8,0},{16,8},{24,16},{9,1},{17,9},{25,17},{10,2},{18,10},{26,18},{... | collective-permute-start | bytes 3145736 | tf_op jit(solution)/shard_map/ppermute | solution.py:13
  367.7 99.4 %collective-permute-start.3 = (f32[1,32,16,512]{3,2,1,0:T(8,128)}, f32[1,32,16,512]{3,2,1,0:T(8,128)S(1)}, u32[]{:S(2)}, u32[]{:S(2)}) collective-permute-start(f32[1,32,16,512]{3,2,1,0:T(8,128)} %slice.202), channel_id=1, source_target_pairs={{0,8},{8,16},{16,24},{1,9},{9,17},{17,25},{2,10},{10,18},{18,26},{... | collective-permute-start | bytes 3145736 | tf_op jit(solution)/shard_map/ppermute | solution.py:13
  494.0 30.1 %all-to-all-start.4 = ((f32[8,4,32,256]{3,2,1,0:T(8,128)}), f32[8,4,32,256]{3,2,1,0:T(8,128)S(1)}, u32[]{:S(2)}, u32[]{:S(2)}) async-start(f32[8,4,32,256]{3,2,1,0:T(8,128)} %reshape.337), calls=%async_computation.4 | async-start | bytes 2097152 | tf_op jit(solution)/shard_map/all_to_all | solution.py:152
  525.0 30.1 %all-to-all-start.5 = ((f32[8,4,32,256]{3,2,1,0:T(8,128)}), f32[8,4,32,256]{3,2,1,0:T(8,128)S(1)}, u32[]{:S(2)}, u32[]{:S(2)}) async-start(f32[8,4,32,256]{3,2,1,0:T(8,128)} %reshape.342), calls=%async_computation.5 | async-start | bytes 2097152 | tf_op jit(solution)/shard_map/all_to_all | solution.py:152
  556.1 30.1 %all-to-all-start.6 = ((f32[8,4,32,256]{3,2,1,0:T(8,128)}), f32[8,4,32,256]{3,2,1,0:T(8,128)S(1)}, u32[]{:S(2)}, u32[]{:S(2)}) async-start(f32[8,4,32,256]{3,2,1,0:T(8,128)} %reshape.347), calls=%async_computation.6 | async-start | bytes 2097152 | tf_op jit(solution)/shard_map/all_to_all | solution.py:152
  586.2 31.0 %all-to-all-start.7 = ((f32[8,4,32,256]{3,2,1,0:T(8,128)}), f32[8,4,32,256]{3,2,1,0:T(8,128)}, u32[]{:S(2)}, u32[]{:S(2)}) async-start(f32[8,4,32,256]{3,2,1,0:T(8,128)} %reshape.352), calls=%async_computation.7 | async-start | bytes 2097152 | tf_op jit(solution)/shard_map/all_to_all | solution.py:152
  596.6 23.2 %collective-permute-start.4 = (f32[4,64,256]{2,1,0:T(8,128)}, f32[4,64,256]{2,1,0:T(8,128)}, u32[]{:S(2)}, u32[]{:S(2)}) collective-permute-start(f32[4,64,256]{2,1,0:T(8,128)} %get-tuple-element.17), channel_id=1, source_target_pairs={{0,8},{8,16},{16,24},{24,0},{1,9},{9,17},{17,25},{25,1},{2,10},{10... | collective-permute-start | bytes 786440 | tf_op jit(solution)/shard_map/ppermute | solution.py:143
  598.1 24.2 %collective-permute-start.5 = (f32[4,64,256]{2,1,0:T(8,128)}, f32[4,64,256]{2,1,0:T(8,128)}, u32[]{:S(2)}, u32[]{:S(2)}) collective-permute-start(f32[4,64,256]{2,1,0:T(8,128)} %get-tuple-element.16), channel_id=1, source_target_pairs={{0,16},{8,24},{16,0},{24,8},{1,17},{9,25},{17,1},{25,9},{2,18},{10... | collective-permute-start | bytes 786440 | tf_op jit(solution)/shard_map/ppermute | solution.py:143
  599.6 22.7 %collective-permute-start.6 = (f32[4,64,256]{2,1,0:T(8,128)}, f32[4,64,256]{2,1,0:T(8,128)}, u32[]{:S(2)}, u32[]{:S(2)}) collective-permute-start(f32[4,64,256]{2,1,0:T(8,128)} %get-tuple-element.15), channel_id=1, source_target_pairs={{0,24},{8,0},{16,8},{24,16},{1,25},{9,1},{17,9},{25,17},{2,26},{10... | collective-permute-start | bytes 786440 | tf_op jit(solution)/shard_map/ppermute | solution.py:143
  603.1 23.4 %collective-permute-start.10 = (f32[4,64,256]{2,1,0:T(8,128)}, f32[4,64,256]{2,1,0:T(8,128)}, u32[]{:S(2)}, u32[]{:S(2)}) collective-permute-start(f32[4,64,256]{2,1,0:T(8,128)} %get-tuple-element.29), channel_id=1, source_target_pairs={{0,8},{8,16},{16,24},{24,0},{1,9},{9,17},{17,25},{25,1},{2,10},{10... | collective-permute-start | bytes 786440 | tf_op jit(solution)/shard_map/ppermute | solution.py:143
  603.7 25.2 %collective-permute-start.11 = (f32[4,64,256]{2,1,0:T(8,128)}, f32[4,64,256]{2,1,0:T(8,128)}, u32[]{:S(2)}, u32[]{:S(2)}) collective-permute-start(f32[4,64,256]{2,1,0:T(8,128)} %get-tuple-element.28), channel_id=1, source_target_pairs={{0,16},{8,24},{16,0},{24,8},{1,17},{9,25},{17,1},{25,9},{2,18},{10... | collective-permute-start | bytes 786440 | tf_op jit(solution)/shard_map/ppermute | solution.py:143
  628.8 18.1 %collective-permute-start.22 = (f32[4,64,256]{2,1,0:T(8,128)S(1)}, f32[4,64,256]{2,1,0:T(8,128)S(1)}, u32[]{:S(2)}, u32[]{:S(2)}) collective-permute-start(f32[4,64,256]{2,1,0:T(8,128)S(1)} %get-tuple-element.53), channel_id=1, source_target_pairs={{0,8},{8,16},{16,24},{24,0},{1,9},{9,17},{17,25},{25,1},{2,10},{10... | collective-permute-start | bytes 786440 | tf_op jit(solution)/shard_map/ppermute | solution.py:143
  629.1 19.4 %collective-permute-start.23 = (f32[4,64,256]{2,1,0:T(8,128)S(1)}, f32[4,64,256]{2,1,0:T(8,128)S(1)}, u32[]{:S(2)}, u32[]{:S(2)}) collective-permute-start(f32[4,64,256]{2,1,0:T(8,128)S(1)} %get-tuple-element.52), channel_id=1, source_target_pairs={{0,16},{8,24},{16,0},{24,8},{1,17},{9,25},{17,1},{25,9},{2,18},{10... | collective-permute-start | bytes 786440 | tf_op jit(solution)/shard_map/ppermute | solution.py:143
  637.1 23.9 %collective-permute-start.7 = (f32[4,64,256]{2,1,0:T(8,128)S(1)}, f32[4,64,256]{2,1,0:T(8,128)S(1)}, u32[]{:S(2)}, u32[]{:S(2)}) collective-permute-start(f32[4,64,256]{2,1,0:T(8,128)S(1)} %bitcast.327), channel_id=1, source_target_pairs={{0,24},{8,0},{16,8},{24,16},{1,25},{9,1},{17,9},{25,17},{2,26},{10... | collective-permute-start | bytes 786440 | tf_op jit(solution)/shard_map/ppermute | solution.py:143
  640.3 23.2 %collective-permute-start.8 = (f32[4,64,256]{2,1,0:T(8,128)S(1)}, f32[4,64,256]{2,1,0:T(8,128)S(1)}, u32[]{:S(2)}, u32[]{:S(2)}) collective-permute-start(f32[4,64,256]{2,1,0:T(8,128)S(1)} %bitcast.326), channel_id=1, source_target_pairs={{0,16},{8,24},{16,0},{24,8},{1,17},{9,25},{17,1},{25,9},{2,18},{10... | collective-permute-start | bytes 786440 | tf_op jit(solution)/shard_map/ppermute | solution.py:143
  647.0 19.2 %collective-permute-start.9 = (f32[4,64,256]{2,1,0:T(8,128)S(1)}, f32[4,64,256]{2,1,0:T(8,128)S(1)}, u32[]{:S(2)}, u32[]{:S(2)}) collective-permute-start(f32[4,64,256]{2,1,0:T(8,128)S(1)} %bitcast.329), channel_id=1, source_target_pairs={{0,8},{8,16},{16,24},{24,0},{1,9},{9,17},{17,25},{25,1},{2,10},{10... | collective-permute-start | bytes 786440 | tf_op jit(solution)/shard_map/ppermute | solution.py:143
  648.4 20.2 %collective-permute-start.13 = (f32[4,64,256]{2,1,0:T(8,128)}, f32[4,64,256]{2,1,0:T(8,128)S(1)}, u32[]{:S(2)}, u32[]{:S(2)}) collective-permute-start(f32[4,64,256]{2,1,0:T(8,128)} %bitcast.265), channel_id=1, source_target_pairs={{0,24},{8,0},{16,8},{24,16},{1,25},{9,1},{17,9},{25,17},{2,26},{10... | collective-permute-start | bytes 786440 | tf_op jit(solution)/shard_map/ppermute | solution.py:143
  651.6 19.3 %collective-permute-start.14 = (f32[4,64,256]{2,1,0:T(8,128)}, f32[4,64,256]{2,1,0:T(8,128)S(1)}, u32[]{:S(2)}, u32[]{:S(2)}) collective-permute-start(f32[4,64,256]{2,1,0:T(8,128)} %bitcast.264), channel_id=1, source_target_pairs={{0,16},{8,24},{16,0},{24,8},{1,17},{9,25},{17,1},{25,9},{2,18},{10... | collective-permute-start | bytes 786440 | tf_op jit(solution)/shard_map/ppermute | solution.py:143
  668.6 17.8 %collective-permute-start.21 = (f32[4,64,256]{2,1,0:T(8,128)}, f32[4,64,256]{2,1,0:T(8,128)S(1)}, u32[]{:S(2)}, u32[]{:S(2)}) collective-permute-start(f32[4,64,256]{2,1,0:T(8,128)} %bitcast.328), channel_id=1, source_target_pairs={{0,8},{8,16},{16,24},{24,0},{1,9},{9,17},{17,25},{25,1},{2,10},{10... | collective-permute-start | bytes 786440 | tf_op jit(solution)/shard_map/ppermute | solution.py:143
  670.9 20.6 %collective-permute-start.25 = (f32[4,64,256]{2,1,0:T(8,128)}, f32[4,64,256]{2,1,0:T(8,128)}, u32[]{:S(2)}, u32[]{:S(2)}) collective-permute-start(f32[4,64,256]{2,1,0:T(8,128)} %bitcast.325), channel_id=1, source_target_pairs={{0,24},{8,0},{16,8},{24,16},{1,25},{9,1},{17,9},{25,17},{2,26},{10... | collective-permute-start | bytes 786440 | tf_op jit(solution)/shard_map/ppermute | solution.py:143
  (33 other events, 433.4 us)

commit v5 on v4

--- a/solution.py
+++ b/solution.py
@@ -78,16 +78,16 @@
         got = lax.all_to_all(blocks, "rad", 0, 0, tiled=True).reshape(n, kl, rl, mb)
         return jnp.transpose(got, (1, 2, 0, 3)).reshape(kl, rl, vc, cc)
 
-    def hamiltonian(current):
-        columns = to_radial_columns(current)
-        applied = jnp.einsum(
+    def kinetic(columns):
+        return jnp.einsum(
             "krs,ksm->krm",
             kinetic_batched,
             columns,
             precision=PRECISE,
             preferred_element_type=jnp.float32,
         )
-        kinetic_image = to_radial_rows(applied)
+
+    def local_part(current):
         angles = jnp.dot(
             current.reshape(-1, cc), transform.T, precision=PRECISE,
             preferred_element_type=jnp.float32,
@@ -112,19 +112,24 @@
         upper_side = jnp.concatenate([current[1:], from_above], axis=0)
         lower_side = jnp.concatenate([from_below, weighted[:-1]], axis=0)
         return (
-            kinetic_image
-            + (angular.reshape(current.shape) + vib_energy[None, None, :, None] * current)
-            + radial_local[None, :, None, None]
-            * (coriolis[:, None, None, :] * upper_side + lower_side)
-        )
-
+            angular.reshape(current.shape) + vib_energy[None, None, :, None] * current
+        ) + radial_local[None, :, None, None] * (
+            coriolis[:, None, None, :] * upper_side + lower_side
+        )
+
+    damp_columns = damping[None, :, None]
     earlier = prev_vector
     current = curr_vector
-    for iteration in range(STEPS):
-        image = hamiltonian(current)
-        following = damp_full * (2.0 * image - damp_full * earlier)
+    columns = to_radial_columns(current)
+    for iteration in range(STEPS - 1):
+        rest = damp_full * (2.0 * local_part(current) - damp_full * earlier)
+        following_columns = damp_columns * (2.0 * kinetic(columns)) + to_radial_columns(rest)
         earlier = current
-        current = following
+        current = to_radial_rows(following_columns)
+        columns = following_columns
+    kinetic_image = to_radial_rows(kinetic(columns))
+    image = kinetic_image + local_part(current)
+    current = damp_full * (2.0 * image - damp_full * earlier)
 
     hel_index = lax.axis_index("hel")
     interp = interp_matrix(stencil, interp_weights, radial)

time: 712 us -> 691 us (0.971)
  blocking collectives: 197 us -> 0 us
  waiting for transfers between devices: 204 us -> 355 us
  local copies, waits for them, and re-layouts: 123 us -> 149 us
  matrix products: 87.6 us -> 78.1 us
  starting transfers between devices: 74.4 us -> 83.1 us
    all_to_all x2 -> x0, blocking collectives: 197 us -> none  [to_radial_columns(): got = lax.all_to_all(blocks, 'rad', 0, 0, tiled=True).reshape(n, kl, rl, mb)]
    all_to_all x0 -> x2, waiting for transfers between devices: none -> 116 us  [to_radial_columns(): got = lax.all_to_all(blocks, 'rad', 0, 0, tiled=True).reshape(n, kl, rl, mb)]
    all_to_all x2, waiting for transfers between devices: 115 us -> 146 us  [to_radial_rows(): got = lax.all_to_all(blocks, 'rad', 0, 0, tiled=True).reshape(n, kl, rl, mb)]
    all_to_all x0 -> x2, starting transfers between devices: none -> 11.5 us  [to_radial_columns(): got = lax.all_to_all(blocks, 'rad', 0, 0, tiled=True).reshape(n, kl, rl, mb)]
    dot_general x8, matrix products: 78.1 us -> 68.6 us  [the longest x2 25 us: local_part(): jnp.dot(current.reshape(-1, cc), transform.T, precision=PRECISE, preferre...]
    slice x8 -> x14, local copies, waits for them, and re-layouts: 14.8 us -> 23.6 us  [the longest x4 15.9 us: local_part(): upper_side = jnp.concatenate([current[1:], from_above], axis=0)]
  transfers between devices with their start and end apart: 34 -> 36, of which waited for: 15 -> 18; matrix products, arithmetic and copies ran while one was open for 20% -> 28% of each run, Pallas kernels for 0% -> 0%
where the time goes in v5:
time: 691 us; the launch traced here: 685 us
  waiting for transfers between devices  355 us (51%)
  local copies, waits for them, and re-layouts  149 us (22%)
  starting transfers between devices  83.1 us (12%)
  matrix products  78.1 us (11%)
  other arithmetic  18.5 us (3%)
    all_to_all x2, waiting for transfers between devices, to_radial_rows(): got = lax.all_to_all(blocks, 'rad', 0, 0, tiled=True).reshape(n, kl, rl, mb)  146 us
    all_to_all x2, waiting for transfers between devices, to_radial_columns(): got = lax.all_to_all(blocks, 'rad', 0, 0, tiled=True).reshape(n, kl, rl, mb)  116 us
    all_to_all x4, waiting for transfers between devices, shards(): lax.all_to_all(chans.reshape(n, kl, rl, width), 'rad', 0, 0, tiled=True)  68.4 us
    ppermute x24, starting transfers between devices, hel_shift(): return lax.ppermute(x, 'hel', [(i, (i + d) % nh) for i in range(nh)])  34.9 us
    dot_general x2, matrix products, local_part(): jnp.dot(current.reshape(-1, cc), transform.T, precision=PRECISE, preferre...  25 us
    ppermute x24, waiting for transfers between devices, hel_shift(): return lax.ppermute(x, 'hel', [(i, (i + d) % nh) for i in range(nh)])  24.9 us
    dot_general x2, matrix products, local_part(): jnp.dot(angles.reshape(-1, angles.shape[3]), transform, precision=PRECISE...  23 us
    reshape x3, local copies, waits for them, and re-layouts, to_radial_columns(): blocks = jnp.transpose(x.reshape(kl, rl, n, mb), (2, 0, 1, 3))  17.1 us
  transfers between devices with their start and end apart: 36, of which 18 were waited for; matrix products, arithmetic and copies ran while one was open for 28% of the time, Pallas kernels for 0%

profile of v5, /device:TPU:0, one launch (start us, length us, event | category | flops | bytes accessed | tf_op | source)
XLA Modules:
  0.0 685.2 jit_solution(70113601354472805)
XLA Ops:
  0.6 5.3 reshape.326
  5.9 6.7 copy.100
  12.6 6.5 all-to-all-start
  35.7 16.4 %convolution_bitcast_fusion = f32[2048,512]{0,1:T(8,128)} fusion(f32[512,512]{1,0:T(8,128)S(1)} %convolution_multiply_fusion, f32[2048,512]{1,0:T(8,128)} %bitcast.273), kind=kOutput, calls=%fused_computation.27 | convolution fusion | flops 6442450944 | bytes 9437184 | tf_op jit(solution)/shard_map/dot_general | solution.py:91
  52.1 5.4 copy.102
  57.6 5.7 fusion.37
  63.3 11.5 %fusion.5 = f32[4,32,16,512]{3,2,1,0:T(8,128)} fusion(f32[1,32,16,512]{3,2,1,0:T(8,128)S(1)} %collective-permute-done, f32[3,32,16,512]{3,2,1,0:T(8,128)} %slice.154, f32[3,32,16,512]{3,2,1,0:T(8,128)S(1)} %slice-done.1, f32[1,32,16,512]{3,2,1,0:T(8,128)S(1)} %collective-permute-done.1, f32[4,32,16,512]{3,2,1,0:T(8,128)} %param.15, ...), kind=kOutput, calls=%fused_computation.9 | convolution fusion | flops 6456082432 | bytes 26288448 | tf_op jit(solution)/shard_map/dot_general | solution.py:103
  74.8 5.2 reshape.331
  80.1 6.6 copy.183
  86.7 26.5 %all-to-all-done = f32[8,4,32,1024]{3,2,1,0:T(8,128)} async-done(((f32[8,4,32,1024]{3,2,1,0:T(8,128)}), f32[8,4,32,1024]{3,2,1,0:T(8,128)}, u32[]{:S(2)}, u32[]{:S(2)}) %all-to-all-start) | async-done | bytes 4194336 | tf_op jit(solution)/shard_map/all_to_all | solution.py:73
  123.1 89.2 %all-to-all-done.1 = f32[8,4,32,1024]{3,2,1,0:T(8,128)} async-done(((f32[8,4,32,1024]{3,2,1,0:T(8,128)}), f32[8,4,32,1024]{3,2,1,0:T(8,128)}, u32[]{:S(2)}, u32[]{:S(2)}) %all-to-all-start.1) | async-done | bytes 4194336 | tf_op jit(solution)/shard_map/all_to_all | solution.py:73
  227.6 5.6 fusion.39
  235.8 85.7 %all-to-all-done.3 = f32[8,4,32,1024]{3,2,1,0:T(8,128)} async-done(((f32[8,4,32,1024]{3,2,1,0:T(8,128)}), f32[8,4,32,1024]{3,2,1,0:T(8,128)}, u32[]{:S(2)}, u32[]{:S(2)}) %all-to-all-start.3) | async-done | bytes 4194336 | tf_op jit(solution)/shard_map/all_to_all | solution.py:78
  327.4 6.6 copy.108
  359.7 60.4 %all-to-all-done.2 = f32[8,4,32,1024]{3,2,1,0:T(8,128)} async-done(((f32[8,4,32,1024]{3,2,1,0:T(8,128)}), f32[8,4,32,1024]{3,2,1,0:T(8,128)}, u32[]{:S(2)}, u32[]{:S(2)}) %all-to-all-start.2) | async-done | bytes 4194336 | tf_op jit(solution)/shard_map/all_to_all | solution.py:78
  420.1 6.6 copy.106
  431.7 5.4 copy.110
  441.7 8.7 %fusion.25 = f32[128,16,512]{2,1,0:T(8,128)S(1)} fusion(f32[128,16,512]{2,1,0:T(8,128)} %dot_general.74, f32[512,512]{1,0:T(8,128)S(1)} %convolution_multiply_fusion), kind=kOutput, calls=%fused_computation.47 | convolution fusion | flops 6442450944 | bytes 9437184 | tf_op jit(solution)/shard_map/dot_general | solution.py:91
  450.3 5.2 fusion.35
  455.6 11.5 %fusion.12 = f32[4,32,16,512]{3,2,1,0:T(8,128)S(1)} fusion(f32[4,32,16,512]{3,2,1,0:T(8,128)} %reshape.334, f32[1,32,16,512]{3,2,1,0:T(8,128)S(1)} %collective-permute-done.2, f32[3,32,16,512]{3,2,1,0:T(8,128)} %slice.159, f32[3,32,16,512]{3,2,1,0:T(8,128)S(1)} %slice-done, f32[1,32,16,512]{3,2,1,0:T(8,128)S(1)} %collective-permute-done.3, ...), kind=kOutput, calls=%fused_computation.17 | convolution fusion | flops 6457131008 | bytes 30482752 | tf_op jit(solution)/shard_map/dot_general | solution.py:103
  486.3 19.6 %all-to-all-done.7 = f32[8,4,32,256]{3,2,1,0:T(8,128)S(1)} async-done(((f32[8,4,32,256]{3,2,1,0:T(8,128)}), f32[8,4,32,256]{3,2,1,0:T(8,128)S(1)}, u32[]{:S(2)}, u32[]{:S(2)}) %all-to-all-start.7) | async-done | bytes 1048608 | tf_op jit(solution)/shard_map/all_to_all | solution.py:157
  517.8 19.6 %all-to-all-done.6 = f32[8,4,32,256]{3,2,1,0:T(8,128)S(1)} async-done(((f32[8,4,32,256]{3,2,1,0:T(8,128)}), f32[8,4,32,256]{3,2,1,0:T(8,128)S(1)}, u32[]{:S(2)}, u32[]{:S(2)}) %all-to-all-start.6) | async-done | bytes 1048608 | tf_op jit(solution)/shard_map/all_to_all | solution.py:157
  549.4 19.1 %all-to-all-done.5 = f32[8,4,32,256]{3,2,1,0:T(8,128)S(1)} async-done(((f32[8,4,32,256]{3,2,1,0:T(8,128)}), f32[8,4,32,256]{3,2,1,0:T(8,128)S(1)}, u32[]{:S(2)}, u32[]{:S(2)}) %all-to-all-start.5) | async-done | bytes 1048608 | tf_op jit(solution)/shard_map/all_to_all | solution.py:157
  589.2 10.1 %all-to-all-done.4 = f32[8,4,32,256]{3,2,1,0:T(8,128)} async-done(((f32[8,4,32,256]{3,2,1,0:T(8,128)}), f32[8,4,32,256]{3,2,1,0:T(8,128)}, u32[]{:S(2)}, u32[]{:S(2)}) %all-to-all-start.4) | async-done | bytes 1048608 | tf_op jit(solution)/shard_map/all_to_all | solution.py:157
  (236 shorter events, 234.4 us)
Async XLA Ops:
  12.6 100.6 %all-to-all-start = ((f32[8,4,32,1024]{3,2,1,0:T(8,128)}), f32[8,4,32,1024]{3,2,1,0:T(8,128)}, u32[]{:S(2)}, u32[]{:S(2)}) async-start(f32[8,4,32,1024]{3,2,1,0:T(8,128)} %copy.100), calls=%async_computation | async-start | bytes 8388608 | tf_op jit(solution)/shard_map/all_to_all | solution.py:73
  21.4 41.9 %collective-permute-start = (f32[1,32,16,512]{3,2,1,0:T(8,128)}, f32[1,32,16,512]{3,2,1,0:T(8,128)S(1)}, u32[]{:S(2)}, u32[]{:S(2)}) collective-permute-start(f32[1,32,16,512]{3,2,1,0:T(8,128)} %slice.155), channel_id=1, source_target_pairs={{8,0},{16,8},{24,16},{9,1},{17,9},{25,17},{10,2},{18,10},{26,18},{... | collective-permute-start | bytes 3145736 | tf_op jit(solution)/shard_map/ppermute | solution.py:13
  26.8 36.4 %collective-permute-start.1 = (f32[1,32,16,512]{3,2,1,0:T(8,128)}, f32[1,32,16,512]{3,2,1,0:T(8,128)S(1)}, u32[]{:S(2)}, u32[]{:S(2)}) collective-permute-start(f32[1,32,16,512]{3,2,1,0:T(8,128)} %slice.206), channel_id=1, source_target_pairs={{0,8},{8,16},{16,24},{1,9},{9,17},{17,25},{2,10},{10,18},{18,26},{... | collective-permute-start | bytes 3145736 | tf_op jit(solution)/shard_map/ppermute | solution.py:13
  113.2 99.1 %all-to-all-start.1 = ((f32[8,4,32,1024]{3,2,1,0:T(8,128)}), f32[8,4,32,1024]{3,2,1,0:T(8,128)}, u32[]{:S(2)}, u32[]{:S(2)}) async-start(f32[8,4,32,1024]{3,2,1,0:T(8,128)} %bitcast.278), calls=%async_computation.1 | async-start | bytes 8388608 | tf_op jit(solution)/shard_map/all_to_all | solution.py:73
  223.0 98.6 %all-to-all-start.3 = ((f32[8,4,32,1024]{3,2,1,0:T(8,128)}), f32[8,4,32,1024]{3,2,1,0:T(8,128)}, u32[]{:S(2)}, u32[]{:S(2)}) async-start(f32[8,4,32,1024]{3,2,1,0:T(8,128)} %bitcast.279), calls=%async_computation.3 | async-start | bytes 8388608 | tf_op jit(solution)/shard_map/all_to_all | solution.py:78
  321.6 98.6 %all-to-all-start.2 = ((f32[8,4,32,1024]{3,2,1,0:T(8,128)}), f32[8,4,32,1024]{3,2,1,0:T(8,128)}, u32[]{:S(2)}, u32[]{:S(2)}) async-start(f32[8,4,32,1024]{3,2,1,0:T(8,128)} %bitcast.277), calls=%async_computation.2 | async-start | bytes 8388608 | tf_op jit(solution)/shard_map/all_to_all | solution.py:78
  335.8 119.8 %collective-permute-start.2 = (f32[1,32,16,512]{3,2,1,0:T(8,128)}, f32[1,32,16,512]{3,2,1,0:T(8,128)S(1)}, u32[]{:S(2)}, u32[]{:S(2)}) collective-permute-start(f32[1,32,16,512]{3,2,1,0:T(8,128)} %slice.161), channel_id=1, source_target_pairs={{8,0},{16,8},{24,16},{9,1},{17,9},{25,17},{10,2},{18,10},{26,18},{... | collective-permute-start | bytes 3145736 | tf_op jit(solution)/shard_map/ppermute | solution.py:13
  346.2 109.3 %collective-permute-start.3 = (f32[1,32,16,512]{3,2,1,0:T(8,128)}, f32[1,32,16,512]{3,2,1,0:T(8,128)S(1)}, u32[]{:S(2)}, u32[]{:S(2)}) collective-permute-start(f32[1,32,16,512]{3,2,1,0:T(8,128)} %slice.210), channel_id=1, source_target_pairs={{0,8},{8,16},{16,24},{1,9},{9,17},{17,25},{2,10},{10,18},{18,26},{... | collective-permute-start | bytes 3145736 | tf_op jit(solution)/shard_map/ppermute | solution.py:13
  475.8 30.1 %all-to-all-start.7 = ((f32[8,4,32,256]{3,2,1,0:T(8,128)}), f32[8,4,32,256]{3,2,1,0:T(8,128)S(1)}, u32[]{:S(2)}, u32[]{:S(2)}) async-start(f32[8,4,32,256]{3,2,1,0:T(8,128)} %reshape.354), calls=%async_computation.7 | async-start | bytes 2097152 | tf_op jit(solution)/shard_map/all_to_all | solution.py:157
  506.9 30.5 %all-to-all-start.6 = ((f32[8,4,32,256]{3,2,1,0:T(8,128)}), f32[8,4,32,256]{3,2,1,0:T(8,128)S(1)}, u32[]{:S(2)}, u32[]{:S(2)}) async-start(f32[8,4,32,256]{3,2,1,0:T(8,128)} %reshape.349), calls=%async_computation.6 | async-start | bytes 2097152 | tf_op jit(solution)/shard_map/all_to_all | solution.py:157
  538.3 30.1 %all-to-all-start.5 = ((f32[8,4,32,256]{3,2,1,0:T(8,128)}), f32[8,4,32,256]{3,2,1,0:T(8,128)S(1)}, u32[]{:S(2)}, u32[]{:S(2)}) async-start(f32[8,4,32,256]{3,2,1,0:T(8,128)} %reshape.344), calls=%async_computation.5 | async-start | bytes 2097152 | tf_op jit(solution)/shard_map/all_to_all | solution.py:157
  568.4 30.9 %all-to-all-start.4 = ((f32[8,4,32,256]{3,2,1,0:T(8,128)}), f32[8,4,32,256]{3,2,1,0:T(8,128)}, u32[]{:S(2)}, u32[]{:S(2)}) async-start(f32[8,4,32,256]{3,2,1,0:T(8,128)} %reshape.339), calls=%async_computation.4 | async-start | bytes 2097152 | tf_op jit(solution)/shard_map/all_to_all | solution.py:157
  578.6 23.3 %collective-permute-start.24 = (f32[4,64,256]{2,1,0:T(8,128)}, f32[4,64,256]{2,1,0:T(8,128)}, u32[]{:S(2)}, u32[]{:S(2)}) collective-permute-start(f32[4,64,256]{2,1,0:T(8,128)} %get-tuple-element.51), channel_id=1, source_target_pairs={{0,24},{8,0},{16,8},{24,16},{1,25},{9,1},{17,9},{25,17},{2,26},{10... | collective-permute-start | bytes 786440 | tf_op jit(solution)/shard_map/ppermute | solution.py:148
  581.0 22.4 %collective-permute-start.23 = (f32[4,64,256]{2,1,0:T(8,128)}, f32[4,64,256]{2,1,0:T(8,128)}, u32[]{:S(2)}, u32[]{:S(2)}) collective-permute-start(f32[4,64,256]{2,1,0:T(8,128)} %get-tuple-element.52), channel_id=1, source_target_pairs={{0,16},{8,24},{16,0},{24,8},{1,17},{9,25},{17,1},{25,9},{2,18},{10... | collective-permute-start | bytes 786440 | tf_op jit(solution)/shard_map/ppermute | solution.py:148
  581.5 23.5 %collective-permute-start.22 = (f32[4,64,256]{2,1,0:T(8,128)}, f32[4,64,256]{2,1,0:T(8,128)}, u32[]{:S(2)}, u32[]{:S(2)}) collective-permute-start(f32[4,64,256]{2,1,0:T(8,128)} %get-tuple-element.53), channel_id=1, source_target_pairs={{0,8},{8,16},{16,24},{24,0},{1,9},{9,17},{17,25},{25,1},{2,10},{10... | collective-permute-start | bytes 786440 | tf_op jit(solution)/shard_map/ppermute | solution.py:148
  584.2 25.4 %collective-permute-start.18 = (f32[4,64,256]{2,1,0:T(8,128)}, f32[4,64,256]{2,1,0:T(8,128)}, u32[]{:S(2)}, u32[]{:S(2)}) collective-permute-start(f32[4,64,256]{2,1,0:T(8,128)} %get-tuple-element.39), channel_id=1, source_target_pairs={{0,24},{8,0},{16,8},{24,16},{1,25},{9,1},{17,9},{25,17},{2,26},{10... | collective-permute-start | bytes 786440 | tf_op jit(solution)/shard_map/ppermute | solution.py:148
  586.5 23.7 %collective-permute-start.17 = (f32[4,64,256]{2,1,0:T(8,128)}, f32[4,64,256]{2,1,0:T(8,128)}, u32[]{:S(2)}, u32[]{:S(2)}) collective-permute-start(f32[4,64,256]{2,1,0:T(8,128)} %get-tuple-element.40), channel_id=1, source_target_pairs={{0,16},{8,24},{16,0},{24,8},{1,17},{9,25},{17,1},{25,9},{2,18},{10... | collective-permute-start | bytes 786440 | tf_op jit(solution)/shard_map/ppermute | solution.py:148
  610.2 18.8 %collective-permute-start.6 = (f32[4,64,256]{2,1,0:T(8,128)S(1)}, f32[4,64,256]{2,1,0:T(8,128)S(1)}, u32[]{:S(2)}, u32[]{:S(2)}) collective-permute-start(f32[4,64,256]{2,1,0:T(8,128)S(1)} %get-tuple-element.15), channel_id=1, source_target_pairs={{0,24},{8,0},{16,8},{24,16},{1,25},{9,1},{17,9},{25,17},{2,26},{10... | collective-permute-start | bytes 786440 | tf_op jit(solution)/shard_map/ppermute | solution.py:148
  619.2 24.8 %collective-permute-start.25 = (f32[4,64,256]{2,1,0:T(8,128)S(1)}, f32[4,64,256]{2,1,0:T(8,128)S(1)}, u32[]{:S(2)}, u32[]{:S(2)}) collective-permute-start(f32[4,64,256]{2,1,0:T(8,128)S(1)} %bitcast.327), channel_id=1, source_target_pairs={{0,24},{8,0},{16,8},{24,16},{1,25},{9,1},{17,9},{25,17},{2,26},{10... | collective-permute-start | bytes 786440 | tf_op jit(solution)/shard_map/ppermute | solution.py:148
  623.3 21.2 %collective-permute-start.26 = (f32[4,64,256]{2,1,0:T(8,128)S(1)}, f32[4,64,256]{2,1,0:T(8,128)S(1)}, u32[]{:S(2)}, u32[]{:S(2)}) collective-permute-start(f32[4,64,256]{2,1,0:T(8,128)S(1)} %bitcast.326), channel_id=1, source_target_pairs={{0,16},{8,24},{16,0},{24,8},{1,17},{9,25},{17,1},{25,9},{2,18},{10... | collective-permute-start | bytes 786440 | tf_op jit(solution)/shard_map/ppermute | solution.py:148
  630.5 21.1 %collective-permute-start.19 = (f32[4,64,256]{2,1,0:T(8,128)}, f32[4,64,256]{2,1,0:T(8,128)S(1)}, u32[]{:S(2)}, u32[]{:S(2)}) collective-permute-start(f32[4,64,256]{2,1,0:T(8,128)} %bitcast.266), channel_id=1, source_target_pairs={{0,24},{8,0},{16,8},{24,16},{1,25},{9,1},{17,9},{25,17},{2,26},{10... | collective-permute-start | bytes 786440 | tf_op jit(solution)/shard_map/ppermute | solution.py:148
  634.6 18.4 %collective-permute-start.20 = (f32[4,64,256]{2,1,0:T(8,128)}, f32[4,64,256]{2,1,0:T(8,128)S(1)}, u32[]{:S(2)}, u32[]{:S(2)}) collective-permute-start(f32[4,64,256]{2,1,0:T(8,128)} %bitcast.265), channel_id=1, source_target_pairs={{0,16},{8,24},{16,0},{24,8},{1,17},{9,25},{17,1},{25,9},{2,18},{10... | collective-permute-start | bytes 786440 | tf_op jit(solution)/shard_map/ppermute | solution.py:148
  644.5 18.3 %collective-permute-start.13 = (f32[4,64,256]{2,1,0:T(8,128)}, f32[4,64,256]{2,1,0:T(8,128)S(1)}, u32[]{:S(2)}, u32[]{:S(2)}) collective-permute-start(f32[4,64,256]{2,1,0:T(8,128)} %bitcast.269), channel_id=1, source_target_pairs={{0,24},{8,0},{16,8},{24,16},{1,25},{9,1},{17,9},{25,17},{2,26},{10... | collective-permute-start | bytes 786440 | tf_op jit(solution)/shard_map/ppermute | solution.py:148
  653.1 21.2 %collective-permute-start.7 = (f32[4,64,256]{2,1,0:T(8,128)}, f32[4,64,256]{2,1,0:T(8,128)}, u32[]{:S(2)}, u32[]{:S(2)}) collective-permute-start(f32[4,64,256]{2,1,0:T(8,128)} %bitcast.325), channel_id=1, source_target_pairs={{0,24},{8,0},{16,8},{24,16},{1,25},{9,1},{17,9},{25,17},{2,26},{10... | collective-permute-start | bytes 786440 | tf_op jit(solution)/shard_map/ppermute | solution.py:148
  (43 other events, 623.1 us)

commit v6 on v5

--- a/solution.py
+++ b/solution.py
@@ -151,20 +151,7 @@
     vs = vc // vchunks
     width = vs * cb
     results = []
-    for i in range(vchunks):
-        part = current[:, :, i * vs:(i + 1) * vs, :]
-        chans = jnp.transpose(part.reshape(kl, rl, vs, n, cb), (3, 0, 1, 2, 4))
-        got = lax.all_to_all(chans.reshape(n, kl, rl, width), "rad", 0, 0, tiled=True)
-        radial_block = jnp.transpose(got.reshape(n, kl, rl, width), (1, 0, 2, 3)).reshape(
-            kl, radial, width
-        )
-        placed = jnp.einsum(
-            "kqr,krm->kqm",
-            interp_turned,
-            radial_block,
-            precision=PRECISE,
-            preferred_element_type=jnp.float32,
-        )
+    def finish(placed):
         arrived = [hel_shift(placed[:, d * qb:(d + 1) * qb], d) for d in range(nh)]
         gathered = jnp.stack(arrived, axis=0)
         turned = jnp.dot(
@@ -183,6 +170,27 @@
             blocks.append(pick)
         rotated = jnp.concatenate(blocks, axis=1)
         results.append(rotated.reshape(kl, qq, vs, cb))
+
+    pending = None
+    for i in range(vchunks):
+        part = current[:, :, i * vs:(i + 1) * vs, :]
+        if pending is not None:
+            pending, part = lax.optimization_barrier((pending, part))
+            finish(pending)
+        chans = jnp.transpose(part.reshape(kl, rl, vs, n, cb), (3, 0, 1, 2, 4))
+        got = lax.all_to_all(chans.reshape(n, kl, rl, width), "rad", 0, 0, tiled=True)
+        radial_block = jnp.transpose(got.reshape(n, kl, rl, width), (1, 0, 2, 3)).reshape(
+            kl, radial, width
+        )
+        placed = jnp.einsum(
+            "kqr,krm->kqm",
+            interp_turned,
+            radial_block,
+            precision=PRECISE,
+            preferred_element_type=jnp.float32,
+        )
+        pending = placed
+    finish(pending)
     product_amp = jnp.concatenate(results, axis=2)
     return (current, product_amp)
 

time: 691 us -> 689 us (level)
    all_to_all x4, waiting for transfers between devices: 68.4 us -> 28.7 us  [shards(): lax.all_to_all(chans.reshape(n, kl, rl, width), 'rad', 0, 0, tiled=True)]
    ppermute x24, waiting for transfers between devices: 24.9 us -> 58.7 us  [hel_shift(): return lax.ppermute(x, 'hel', [(i, (i + d) % nh) for i in range(nh)])]
  transfers between devices with their start and end apart: 36 -> 36, of which waited for: 18 -> 20; matrix products, arithmetic and copies ran while one was open for 28% -> 26% of each run, Pallas kernels for 0% -> 0%
where the time goes in v6:
time: 689 us; the launch traced here: 683 us
  waiting for transfers between devices  349 us (51%)
  local copies, waits for them, and re-layouts  153 us (22%)
  matrix products  83.2 us (12%)
  starting transfers between devices  77.7 us (11%)
  other arithmetic  18.4 us (3%)
    all_to_all x2, waiting for transfers between devices, to_radial_rows(): got = lax.all_to_all(blocks, 'rad', 0, 0, tiled=True).reshape(n, kl, rl, mb)  146 us
    all_to_all x2, waiting for transfers between devices, to_radial_columns(): got = lax.all_to_all(blocks, 'rad', 0, 0, tiled=True).reshape(n, kl, rl, mb)  116 us
    ppermute x24, waiting for transfers between devices, hel_shift(): return lax.ppermute(x, 'hel', [(i, (i + d) % nh) for i in range(nh)])  58.7 us
    ppermute x24, starting transfers between devices, hel_shift(): return lax.ppermute(x, 'hel', [(i, (i + d) % nh) for i in range(nh)])  28.9 us
    all_to_all x4, waiting for transfers between devices, shards(): lax.all_to_all(chans.reshape(n, kl, rl, width), 'rad', 0, 0, tiled=True)  28.7 us
    dot_general x2, matrix products, local_part(): jnp.dot(current.reshape(-1, cc), transform.T, precision=PRECISE, preferre...  25 us
    dot_general x2, matrix products, local_part(): jnp.dot(angles.reshape(-1, angles.shape[3]), transform, precision=PRECISE...  23 us
    reshape x3, local copies, waits for them, and re-layouts, to_radial_columns(): blocks = jnp.transpose(x.reshape(kl, rl, n, mb), (2, 0, 1, 3))  17.1 us
  transfers between devices with their start and end apart: 36, of which 20 were waited for; matrix products, arithmetic and copies ran while one was open for 26% of the time, Pallas kernels for 0%

profile of v6, /device:TPU:0, one launch (start us, length us, event | category | flops | bytes accessed | tf_op | source)
XLA Modules:
  0.0 683.2 jit_solution(8660727570417306996)
XLA Ops:
  5.9 6.6 copy.100
  12.6 6.5 all-to-all-start
  35.7 16.4 %convolution_bitcast_fusion = f32[2048,512]{0,1:T(8,128)} fusion(f32[512,512]{1,0:T(8,128)S(1)} %convolution_multiply_fusion, f32[2048,512]{1,0:T(8,128)} %bitcast.273), kind=kOutput, calls=%fused_computation.27 | convolution fusion | flops 6442450944 | bytes 9437184 | tf_op jit(solution)/shard_map/dot_general | solution.py:91
  52.1 5.4 copy.102
  57.5 5.7 fusion.37
  63.2 11.6 %fusion.5 = f32[4,32,16,512]{3,2,1,0:T(8,128)} fusion(f32[1,32,16,512]{3,2,1,0:T(8,128)S(1)} %collective-permute-done, f32[3,32,16,512]{3,2,1,0:T(8,128)} %slice.154, f32[3,32,16,512]{3,2,1,0:T(8,128)S(1)} %slice-done.1, f32[1,32,16,512]{3,2,1,0:T(8,128)S(1)} %collective-permute-done.1, f32[4,32,16,512]{3,2,1,0:T(8,128)} %param.15, ...), kind=kOutput, calls=%fused_computation.9 | convolution fusion | flops 6456082432 | bytes 26288448 | tf_op jit(solution)/shard_map/dot_general | solution.py:103
  80.0 6.6 copy.183
  86.7 26.5 %all-to-all-done = f32[8,4,32,1024]{3,2,1,0:T(8,128)} async-done(((f32[8,4,32,1024]{3,2,1,0:T(8,128)}), f32[8,4,32,1024]{3,2,1,0:T(8,128)}, u32[]{:S(2)}, u32[]{:S(2)}) %all-to-all-start) | async-done | bytes 4194336 | tf_op jit(solution)/shard_map/all_to_all | solution.py:73
  123.1 89.2 %all-to-all-done.1 = f32[8,4,32,1024]{3,2,1,0:T(8,128)} async-done(((f32[8,4,32,1024]{3,2,1,0:T(8,128)}), f32[8,4,32,1024]{3,2,1,0:T(8,128)}, u32[]{:S(2)}, u32[]{:S(2)}) %all-to-all-start.1) | async-done | bytes 4194336 | tf_op jit(solution)/shard_map/all_to_all | solution.py:73
  227.6 5.6 fusion.39
  235.8 85.7 %all-to-all-done.3 = f32[8,4,32,1024]{3,2,1,0:T(8,128)} async-done(((f32[8,4,32,1024]{3,2,1,0:T(8,128)}), f32[8,4,32,1024]{3,2,1,0:T(8,128)}, u32[]{:S(2)}, u32[]{:S(2)}) %all-to-all-start.3) | async-done | bytes 4194336 | tf_op jit(solution)/shard_map/all_to_all | solution.py:78
  327.4 6.6 copy.108
  359.7 60.4 %all-to-all-done.2 = f32[8,4,32,1024]{3,2,1,0:T(8,128)} async-done(((f32[8,4,32,1024]{3,2,1,0:T(8,128)}), f32[8,4,32,1024]{3,2,1,0:T(8,128)}, u32[]{:S(2)}, u32[]{:S(2)}) %all-to-all-start.2) | async-done | bytes 4194336 | tf_op jit(solution)/shard_map/all_to_all | solution.py:78
  420.1 6.6 copy.106
  431.7 5.4 copy.110
  441.7 8.7 %fusion.25 = f32[128,16,512]{2,1,0:T(8,128)S(1)} fusion(f32[128,16,512]{2,1,0:T(8,128)} %dot_general.74, f32[512,512]{1,0:T(8,128)S(1)} %convolution_multiply_fusion), kind=kOutput, calls=%fused_computation.47 | convolution fusion | flops 6442450944 | bytes 9437184 | tf_op jit(solution)/shard_map/dot_general | solution.py:91
  455.6 11.5 %fusion.12 = f32[4,32,16,512]{3,2,1,0:T(8,128)S(1)} fusion(f32[4,32,16,512]{3,2,1,0:T(8,128)} %reshape.334, f32[1,32,16,512]{3,2,1,0:T(8,128)S(1)} %collective-permute-done.2, f32[3,32,16,512]{3,2,1,0:T(8,128)} %slice.159, f32[3,32,16,512]{3,2,1,0:T(8,128)S(1)} %slice-done, f32[1,32,16,512]{3,2,1,0:T(8,128)S(1)} %collective-permute-done.3, ...), kind=kOutput, calls=%fused_computation.17 | convolution fusion | flops 6457131008 | bytes 30482752 | tf_op jit(solution)/shard_map/dot_general | solution.py:103
  480.9 25.0 %all-to-all-done.4 = f32[8,4,32,256]{3,2,1,0:T(8,128)S(1)} async-done(((f32[8,4,32,256]{3,2,1,0:T(8,128)}), f32[8,4,32,256]{3,2,1,0:T(8,128)S(1)}, u32[]{:S(2)}, u32[]{:S(2)}) %all-to-all-start.4) | async-done | bytes 1048608 | tf_op jit(solution)/shard_map/all_to_all | solution.py:181
  525.0 5.4 collective-permute-done.6
  530.3 6.5 collective-permute-done.5
  572.2 6.3 collective-permute-done.8
  581.3 7.7 %collective-permute-done.11 = f32[4,64,256]{2,1,0:T(8,128)S(1)} collective-permute-done((f32[4,64,256]{2,1,0:T(8,128)S(1)}, f32[4,64,256]{2,1,0:T(8,128)S(1)}, u32[]{:S(2)}, u32[]{:S(2)}) %collective-permute-start.11) | collective-permute-done | bytes 262176 | tf_op jit(solution)/shard_map/ppermute | solution.py:148
  629.4 6.2 collective-permute-done.17
  649.6 5.3 collective-permute-done.23
  (252 shorter events, 254.3 us)
Async XLA Ops:
  12.6 100.6 %all-to-all-start = ((f32[8,4,32,1024]{3,2,1,0:T(8,128)}), f32[8,4,32,1024]{3,2,1,0:T(8,128)}, u32[]{:S(2)}, u32[]{:S(2)}) async-start(f32[8,4,32,1024]{3,2,1,0:T(8,128)} %copy.100), calls=%async_computation | async-start | bytes 8388608 | tf_op jit(solution)/shard_map/all_to_all | solution.py:73
  21.3 41.8 %collective-permute-start = (f32[1,32,16,512]{3,2,1,0:T(8,128)}, f32[1,32,16,512]{3,2,1,0:T(8,128)S(1)}, u32[]{:S(2)}, u32[]{:S(2)}) collective-permute-start(f32[1,32,16,512]{3,2,1,0:T(8,128)} %slice.155), channel_id=1, source_target_pairs={{8,0},{16,8},{24,16},{9,1},{17,9},{25,17},{10,2},{18,10},{26,18},{... | collective-permute-start | bytes 3145736 | tf_op jit(solution)/shard_map/ppermute | solution.py:13
  26.8 36.4 %collective-permute-start.1 = (f32[1,32,16,512]{3,2,1,0:T(8,128)}, f32[1,32,16,512]{3,2,1,0:T(8,128)S(1)}, u32[]{:S(2)}, u32[]{:S(2)}) collective-permute-start(f32[1,32,16,512]{3,2,1,0:T(8,128)} %slice.206), channel_id=1, source_target_pairs={{0,8},{8,16},{16,24},{1,9},{9,17},{17,25},{2,10},{10,18},{18,26},{... | collective-permute-start | bytes 3145736 | tf_op jit(solution)/shard_map/ppermute | solution.py:13
  113.1 99.2 %all-to-all-start.1 = ((f32[8,4,32,1024]{3,2,1,0:T(8,128)}), f32[8,4,32,1024]{3,2,1,0:T(8,128)}, u32[]{:S(2)}, u32[]{:S(2)}) async-start(f32[8,4,32,1024]{3,2,1,0:T(8,128)} %bitcast.278), calls=%async_computation.1 | async-start | bytes 8388608 | tf_op jit(solution)/shard_map/all_to_all | solution.py:73
  223.0 98.6 %all-to-all-start.3 = ((f32[8,4,32,1024]{3,2,1,0:T(8,128)}), f32[8,4,32,1024]{3,2,1,0:T(8,128)}, u32[]{:S(2)}, u32[]{:S(2)}) async-start(f32[8,4,32,1024]{3,2,1,0:T(8,128)} %bitcast.279), calls=%async_computation.3 | async-start | bytes 8388608 | tf_op jit(solution)/shard_map/all_to_all | solution.py:78
  321.6 98.5 %all-to-all-start.2 = ((f32[8,4,32,1024]{3,2,1,0:T(8,128)}), f32[8,4,32,1024]{3,2,1,0:T(8,128)}, u32[]{:S(2)}, u32[]{:S(2)}) async-start(f32[8,4,32,1024]{3,2,1,0:T(8,128)} %bitcast.277), calls=%async_computation.2 | async-start | bytes 8388608 | tf_op jit(solution)/shard_map/all_to_all | solution.py:78
  335.9 119.7 %collective-permute-start.2 = (f32[1,32,16,512]{3,2,1,0:T(8,128)}, f32[1,32,16,512]{3,2,1,0:T(8,128)S(1)}, u32[]{:S(2)}, u32[]{:S(2)}) collective-permute-start(f32[1,32,16,512]{3,2,1,0:T(8,128)} %slice.161), channel_id=1, source_target_pairs={{8,0},{16,8},{24,16},{9,1},{17,9},{25,17},{10,2},{18,10},{26,18},{... | collective-permute-start | bytes 3145736 | tf_op jit(solution)/shard_map/ppermute | solution.py:13
  346.2 109.4 %collective-permute-start.3 = (f32[1,32,16,512]{3,2,1,0:T(8,128)}, f32[1,32,16,512]{3,2,1,0:T(8,128)S(1)}, u32[]{:S(2)}, u32[]{:S(2)}) collective-permute-start(f32[1,32,16,512]{3,2,1,0:T(8,128)} %slice.210), channel_id=1, source_target_pairs={{0,8},{8,16},{16,24},{1,9},{9,17},{17,25},{2,10},{10,18},{18,26},{... | collective-permute-start | bytes 3145736 | tf_op jit(solution)/shard_map/ppermute | solution.py:13
  475.9 30.1 %all-to-all-start.4 = ((f32[8,4,32,256]{3,2,1,0:T(8,128)}), f32[8,4,32,256]{3,2,1,0:T(8,128)S(1)}, u32[]{:S(2)}, u32[]{:S(2)}) async-start(f32[8,4,32,256]{3,2,1,0:T(8,128)} %reshape.339), calls=%async_computation.4 | async-start | bytes 2097152 | tf_op jit(solution)/shard_map/all_to_all | solution.py:181
  515.1 30.1 %all-to-all-start.5 = ((f32[8,4,32,256]{3,2,1,0:T(8,128)}), f32[8,4,32,256]{3,2,1,0:T(8,128)S(1)}, u32[]{:S(2)}, u32[]{:S(2)}) async-start(f32[8,4,32,256]{3,2,1,0:T(8,128)} %reshape.344), calls=%async_computation.5 | async-start | bytes 2097152 | tf_op jit(solution)/shard_map/all_to_all | solution.py:181
  554.3 37.5 %all-to-all-start.6 = ((f32[8,4,32,256]{3,2,1,0:T(8,128)}), f32[8,4,32,256]{3,2,1,0:T(8,128)S(1)}, u32[]{:S(2)}, u32[]{:S(2)}) async-start(f32[8,4,32,256]{3,2,1,0:T(8,128)} %reshape.349), calls=%async_computation.6 | async-start | bytes 2097152 | tf_op jit(solution)/shard_map/all_to_all | solution.py:181
  563.5 15.0 %collective-permute-start.8 = (f32[4,64,256]{2,1,0:T(8,128)}, f32[4,64,256]{2,1,0:T(8,128)S(1)}, u32[]{:S(2)}, u32[]{:S(2)}) collective-permute-start(f32[4,64,256]{2,1,0:T(8,128)} %bitcast.271), channel_id=1, source_target_pairs={{0,16},{8,24},{16,0},{24,8},{1,17},{9,25},{17,1},{25,9},{2,18},{10... | collective-permute-start | bytes 786440 | tf_op jit(solution)/shard_map/ppermute | solution.py:148
  565.5 15.8 %collective-permute-start.12 = (f32[4,64,256]{2,1,0:T(8,128)S(1)}, f32[4,64,256]{2,1,0:T(8,128)S(1)}, u32[]{:S(2)}, u32[]{:S(2)}) collective-permute-start(f32[4,64,256]{2,1,0:T(8,128)S(1)} %get-tuple-element.39), channel_id=1, source_target_pairs={{0,24},{8,0},{16,8},{24,16},{1,25},{9,1},{17,9},{25,17},{2,26},{10... | collective-permute-start | bytes 786440 | tf_op jit(solution)/shard_map/ppermute | solution.py:148
  567.9 21.1 %collective-permute-start.11 = (f32[4,64,256]{2,1,0:T(8,128)S(1)}, f32[4,64,256]{2,1,0:T(8,128)S(1)}, u32[]{:S(2)}, u32[]{:S(2)}) collective-permute-start(f32[4,64,256]{2,1,0:T(8,128)S(1)} %get-tuple-element.40), channel_id=1, source_target_pairs={{0,16},{8,24},{16,0},{24,8},{1,17},{9,25},{17,1},{25,9},{2,18},{10... | collective-permute-start | bytes 786440 | tf_op jit(solution)/shard_map/ppermute | solution.py:148
  569.8 19.2 %collective-permute-start.10 = (f32[4,64,256]{2,1,0:T(8,128)S(1)}, f32[4,64,256]{2,1,0:T(8,128)S(1)}, u32[]{:S(2)}, u32[]{:S(2)}) collective-permute-start(f32[4,64,256]{2,1,0:T(8,128)S(1)} %get-tuple-element.41), channel_id=1, source_target_pairs={{0,8},{8,16},{16,24},{24,0},{1,9},{9,17},{17,25},{25,1},{2,10},{10... | collective-permute-start | bytes 786440 | tf_op jit(solution)/shard_map/ppermute | solution.py:148
  600.8 37.6 %all-to-all-start.7 = ((f32[8,4,32,256]{3,2,1,0:T(8,128)}), f32[8,4,32,256]{3,2,1,0:T(8,128)S(1)}, u32[]{:S(2)}, u32[]{:S(2)}) async-start(f32[8,4,32,256]{3,2,1,0:T(8,128)} %reshape.354), calls=%async_computation.7 | async-start | bytes 2097152 | tf_op jit(solution)/shard_map/all_to_all | solution.py:181
  610.0 15.1 %collective-permute-start.14 = (f32[4,64,256]{2,1,0:T(8,128)}, f32[4,64,256]{2,1,0:T(8,128)}, u32[]{:S(2)}, u32[]{:S(2)}) collective-permute-start(f32[4,64,256]{2,1,0:T(8,128)} %bitcast.268), channel_id=1, source_target_pairs={{0,16},{8,24},{16,0},{24,8},{1,17},{9,25},{17,1},{25,9},{2,18},{10... | collective-permute-start | bytes 786440 | tf_op jit(solution)/shard_map/ppermute | solution.py:148
  618.9 16.7 %collective-permute-start.17 = (f32[4,64,256]{2,1,0:T(8,128)}, f32[4,64,256]{2,1,0:T(8,128)}, u32[]{:S(2)}, u32[]{:S(2)}) collective-permute-start(f32[4,64,256]{2,1,0:T(8,128)} %get-tuple-element.52), channel_id=1, source_target_pairs={{0,16},{8,24},{16,0},{24,8},{1,17},{9,25},{17,1},{25,9},{2,18},{10... | collective-permute-start | bytes 786440 | tf_op jit(solution)/shard_map/ppermute | solution.py:148
  620.2 15.4 %collective-permute-start.16 = (f32[4,64,256]{2,1,0:T(8,128)S(1)}, f32[4,64,256]{2,1,0:T(8,128)}, u32[]{:S(2)}, u32[]{:S(2)}) collective-permute-start(f32[4,64,256]{2,1,0:T(8,128)S(1)} %get-tuple-element.53), channel_id=1, source_target_pairs={{0,8},{8,16},{16,24},{24,0},{1,9},{9,17},{17,25},{25,1},{2,10},{10... | collective-permute-start | bytes 786440 | tf_op jit(solution)/shard_map/ppermute | solution.py:148
  642.6 18.8 %collective-permute-start.19 = (f32[4,64,256]{2,1,0:T(8,128)S(1)}, f32[4,64,256]{2,1,0:T(8,128)S(1)}, u32[]{:S(2)}, u32[]{:S(2)}) collective-permute-start(f32[4,64,256]{2,1,0:T(8,128)S(1)} %bitcast.325), channel_id=1, source_target_pairs={{0,24},{8,0},{16,8},{24,16},{1,25},{9,1},{17,9},{25,17},{2,26},{10... | collective-permute-start | bytes 786440 | tf_op jit(solution)/shard_map/ppermute | solution.py:148
  644.0 20.4 %collective-permute-start.20 = (f32[4,64,256]{2,1,0:T(8,128)S(1)}, f32[4,64,256]{2,1,0:T(8,128)S(1)}, u32[]{:S(2)}, u32[]{:S(2)}) collective-permute-start(f32[4,64,256]{2,1,0:T(8,128)S(1)} %bitcast.324), channel_id=1, source_target_pairs={{0,16},{8,24},{16,0},{24,8},{1,17},{9,25},{17,1},{25,9},{2,18},{10... | collective-permute-start | bytes 786440 | tf_op jit(solution)/shard_map/ppermute | solution.py:148
  648.9 17.0 %collective-permute-start.21 = (f32[4,64,256]{2,1,0:T(8,128)S(1)}, f32[4,64,256]{2,1,0:T(8,128)S(1)}, u32[]{:S(2)}, u32[]{:S(2)}) collective-permute-start(f32[4,64,256]{2,1,0:T(8,128)S(1)} %bitcast.326), channel_id=1, source_target_pairs={{0,8},{8,16},{16,24},{24,0},{1,9},{9,17},{17,25},{25,1},{2,10},{10... | collective-permute-start | bytes 786440 | tf_op jit(solution)/shard_map/ppermute | solution.py:148
  660.0 16.3 %collective-permute-start.26 = (f32[4,64,256]{2,1,0:T(8,128)}, f32[4,64,256]{2,1,0:T(8,128)}, u32[]{:S(2)}, u32[]{:S(2)}) collective-permute-start(f32[4,64,256]{2,1,0:T(8,128)} %bitcast.262), channel_id=1, source_target_pairs={{0,16},{8,24},{16,0},{24,8},{1,17},{9,25},{17,1},{25,9},{2,18},{10... | collective-permute-start | bytes 786440 | tf_op jit(solution)/shard_map/ppermute | solution.py:148
  661.4 14.9 %collective-permute-start.27 = (f32[4,64,256]{2,1,0:T(8,128)}, f32[4,64,256]{2,1,0:T(8,128)}, u32[]{:S(2)}, u32[]{:S(2)}) collective-permute-start(f32[4,64,256]{2,1,0:T(8,128)} %bitcast.261), channel_id=1, source_target_pairs={{0,8},{8,16},{16,24},{24,0},{1,9},{9,17},{17,25},{25,1},{2,10},{10... | collective-permute-start | bytes 786440 | tf_op jit(solution)/shard_map/ppermute | solution.py:148
  (51 other events, 611.8 us)

commit v7 on v6

--- a/solution.py
+++ b/solution.py
@@ -128,8 +128,17 @@
         current = to_radial_rows(following_columns)
         columns = following_columns
     kinetic_image = to_radial_rows(kinetic(columns))
-    image = kinetic_image + local_part(current)
-    current = damp_full * (2.0 * image - damp_full * earlier)
+    local_image = local_part(current)
+    if vc % 8 == 0:
+        sizes = [vc // 4] * 3 + [vc // 8] * 2
+    else:
+        sizes = [vc]
+    bounds = [sum(sizes[:i]) for i in range(len(sizes) + 1)]
+    final_parts = []
+    for lo, hi in zip(bounds[:-1], bounds[1:]):
+        image = kinetic_image[:, :, lo:hi] + local_image[:, :, lo:hi]
+        final_parts.append(damp_full * (2.0 * image - damp_full * earlier[:, :, lo:hi]))
+    current = jnp.concatenate(final_parts, axis=2)
 
     hel_index = lax.axis_index("hel")
     interp = interp_matrix(stencil, interp_weights, radial)
@@ -147,11 +156,11 @@
             return x
         return lax.ppermute(x, "hel", [(i, (i + d) % nh) for i in range(nh)])
 
-    vchunks = 4 if vc % 4 == 0 else 1
-    vs = vc // vchunks
-    width = vs * cb
     results = []
+
     def finish(placed):
+        vs = placed.shape[2] // cb
+        width = vs * cb
         arrived = [hel_shift(placed[:, d * qb:(d + 1) * qb], d) for d in range(nh)]
         gathered = jnp.stack(arrived, axis=0)
         turned = jnp.dot(
@@ -172,8 +181,9 @@
         results.append(rotated.reshape(kl, qq, vs, cb))
 
     pending = None
-    for i in range(vchunks):
-        part = current[:, :, i * vs:(i + 1) * vs, :]
+    for part in final_parts:
+        vs = part.shape[2]
+        width = vs * cb
         if pending is not None:
             pending, part = lax.optimization_barrier((pending, part))
             finish(pending)

time: 689 us -> 695 us (level)
  waiting for transfers between devices: 349 us -> 320 us
  local copies, waits for them, and re-layouts: 153 us -> 172 us
  starting transfers between devices: 77.7 us -> 90.8 us
  other arithmetic: 18.4 us -> 26.1 us
    ppermute x24 -> x30, waiting for transfers between devices: 58.7 us -> 27 us  [hel_shift(): return lax.ppermute(x, 'hel', [(i, (i + d) % nh) for i in range(nh)])]
    all_to_all x4 -> x5, waiting for transfers between devices: 28.7 us -> 42.8 us  [shards(): lax.all_to_all(chans.reshape(n, kl, rl, width), 'rad', 0, 0, tiled=True)]
    concatenate x0 -> x2, local copies, waits for them, and re-layouts: none -> 12 us  [the longest x1 11.2 us: shards(): current = jnp.concatenate(final_parts, axis=2)]
    all_to_all x2, waiting for transfers between devices: 146 us -> 134 us  [to_radial_rows(): got = lax.all_to_all(blocks, 'rad', 0, 0, tiled=True).reshape(n, kl, rl, mb)]
    mul x0 -> x2, other arithmetic: none -> 10.5 us  [shards(): damp_full * (2.0 * image - damp_full * earlier[:, :, lo:hi])]
    ppermute x24 -> x30, starting transfers between devices: 28.9 us -> 35.6 us  [hel_shift(): return lax.ppermute(x, 'hel', [(i, (i + d) % nh) for i in range(nh)])]
    reshape x8 -> x10, local copies, waits for them, and re-layouts: 13.6 us -> 20.2 us  [shards(): chans = jnp.transpose(part.reshape(kl, rl, vs, n, cb), (3, 0, 1, 2, 4))]
    all_to_all x4 -> x5, starting transfers between devices: 15.8 us -> 22.4 us  [shards(): lax.all_to_all(chans.reshape(n, kl, rl, width), 'rad', 0, 0, tiled=True)]
  transfers between devices with their start and end apart: 36 -> 43, of which waited for: 20 -> 17; matrix products, arithmetic and copies ran while one was open for 26% -> 31% of each run, Pallas kernels for 0% -> 0%
where the time goes in v7:
time: 695 us; the launch traced here: 689 us
  waiting for transfers between devices  320 us (46%)
  local copies, waits for them, and re-layouts  172 us (25%)
  starting transfers between devices  90.8 us (13%)
  matrix products  78.1 us (11%)
  other arithmetic  26.1 us (4%)
    all_to_all x2, waiting for transfers between devices, to_radial_rows(): got = lax.all_to_all(blocks, 'rad', 0, 0, tiled=True).reshape(n, kl, rl, mb)  134 us
    all_to_all x2, waiting for transfers between devices, to_radial_columns(): got = lax.all_to_all(blocks, 'rad', 0, 0, tiled=True).reshape(n, kl, rl, mb)  116 us
    all_to_all x5, waiting for transfers between devices, shards(): lax.all_to_all(chans.reshape(n, kl, rl, width), 'rad', 0, 0, tiled=True)  42.8 us
    ppermute x30, starting transfers between devices, hel_shift(): return lax.ppermute(x, 'hel', [(i, (i + d) % nh) for i in range(nh)])  35.6 us
    ppermute x30, waiting for transfers between devices, hel_shift(): return lax.ppermute(x, 'hel', [(i, (i + d) % nh) for i in range(nh)])  27 us
    dot_general x2, matrix products, local_part(): jnp.dot(current.reshape(-1, cc), transform.T, precision=PRECISE, preferre...  25.1 us
    all_to_all x5, starting transfers between devices, shards(): lax.all_to_all(chans.reshape(n, kl, rl, width), 'rad', 0, 0, tiled=True)  22.4 us
    dot_general x2, matrix products, local_part(): jnp.dot(angles.reshape(-1, angles.shape[3]), transform, precision=PRECISE...  21.7 us
  transfers between devices with their start and end apart: 43, of which 17 were waited for; matrix products, arithmetic and copies ran while one was open for 31% of the time, Pallas kernels for 0%

profile of v7, /device:TPU:0, one launch (start us, length us, event | category | flops | bytes accessed | tf_op | source)
XLA Modules:
  0.0 688.9 jit_solution(2506086435348791192)
XLA Ops:
  0.6 5.3 reshape.350
  5.9 6.6 copy.110
  12.5 6.5 all-to-all-start
  35.7 16.4 %convolution_bitcast_fusion = f32[2048,512]{0,1:T(8,128)} fusion(f32[512,512]{1,0:T(8,128)S(1)} %convolution_multiply_fusion, f32[2048,512]{1,0:T(8,128)} %bitcast.334), kind=kOutput, calls=%fused_computation.22 | convolution fusion | flops 6442450944 | bytes 9437184 | tf_op jit(solution)/shard_map/dot_general | solution.py:91
  52.0 5.4 copy.112
  57.4 5.7 fusion.56
  63.2 11.5 %fusion.5 = f32[4,32,16,512]{3,2,1,0:T(8,128)} fusion(f32[1,32,16,512]{3,2,1,0:T(8,128)S(1)} %collective-permute-done, f32[3,32,16,512]{3,2,1,0:T(8,128)} %slice.215, f32[3,32,16,512]{3,2,1,0:T(8,128)S(1)} %slice-done.1, f32[1,32,16,512]{3,2,1,0:T(8,128)S(1)} %collective-permute-done.1, f32[4,32,16,512]{3,2,1,0:T(8,128)} %param.15, ...), kind=kOutput, calls=%fused_computation.9 | convolution fusion | flops 6456082432 | bytes 26288448 | tf_op jit(solution)/shard_map/dot_general | solution.py:103
  74.7 5.2 reshape.355
  79.9 6.6 copy.217
  86.6 26.6 %all-to-all-done = f32[8,4,32,1024]{3,2,1,0:T(8,128)} async-done(((f32[8,4,32,1024]{3,2,1,0:T(8,128)}), f32[8,4,32,1024]{3,2,1,0:T(8,128)}, u32[]{:S(2)}, u32[]{:S(2)}) %all-to-all-start) | async-done | bytes 4194336 | tf_op jit(solution)/shard_map/all_to_all | solution.py:73
  123.0 89.2 %all-to-all-done.1 = f32[8,4,32,1024]{3,2,1,0:T(8,128)} async-done(((f32[8,4,32,1024]{3,2,1,0:T(8,128)}), f32[8,4,32,1024]{3,2,1,0:T(8,128)}, u32[]{:S(2)}, u32[]{:S(2)}) %all-to-all-start.1) | async-done | bytes 4194336 | tf_op jit(solution)/shard_map/all_to_all | solution.py:73
  227.5 5.6 fusion.58
  235.8 85.7 %all-to-all-done.3 = f32[8,4,32,1024]{3,2,1,0:T(8,128)} async-done(((f32[8,4,32,1024]{3,2,1,0:T(8,128)}), f32[8,4,32,1024]{3,2,1,0:T(8,128)}, u32[]{:S(2)}, u32[]{:S(2)}) %all-to-all-start.3) | async-done | bytes 4194336 | tf_op jit(solution)/shard_map/all_to_all | solution.py:78
  327.4 6.6 copy.118
  361.5 5.4 copy.120
  371.5 48.6 %all-to-all-done.2 = f32[8,4,32,1024]{3,2,1,0:T(8,128)} async-done(((f32[8,4,32,1024]{3,2,1,0:T(8,128)}), f32[8,4,32,1024]{3,2,1,0:T(8,128)}, u32[]{:S(2)}, u32[]{:S(2)}) %all-to-all-start.2) | async-done | bytes 4194336 | tf_op jit(solution)/shard_map/all_to_all | solution.py:78
  420.1 6.6 copy.116
  431.6 8.7 %fusion.30 = f32[128,16,512]{2,1,0:T(8,128)S(1)} fusion(f32[128,16,512]{2,1,0:T(8,128)} %dot_general.80, f32[512,512]{1,0:T(8,128)S(1)} %convolution_multiply_fusion), kind=kOutput, calls=%fused_computation.51 | convolution fusion | flops 6442450944 | bytes 9437184 | tf_op jit(solution)/shard_map/dot_general | solution.py:91
  444.5 10.2 %fusion.8 = f32[4,32,16,512]{3,2,1,0:T(8,128)S(1)} fusion(f32[1,32,16,512]{3,2,1,0:T(8,128)S(1)} %collective-permute-done.2, f32[3,32,16,512]{3,2,1,0:T(8,128)} %slice.221, f32[3,32,16,512]{3,2,1,0:T(8,128)S(1)} %slice-done, f32[1,32,16,512]{3,2,1,0:T(8,128)S(1)} %collective-permute-done.3, f32[4,32,16,512]{3,2,1,0:T(8,128)S(1)} %copy-done.5, ...), kind=kOutput, calls=%fused_computation.13 | convolution fusion | flops 6451888128 | bytes 22094016 | tf_op jit(solution)/shard_map/dot_general | solution.py:103
  474.2 24.0 %all-to-all-done.4 = f32[8,4,32,256]{3,2,1,0:T(8,128)} async-done(((f32[8,4,32,256]{3,2,1,0:T(8,128)}), f32[8,4,32,256]{3,2,1,0:T(8,128)}, u32[]{:S(2)}, u32[]{:S(2)}) %all-to-all-start.4) | async-done | bytes 1048608 | tf_op jit(solution)/shard_map/all_to_all | solution.py:191
  527.8 7.4 %fusion.40 = (f32[4,32,2,512]{3,2,1,0:T(2,128)S(1)}, f32[4,32,2,512]{3,2,1,0:T(2,128)}) fusion(f32[4,32,16,512]{3,2,1,0:T(8,128)} %copy-done.7, f32[4,32,16,512]{3,2,1,0:T(8,128)} %reshape.358, f32[4,32,16,512]{3,2,1,0:T(8,128)} %param.16, f32[32]{0:T(128)S(1)} %dynamic_slice.6), kind=kLoop, calls=%fused_computation.66 | loop fusion | flops 1310720 | bytes 4194432 | tf_op jit(solution)/shard_map/mul | solution.py:140
  535.2 11.2 %concatenate.37 = f32[4,32,16,512]{3,2,1,0:T(8,128)} concatenate(f32[4,32,4,512]{3,2,1,0:T(4,128)} %get-tuple-element.22, f32[4,32,4,512]{3,2,1,0:T(4,128)S(1)} %get-tuple-element.11, f32[4,32,4,512]{3,2,1,0:T(4,128)S(1)} %get-tuple-element.13, f32[4,32,2,512]{3,2,1,0:T(2,128)} %get-tuple-element.15, f32[4,32,2,512]{3,2,1,0:T(2,128)S(1)} %get-tuple-element.17), dimensions={2} | concatenate | bytes 8388608 | tf_op jit(solution)/shard_map/concatenate | solution.py:141
  580.8 16.9 %all-to-all-done.6 = f32[8,4,32,256]{3,2,1,0:T(8,128)S(1)} async-done(((f32[8,4,32,256]{3,2,1,0:T(8,128)}), f32[8,4,32,256]{3,2,1,0:T(8,128)S(1)}, u32[]{:S(2)}, u32[]{:S(2)}) %all-to-all-start.6) | async-done | bytes 1048608 | tf_op jit(solution)/shard_map/all_to_all | solution.py:191
  630.5 8.0 %collective-permute-done.20 = f32[4,64,256]{2,1,0:T(8,128)} collective-permute-done((f32[4,64,256]{2,1,0:T(8,128)}, f32[4,64,256]{2,1,0:T(8,128)}, u32[]{:S(2)}, u32[]{:S(2)}) %collective-permute-start.20) | collective-permute-done | bytes 262176 | tf_op jit(solution)/shard_map/ppermute | solution.py:157
  (286 shorter events, 257.1 us)
Async XLA Ops:
  12.5 100.6 %all-to-all-start = ((f32[8,4,32,1024]{3,2,1,0:T(8,128)}), f32[8,4,32,1024]{3,2,1,0:T(8,128)}, u32[]{:S(2)}, u32[]{:S(2)}) async-start(f32[8,4,32,1024]{3,2,1,0:T(8,128)} %copy.110), calls=%async_computation | async-start | bytes 8388608 | tf_op jit(solution)/shard_map/all_to_all | solution.py:73
  21.3 41.8 %collective-permute-start = (f32[1,32,16,512]{3,2,1,0:T(8,128)}, f32[1,32,16,512]{3,2,1,0:T(8,128)S(1)}, u32[]{:S(2)}, u32[]{:S(2)}) collective-permute-start(f32[1,32,16,512]{3,2,1,0:T(8,128)} %slice.216), channel_id=1, source_target_pairs={{8,0},{16,8},{24,16},{9,1},{17,9},{25,17},{10,2},{18,10},{26,18},{... | collective-permute-start | bytes 3145736 | tf_op jit(solution)/shard_map/ppermute | solution.py:13
  26.8 36.3 %collective-permute-start.1 = (f32[1,32,16,512]{3,2,1,0:T(8,128)}, f32[1,32,16,512]{3,2,1,0:T(8,128)S(1)}, u32[]{:S(2)}, u32[]{:S(2)}) collective-permute-start(f32[1,32,16,512]{3,2,1,0:T(8,128)} %slice.286), channel_id=1, source_target_pairs={{0,8},{8,16},{16,24},{1,9},{9,17},{17,25},{2,10},{10,18},{18,26},{... | collective-permute-start | bytes 3145736 | tf_op jit(solution)/shard_map/ppermute | solution.py:13
  113.1 99.1 %all-to-all-start.1 = ((f32[8,4,32,1024]{3,2,1,0:T(8,128)}), f32[8,4,32,1024]{3,2,1,0:T(8,128)}, u32[]{:S(2)}, u32[]{:S(2)}) async-start(f32[8,4,32,1024]{3,2,1,0:T(8,128)} %bitcast.340), calls=%async_computation.1 | async-start | bytes 8388608 | tf_op jit(solution)/shard_map/all_to_all | solution.py:73
  222.9 98.6 %all-to-all-start.3 = ((f32[8,4,32,1024]{3,2,1,0:T(8,128)}), f32[8,4,32,1024]{3,2,1,0:T(8,128)}, u32[]{:S(2)}, u32[]{:S(2)}) async-start(f32[8,4,32,1024]{3,2,1,0:T(8,128)} %bitcast.341), calls=%async_computation.3 | async-start | bytes 8388608 | tf_op jit(solution)/shard_map/all_to_all | solution.py:78
  321.5 98.6 %all-to-all-start.2 = ((f32[8,4,32,1024]{3,2,1,0:T(8,128)}), f32[8,4,32,1024]{3,2,1,0:T(8,128)}, u32[]{:S(2)}, u32[]{:S(2)}) async-start(f32[8,4,32,1024]{3,2,1,0:T(8,128)} %bitcast.339), calls=%async_computation.2 | async-start | bytes 8388608 | tf_op jit(solution)/shard_map/all_to_all | solution.py:78
  335.8 108.7 %collective-permute-start.2 = (f32[1,32,16,512]{3,2,1,0:T(8,128)}, f32[1,32,16,512]{3,2,1,0:T(8,128)S(1)}, u32[]{:S(2)}, u32[]{:S(2)}) collective-permute-start(f32[1,32,16,512]{3,2,1,0:T(8,128)} %slice.223), channel_id=1, source_target_pairs={{8,0},{16,8},{24,16},{9,1},{17,9},{25,17},{10,2},{18,10},{26,18},{... | collective-permute-start | bytes 3145736 | tf_op jit(solution)/shard_map/ppermute | solution.py:13
  348.0 96.5 %collective-permute-start.3 = (f32[1,32,16,512]{3,2,1,0:T(8,128)}, f32[1,32,16,512]{3,2,1,0:T(8,128)S(1)}, u32[]{:S(2)}, u32[]{:S(2)}) collective-permute-start(f32[1,32,16,512]{3,2,1,0:T(8,128)} %slice.291), channel_id=1, source_target_pairs={{0,8},{8,16},{16,24},{1,9},{9,17},{17,25},{2,10},{10,18},{18,26},{... | collective-permute-start | bytes 3145736 | tf_op jit(solution)/shard_map/ppermute | solution.py:13
  467.4 30.8 %all-to-all-start.4 = ((f32[8,4,32,256]{3,2,1,0:T(8,128)}), f32[8,4,32,256]{3,2,1,0:T(8,128)}, u32[]{:S(2)}, u32[]{:S(2)}) async-start(f32[8,4,32,256]{3,2,1,0:T(8,128)} %reshape.363), calls=%async_computation.4 | async-start | bytes 2097152 | tf_op jit(solution)/shard_map/all_to_all | solution.py:191
  501.5 17.0 %collective-permute-start.6 = (f32[4,64,256]{2,1,0:T(8,128)}, f32[4,64,256]{2,1,0:T(8,128)S(1)}, u32[]{:S(2)}, u32[]{:S(2)}) collective-permute-start(f32[4,64,256]{2,1,0:T(8,128)} %get-tuple-element.56), channel_id=1, source_target_pairs={{0,24},{8,0},{16,8},{24,16},{1,25},{9,1},{17,9},{25,17},{2,26},{10... | collective-permute-start | bytes 786440 | tf_op jit(solution)/shard_map/ppermute | solution.py:157
  514.2 34.9 %all-to-all-start.5 = ((f32[8,4,32,256]{3,2,1,0:T(8,128)}), f32[8,4,32,256]{3,2,1,0:T(8,128)}, u32[]{:S(2)}, u32[]{:S(2)}) async-start(f32[8,4,32,256]{3,2,1,0:T(8,128)} %reshape.368), calls=%async_computation.5 | async-start | bytes 2097152 | tf_op jit(solution)/shard_map/all_to_all | solution.py:191
  522.2 24.2 %collective-permute-start.7 = (f32[4,64,256]{2,1,0:T(8,128)}, f32[4,64,256]{2,1,0:T(8,128)S(1)}, u32[]{:S(2)}, u32[]{:S(2)}) collective-permute-start(f32[4,64,256]{2,1,0:T(8,128)} %bitcast.327), channel_id=1, source_target_pairs={{0,24},{8,0},{16,8},{24,16},{1,25},{9,1},{17,9},{25,17},{2,26},{10... | collective-permute-start | bytes 786440 | tf_op jit(solution)/shard_map/ppermute | solution.py:157
  525.3 21.1 %collective-permute-start.8 = (f32[4,64,256]{2,1,0:T(8,128)}, f32[4,64,256]{2,1,0:T(8,128)}, u32[]{:S(2)}, u32[]{:S(2)}) collective-permute-start(f32[4,64,256]{2,1,0:T(8,128)} %bitcast.326), channel_id=1, source_target_pairs={{0,16},{8,24},{16,0},{24,8},{1,17},{9,25},{17,1},{25,9},{2,18},{10... | collective-permute-start | bytes 786440 | tf_op jit(solution)/shard_map/ppermute | solution.py:157
  527.6 18.8 %collective-permute-start.9 = (f32[4,64,256]{2,1,0:T(8,128)}, f32[4,64,256]{2,1,0:T(8,128)}, u32[]{:S(2)}, u32[]{:S(2)}) collective-permute-start(f32[4,64,256]{2,1,0:T(8,128)} %bitcast.325), channel_id=1, source_target_pairs={{0,8},{8,16},{16,24},{24,0},{1,9},{9,17},{17,25},{25,1},{2,10},{10... | collective-permute-start | bytes 786440 | tf_op jit(solution)/shard_map/ppermute | solution.py:157
  552.6 18.5 %collective-permute-start.12 = (f32[4,64,256]{2,1,0:T(8,128)}, f32[4,64,256]{2,1,0:T(8,128)}, u32[]{:S(2)}, u32[]{:S(2)}) collective-permute-start(f32[4,64,256]{2,1,0:T(8,128)} %get-tuple-element.44), channel_id=1, source_target_pairs={{0,24},{8,0},{16,8},{24,16},{1,25},{9,1},{17,9},{25,17},{2,26},{10... | collective-permute-start | bytes 786440 | tf_op jit(solution)/shard_map/ppermute | solution.py:157
  555.5 15.6 %collective-permute-start.11 = (f32[4,64,256]{2,1,0:T(8,128)}, f32[4,64,256]{2,1,0:T(8,128)}, u32[]{:S(2)}, u32[]{:S(2)}) collective-permute-start(f32[4,64,256]{2,1,0:T(8,128)} %get-tuple-element.45), channel_id=1, source_target_pairs={{0,16},{8,24},{16,0},{24,8},{1,17},{9,25},{17,1},{25,9},{2,18},{10... | collective-permute-start | bytes 786440 | tf_op jit(solution)/shard_map/ppermute | solution.py:157
  556.1 15.1 %collective-permute-start.10 = (f32[4,64,256]{2,1,0:T(8,128)}, f32[4,64,256]{2,1,0:T(8,128)}, u32[]{:S(2)}, u32[]{:S(2)}) collective-permute-start(f32[4,64,256]{2,1,0:T(8,128)} %get-tuple-element.46), channel_id=1, source_target_pairs={{0,8},{8,16},{16,24},{24,0},{1,9},{9,17},{17,25},{25,1},{2,10},{10... | collective-permute-start | bytes 786440 | tf_op jit(solution)/shard_map/ppermute | solution.py:157
  566.1 31.6 %all-to-all-start.6 = ((f32[8,4,32,256]{3,2,1,0:T(8,128)}), f32[8,4,32,256]{3,2,1,0:T(8,128)S(1)}, u32[]{:S(2)}, u32[]{:S(2)}) async-start(f32[8,4,32,256]{3,2,1,0:T(8,128)} %reshape.373), calls=%async_computation.6 | async-start | bytes 2097152 | tf_op jit(solution)/shard_map/all_to_all | solution.py:191
  574.9 29.2 %collective-permute-start.13 = (f32[4,64,256]{2,1,0:T(8,128)}, f32[4,64,256]{2,1,0:T(8,128)S(1)}, u32[]{:S(2)}, u32[]{:S(2)}) collective-permute-start(f32[4,64,256]{2,1,0:T(8,128)} %bitcast.324), channel_id=1, source_target_pairs={{0,24},{8,0},{16,8},{24,16},{1,25},{9,1},{17,9},{25,17},{2,26},{10... | collective-permute-start | bytes 786440 | tf_op jit(solution)/shard_map/ppermute | solution.py:157
  578.6 25.8 %collective-permute-start.14 = (f32[4,64,256]{2,1,0:T(8,128)}, f32[4,64,256]{2,1,0:T(8,128)}, u32[]{:S(2)}, u32[]{:S(2)}) collective-permute-start(f32[4,64,256]{2,1,0:T(8,128)} %bitcast.323), channel_id=1, source_target_pairs={{0,16},{8,24},{16,0},{24,8},{1,17},{9,25},{17,1},{25,9},{2,18},{10... | collective-permute-start | bytes 786440 | tf_op jit(solution)/shard_map/ppermute | solution.py:157
  580.8 23.5 %collective-permute-start.15 = (f32[4,64,256]{2,1,0:T(8,128)}, f32[4,64,256]{2,1,0:T(8,128)S(1)}, u32[]{:S(2)}, u32[]{:S(2)}) collective-permute-start(f32[4,64,256]{2,1,0:T(8,128)} %bitcast.322), channel_id=1, source_target_pairs={{0,8},{8,16},{16,24},{24,0},{1,9},{9,17},{17,25},{25,1},{2,10},{10... | collective-permute-start | bytes 786440 | tf_op jit(solution)/shard_map/ppermute | solution.py:157
  599.8 16.3 %collective-permute-start.18 = (f32[4,64,256]{2,1,0:T(8,128)}, f32[4,64,256]{2,1,0:T(8,128)}, u32[]{:S(2)}, u32[]{:S(2)}) collective-permute-start(f32[4,64,256]{2,1,0:T(8,128)} %get-tuple-element.32), channel_id=1, source_target_pairs={{0,24},{8,0},{16,8},{24,16},{1,25},{9,1},{17,9},{25,17},{2,26},{10... | collective-permute-start | bytes 786440 | tf_op jit(solution)/shard_map/ppermute | solution.py:157
  611.9 28.2 %all-to-all-start.7 = ((f32[8,4,32,128]{3,2,1,0:T(8,128)}), f32[8,4,32,128]{3,2,1,0:T(8,128)}, u32[]{:S(2)}, u32[]{:S(2)}) async-start(f32[8,4,32,128]{3,2,1,0:T(8,128)} %reshape.378), calls=%async_computation.7 | async-start | bytes 1048576 | tf_op jit(solution)/shard_map/all_to_all | solution.py:191
  647.8 20.1 %all-to-all-start.8 = ((f32[8,4,32,128]{3,2,1,0:T(8,128)}), f32[8,4,32,128]{3,2,1,0:T(8,128)S(1)}, u32[]{:S(2)}, u32[]{:S(2)}) async-start(f32[8,4,32,128]{3,2,1,0:T(8,128)} %reshape.383), calls=%async_computation.8 | async-start | bytes 1048576 | tf_op jit(solution)/shard_map/all_to_all | solution.py:191
  (58 other events, 626.6 us)

commit v8 on v6

--- a/solution.py
+++ b/solution.py
@@ -73,10 +73,12 @@
         got = lax.all_to_all(blocks, "rad", 0, 0, tiled=True).reshape(n, kl, rl, mb)
         return jnp.transpose(got, (1, 0, 2, 3)).reshape(kl, radial, mb)
 
-    def to_radial_rows(y):
+    def to_radial_rows(y, companion=None):
         blocks = jnp.transpose(y.reshape(kl, n, rl, mb), (1, 0, 2, 3))
         got = lax.all_to_all(blocks, "rad", 0, 0, tiled=True).reshape(n, kl, rl, mb)
-        return jnp.transpose(got, (1, 2, 0, 3)).reshape(kl, rl, vc, cc)
+        if companion is not None:
+            companion, got = lax.optimization_barrier((companion, got))
+        return jnp.transpose(got, (1, 2, 0, 3)).reshape(kl, rl, vc, cc), companion
 
     def kinetic(columns):
         return jnp.einsum(
@@ -125,10 +127,10 @@
         rest = damp_full * (2.0 * local_part(current) - damp_full * earlier)
         following_columns = damp_columns * (2.0 * kinetic(columns)) + to_radial_columns(rest)
         earlier = current
-        current = to_radial_rows(following_columns)
+        current, _ = to_radial_rows(following_columns)
         columns = following_columns
-    kinetic_image = to_radial_rows(kinetic(columns))
-    image = kinetic_image + local_part(current)
+    kinetic_image, local_image = to_radial_rows(kinetic(columns), local_part(current))
+    image = kinetic_image + local_image
     current = damp_full * (2.0 * image - damp_full * earlier)
 
     hel_index = lax.axis_index("hel")

time: 689 us -> 660 us (0.958)
  waiting for transfers between devices: 349 us -> 317 us
    all_to_all x2, waiting for transfers between devices: 146 us -> 114 us  [to_radial_rows(): got = lax.all_to_all(blocks, 'rad', 0, 0, tiled=True).reshape(n, kl, rl, mb)]
where the time goes in v8:
time: 660 us; the launch traced here: 654 us
  waiting for transfers between devices  317 us (48%)
  local copies, waits for them, and re-layouts  153 us (23%)
  matrix products  80.4 us (12%)
  starting transfers between devices  77.3 us (12%)
  other arithmetic  24.7 us (4%)
    all_to_all x2, waiting for transfers between devices, to_radial_columns(): got = lax.all_to_all(blocks, 'rad', 0, 0, tiled=True).reshape(n, kl, rl, mb)  115 us
    all_to_all x2, waiting for transfers between devices, to_radial_rows(): got = lax.all_to_all(blocks, 'rad', 0, 0, tiled=True).reshape(n, kl, rl, mb)  114 us
    ppermute x24, waiting for transfers between devices, hel_shift(): return lax.ppermute(x, 'hel', [(i, (i + d) % nh) for i in range(nh)])  59.1 us
    ppermute x24, starting transfers between devices, hel_shift(): return lax.ppermute(x, 'hel', [(i, (i + d) % nh) for i in range(nh)])  29 us
    all_to_all x4, waiting for transfers between devices, shards(): lax.all_to_all(chans.reshape(n, kl, rl, width), 'rad', 0, 0, tiled=True)  28.7 us
    dot_general x2, matrix products, local_part(): jnp.dot(current.reshape(-1, cc), transform.T, precision=PRECISE, preferre...  25 us
    dot_general x2, matrix products, local_part(): jnp.dot(angles.reshape(-1, angles.shape[3]), transform, precision=PRECISE...  21.5 us
    reshape x3, local copies, waits for them, and re-layouts, to_radial_columns(): blocks = jnp.transpose(x.reshape(kl, rl, n, mb), (2, 0, 1, 3))  17.1 us
  transfers between devices with their start and end apart: 36, of which 20 were waited for; matrix products, arithmetic and copies ran while one was open for 26% of the time, Pallas kernels for 0%

profile of v8, /device:TPU:0, one launch (start us, length us, event | category | flops | bytes accessed | tf_op | source)
XLA Modules:
  0.0 654.0 jit_solution(2909044198441299556)
XLA Ops:
  5.9 6.6 %copy.100 = f32[8,4,32,1024]{3,2,1,0:T(8,128)} copy(f32[8,4,32,1024]{3,0,2,1:T(8,128)} %bitcast.282) | data formatting | bytes 8388608 | tf_op jit(solution)/shard_map/transpose | solution.py:72
  12.6 6.5 all-to-all-start
  35.8 16.4 %convolution_bitcast_fusion = f32[2048,512]{0,1:T(8,128)} fusion(f32[512,512]{1,0:T(8,128)S(1)} %convolution_multiply_fusion, f32[2048,512]{1,0:T(8,128)} %bitcast.273), kind=kOutput, calls=%fused_computation.24 | convolution fusion | flops 6442450944 | bytes 9437184 | tf_op jit(solution)/shard_map/dot_general | solution.py:93
  52.2 5.4 copy.102
  57.6 5.7 fusion.33
  63.3 11.8 %fusion.5 = f32[4,32,16,512]{3,2,1,0:T(8,128)} fusion(f32[1,32,16,512]{3,2,1,0:T(8,128)S(1)} %collective-permute-done, f32[3,32,16,512]{3,2,1,0:T(8,128)} %slice.154, f32[3,32,16,512]{3,2,1,0:T(8,128)S(1)} %slice-done.1, f32[1,32,16,512]{3,2,1,0:T(8,128)S(1)} %collective-permute-done.1, f32[4,32,16,512]{3,2,1,0:T(8,128)} %param.15, ...), kind=kOutput, calls=%fused_computation.9 | convolution fusion | flops 6456082432 | bytes 26288448 | tf_op jit(solution)/shard_map/dot_general | solution.py:105
  80.4 6.6 %copy.183 = f32[4,32,8,1024]{3,1,0,2:T(8,128)} copy(f32[4,32,8,1024]{3,2,1,0:T(8,128)} %reshape.331) | data formatting | bytes 8388608 | tf_op jit(solution)/shard_map/reshape | solution.py:72
  87.0 26.1 %all-to-all-done = f32[8,4,32,1024]{3,2,1,0:T(8,128)} async-done(((f32[8,4,32,1024]{3,2,1,0:T(8,128)}), f32[8,4,32,1024]{3,2,1,0:T(8,128)}, u32[]{:S(2)}, u32[]{:S(2)}) %all-to-all-start) | async-done | bytes 4194336 | tf_op jit(solution)/shard_map/all_to_all | solution.py:73
  122.8 89.2 %all-to-all-done.1 = f32[8,4,32,1024]{3,2,1,0:T(8,128)} async-done(((f32[8,4,32,1024]{3,2,1,0:T(8,128)}), f32[8,4,32,1024]{3,2,1,0:T(8,128)}, u32[]{:S(2)}, u32[]{:S(2)}) %all-to-all-start.1) | async-done | bytes 4194336 | tf_op jit(solution)/shard_map/all_to_all | solution.py:73
  227.3 5.6 fusion.35
  235.6 85.7 %all-to-all-done.2 = f32[8,4,32,1024]{3,2,1,0:T(8,128)} async-done(((f32[8,4,32,1024]{3,2,1,0:T(8,128)}), f32[8,4,32,1024]{3,2,1,0:T(8,128)}, u32[]{:S(2)}, u32[]{:S(2)}) %all-to-all-start.2) | async-done | bytes 4194336 | tf_op jit(solution)/shard_map/all_to_all | solution.py:78
  327.2 6.6 %copy.106 = f32[4,32,8,1024]{3,2,1,0:T(8,128)} copy(f32[4,32,8,1024]{3,1,0,2:T(8,128)} %bitcast.15) | data formatting | bytes 8388608 | tf_op jit(solution)/shard_map/transpose | solution.py:81
  359.5 5.4 copy.108
  369.5 8.6 %fusion.21 = f32[128,16,512]{2,1,0:T(8,128)S(1)} fusion(f32[128,16,512]{2,1,0:T(8,128)} %dot_general.72, f32[512,512]{1,0:T(8,128)S(1)} %convolution_multiply_fusion), kind=kOutput, calls=%fused_computation.44 | convolution fusion | flops 6442450944 | bytes 9437184 | tf_op jit(solution)/shard_map/dot_general | solution.py:93
  382.2 9.7 %fusion.8 = f32[4,32,16,512]{3,2,1,0:T(8,128)} fusion(f32[1,32,16,512]{3,2,1,0:T(8,128)S(1)} %collective-permute-done.2, f32[3,32,16,512]{3,2,1,0:T(8,128)S(1)} %copy-done.10, f32[3,32,16,512]{3,2,1,0:T(8,128)S(1)} %slice-done, f32[1,32,16,512]{3,2,1,0:T(8,128)S(1)} %collective-permute-done.3, f32[4,32,16,512]{3,2,1,0:T(8,128)S(1)} %copy-done.4, ...), kind=kOutput, calls=%fused_computation.13 | convolution fusion | flops 6451888128 | bytes 22094016 | tf_op jit(solution)/shard_map/dot_general | solution.py:105
  391.9 28.0 %all-to-all-done.3 = f32[8,4,32,1024]{3,2,1,0:T(8,128)} async-done(((f32[8,4,32,1024]{3,2,1,0:T(8,128)}), f32[8,4,32,1024]{3,2,1,0:T(8,128)}, u32[]{:S(2)}, u32[]{:S(2)}) %all-to-all-start.3) | async-done | bytes 4194336 | tf_op jit(solution)/shard_map/all_to_all | solution.py:78
  419.9 6.6 %copy.111 = f32[4,32,8,1024]{3,2,1,0:T(8,128)} copy(f32[4,32,8,1024]{3,1,0,2:T(8,128)} %bitcast.22) | data formatting | bytes 8388608 | tf_op jit(solution)/shard_map/transpose | solution.py:81
  431.4 6.3 subtract_multiply_fusion
  451.7 25.0 %all-to-all-done.4 = f32[8,4,32,256]{3,2,1,0:T(8,128)S(1)} async-done(((f32[8,4,32,256]{3,2,1,0:T(8,128)}), f32[8,4,32,256]{3,2,1,0:T(8,128)S(1)}, u32[]{:S(2)}, u32[]{:S(2)}) %all-to-all-start.4) | async-done | bytes 1048608 | tf_op jit(solution)/shard_map/all_to_all | solution.py:183
  495.3 5.3 collective-permute-done.6
  500.7 7.0 %collective-permute-done.5 = f32[4,64,256]{2,1,0:T(8,128)S(1)} collective-permute-done((f32[4,64,256]{2,1,0:T(8,128)S(1)}, f32[4,64,256]{2,1,0:T(8,128)S(1)}, u32[]{:S(2)}, u32[]{:S(2)}) %collective-permute-start.5) | collective-permute-done | bytes 262176 | tf_op jit(solution)/shard_map/ppermute | solution.py:150
  543.0 6.2 collective-permute-done.8
  552.0 7.7 %collective-permute-done.11 = f32[4,64,256]{2,1,0:T(8,128)S(1)} collective-permute-done((f32[4,64,256]{2,1,0:T(8,128)S(1)}, f32[4,64,256]{2,1,0:T(8,128)S(1)}, u32[]{:S(2)}, u32[]{:S(2)}) %collective-permute-start.11) | collective-permute-done | bytes 262176 | tf_op jit(solution)/shard_map/ppermute | solution.py:150
  600.2 6.2 collective-permute-done.17
  (253 shorter events, 258.0 us)
Async XLA Ops:
  12.6 100.6 %all-to-all-start = ((f32[8,4,32,1024]{3,2,1,0:T(8,128)}), f32[8,4,32,1024]{3,2,1,0:T(8,128)}, u32[]{:S(2)}, u32[]{:S(2)}) async-start(f32[8,4,32,1024]{3,2,1,0:T(8,128)} %copy.100), calls=%async_computation | async-start | bytes 8388608 | tf_op jit(solution)/shard_map/all_to_all | solution.py:73
  21.3 42.0 %collective-permute-start = (f32[1,32,16,512]{3,2,1,0:T(8,128)}, f32[1,32,16,512]{3,2,1,0:T(8,128)S(1)}, u32[]{:S(2)}, u32[]{:S(2)}) collective-permute-start(f32[1,32,16,512]{3,2,1,0:T(8,128)} %slice.155), channel_id=1, source_target_pairs={{8,0},{16,8},{24,16},{9,1},{17,9},{25,17},{10,2},{18,10},{26,18},{... | collective-permute-start | bytes 3145736 | tf_op jit(solution)/shard_map/ppermute | solution.py:13
  26.8 36.5 %collective-permute-start.1 = (f32[1,32,16,512]{3,2,1,0:T(8,128)}, f32[1,32,16,512]{3,2,1,0:T(8,128)S(1)}, u32[]{:S(2)}, u32[]{:S(2)}) collective-permute-start(f32[1,32,16,512]{3,2,1,0:T(8,128)} %slice.206), channel_id=1, source_target_pairs={{0,8},{8,16},{16,24},{1,9},{9,17},{17,25},{2,10},{10,18},{18,26},{... | collective-permute-start | bytes 3145736 | tf_op jit(solution)/shard_map/ppermute | solution.py:13
  113.1 98.9 %all-to-all-start.1 = ((f32[8,4,32,1024]{3,2,1,0:T(8,128)}), f32[8,4,32,1024]{3,2,1,0:T(8,128)}, u32[]{:S(2)}, u32[]{:S(2)}) async-start(f32[8,4,32,1024]{3,2,1,0:T(8,128)} %bitcast.279), calls=%async_computation.1 | async-start | bytes 8388608 | tf_op jit(solution)/shard_map/all_to_all | solution.py:73
  222.7 98.6 %all-to-all-start.2 = ((f32[8,4,32,1024]{3,2,1,0:T(8,128)}), f32[8,4,32,1024]{3,2,1,0:T(8,128)}, u32[]{:S(2)}, u32[]{:S(2)}) async-start(f32[8,4,32,1024]{3,2,1,0:T(8,128)} %bitcast.280), calls=%async_computation.2 | async-start | bytes 8388608 | tf_op jit(solution)/shard_map/all_to_all | solution.py:78
  321.3 98.6 %all-to-all-start.3 = ((f32[8,4,32,1024]{3,2,1,0:T(8,128)}), f32[8,4,32,1024]{3,2,1,0:T(8,128)}, u32[]{:S(2)}, u32[]{:S(2)}) async-start(f32[8,4,32,1024]{3,2,1,0:T(8,128)} %bitcast.278), calls=%async_computation.3 | async-start | bytes 8388608 | tf_op jit(solution)/shard_map/all_to_all | solution.py:78
  335.6 46.6 %collective-permute-start.2 = (f32[1,32,16,512]{3,2,1,0:T(8,128)}, f32[1,32,16,512]{3,2,1,0:T(8,128)S(1)}, u32[]{:S(2)}, u32[]{:S(2)}) collective-permute-start(f32[1,32,16,512]{3,2,1,0:T(8,128)} %slice.161), channel_id=1, source_target_pairs={{8,0},{16,8},{24,16},{9,1},{17,9},{25,17},{10,2},{18,10},{26,18},{... | collective-permute-start | bytes 3145736 | tf_op jit(solution)/shard_map/ppermute | solution.py:13
  346.0 36.2 %collective-permute-start.3 = (f32[1,32,16,512]{3,2,1,0:T(8,128)}, f32[1,32,16,512]{3,2,1,0:T(8,128)S(1)}, u32[]{:S(2)}, u32[]{:S(2)}) collective-permute-start(f32[1,32,16,512]{3,2,1,0:T(8,128)} %slice.210), channel_id=1, source_target_pairs={{0,8},{8,16},{16,24},{1,9},{9,17},{17,25},{2,10},{10,18},{18,26},{... | collective-permute-start | bytes 3145736 | tf_op jit(solution)/shard_map/ppermute | solution.py:13
  446.5 30.2 %all-to-all-start.4 = ((f32[8,4,32,256]{3,2,1,0:T(8,128)}), f32[8,4,32,256]{3,2,1,0:T(8,128)S(1)}, u32[]{:S(2)}, u32[]{:S(2)}) async-start(f32[8,4,32,256]{3,2,1,0:T(8,128)} %reshape.339), calls=%async_computation.4 | async-start | bytes 2097152 | tf_op jit(solution)/shard_map/all_to_all | solution.py:183
  485.9 30.1 %all-to-all-start.5 = ((f32[8,4,32,256]{3,2,1,0:T(8,128)}), f32[8,4,32,256]{3,2,1,0:T(8,128)S(1)}, u32[]{:S(2)}, u32[]{:S(2)}) async-start(f32[8,4,32,256]{3,2,1,0:T(8,128)} %reshape.344), calls=%async_computation.5 | async-start | bytes 2097152 | tf_op jit(solution)/shard_map/all_to_all | solution.py:183
  525.0 37.5 %all-to-all-start.6 = ((f32[8,4,32,256]{3,2,1,0:T(8,128)}), f32[8,4,32,256]{3,2,1,0:T(8,128)S(1)}, u32[]{:S(2)}, u32[]{:S(2)}) async-start(f32[8,4,32,256]{3,2,1,0:T(8,128)} %reshape.349), calls=%async_computation.6 | async-start | bytes 2097152 | tf_op jit(solution)/shard_map/all_to_all | solution.py:183
  534.3 15.0 %collective-permute-start.8 = (f32[4,64,256]{2,1,0:T(8,128)}, f32[4,64,256]{2,1,0:T(8,128)S(1)}, u32[]{:S(2)}, u32[]{:S(2)}) collective-permute-start(f32[4,64,256]{2,1,0:T(8,128)} %bitcast.271), channel_id=1, source_target_pairs={{0,16},{8,24},{16,0},{24,8},{1,17},{9,25},{17,1},{25,9},{2,18},{10... | collective-permute-start | bytes 786440 | tf_op jit(solution)/shard_map/ppermute | solution.py:150
  536.2 15.8 %collective-permute-start.12 = (f32[4,64,256]{2,1,0:T(8,128)S(1)}, f32[4,64,256]{2,1,0:T(8,128)S(1)}, u32[]{:S(2)}, u32[]{:S(2)}) collective-permute-start(f32[4,64,256]{2,1,0:T(8,128)S(1)} %get-tuple-element.43), channel_id=1, source_target_pairs={{0,24},{8,0},{16,8},{24,16},{1,25},{9,1},{17,9},{25,17},{2,26},{10... | collective-permute-start | bytes 786440 | tf_op jit(solution)/shard_map/ppermute | solution.py:150
  538.6 21.1 %collective-permute-start.11 = (f32[4,64,256]{2,1,0:T(8,128)S(1)}, f32[4,64,256]{2,1,0:T(8,128)S(1)}, u32[]{:S(2)}, u32[]{:S(2)}) collective-permute-start(f32[4,64,256]{2,1,0:T(8,128)S(1)} %get-tuple-element.44), channel_id=1, source_target_pairs={{0,16},{8,24},{16,0},{24,8},{1,17},{9,25},{17,1},{25,9},{2,18},{10... | collective-permute-start | bytes 786440 | tf_op jit(solution)/shard_map/ppermute | solution.py:150
  540.5 19.2 %collective-permute-start.10 = (f32[4,64,256]{2,1,0:T(8,128)S(1)}, f32[4,64,256]{2,1,0:T(8,128)S(1)}, u32[]{:S(2)}, u32[]{:S(2)}) collective-permute-start(f32[4,64,256]{2,1,0:T(8,128)S(1)} %get-tuple-element.45), channel_id=1, source_target_pairs={{0,8},{8,16},{16,24},{24,0},{1,9},{9,17},{17,25},{25,1},{2,10},{10... | collective-permute-start | bytes 786440 | tf_op jit(solution)/shard_map/ppermute | solution.py:150
  571.5 37.6 %all-to-all-start.7 = ((f32[8,4,32,256]{3,2,1,0:T(8,128)}), f32[8,4,32,256]{3,2,1,0:T(8,128)S(1)}, u32[]{:S(2)}, u32[]{:S(2)}) async-start(f32[8,4,32,256]{3,2,1,0:T(8,128)} %reshape.354), calls=%async_computation.7 | async-start | bytes 2097152 | tf_op jit(solution)/shard_map/all_to_all | solution.py:183
  580.8 15.1 %collective-permute-start.14 = (f32[4,64,256]{2,1,0:T(8,128)}, f32[4,64,256]{2,1,0:T(8,128)}, u32[]{:S(2)}, u32[]{:S(2)}) collective-permute-start(f32[4,64,256]{2,1,0:T(8,128)} %bitcast.268), channel_id=1, source_target_pairs={{0,16},{8,24},{16,0},{24,8},{1,17},{9,25},{17,1},{25,9},{2,18},{10... | collective-permute-start | bytes 786440 | tf_op jit(solution)/shard_map/ppermute | solution.py:150
  589.6 16.7 %collective-permute-start.17 = (f32[4,64,256]{2,1,0:T(8,128)}, f32[4,64,256]{2,1,0:T(8,128)}, u32[]{:S(2)}, u32[]{:S(2)}) collective-permute-start(f32[4,64,256]{2,1,0:T(8,128)} %get-tuple-element.56), channel_id=1, source_target_pairs={{0,16},{8,24},{16,0},{24,8},{1,17},{9,25},{17,1},{25,9},{2,18},{10... | collective-permute-start | bytes 786440 | tf_op jit(solution)/shard_map/ppermute | solution.py:150
  591.0 15.4 %collective-permute-start.16 = (f32[4,64,256]{2,1,0:T(8,128)S(1)}, f32[4,64,256]{2,1,0:T(8,128)}, u32[]{:S(2)}, u32[]{:S(2)}) collective-permute-start(f32[4,64,256]{2,1,0:T(8,128)S(1)} %get-tuple-element.57), channel_id=1, source_target_pairs={{0,8},{8,16},{16,24},{24,0},{1,9},{9,17},{17,25},{25,1},{2,10},{10... | collective-permute-start | bytes 786440 | tf_op jit(solution)/shard_map/ppermute | solution.py:150
  613.3 18.8 %collective-permute-start.19 = (f32[4,64,256]{2,1,0:T(8,128)S(1)}, f32[4,64,256]{2,1,0:T(8,128)S(1)}, u32[]{:S(2)}, u32[]{:S(2)}) collective-permute-start(f32[4,64,256]{2,1,0:T(8,128)S(1)} %bitcast.325), channel_id=1, source_target_pairs={{0,24},{8,0},{16,8},{24,16},{1,25},{9,1},{17,9},{25,17},{2,26},{10... | collective-permute-start | bytes 786440 | tf_op jit(solution)/shard_map/ppermute | solution.py:150
  614.8 20.4 %collective-permute-start.20 = (f32[4,64,256]{2,1,0:T(8,128)S(1)}, f32[4,64,256]{2,1,0:T(8,128)S(1)}, u32[]{:S(2)}, u32[]{:S(2)}) collective-permute-start(f32[4,64,256]{2,1,0:T(8,128)S(1)} %bitcast.324), channel_id=1, source_target_pairs={{0,16},{8,24},{16,0},{24,8},{1,17},{9,25},{17,1},{25,9},{2,18},{10... | collective-permute-start | bytes 786440 | tf_op jit(solution)/shard_map/ppermute | solution.py:150
  619.7 17.0 %collective-permute-start.21 = (f32[4,64,256]{2,1,0:T(8,128)S(1)}, f32[4,64,256]{2,1,0:T(8,128)S(1)}, u32[]{:S(2)}, u32[]{:S(2)}) collective-permute-start(f32[4,64,256]{2,1,0:T(8,128)S(1)} %bitcast.326), channel_id=1, source_target_pairs={{0,8},{8,16},{16,24},{24,0},{1,9},{9,17},{17,25},{25,1},{2,10},{10... | collective-permute-start | bytes 786440 | tf_op jit(solution)/shard_map/ppermute | solution.py:150
  630.7 16.3 %collective-permute-start.26 = (f32[4,64,256]{2,1,0:T(8,128)}, f32[4,64,256]{2,1,0:T(8,128)}, u32[]{:S(2)}, u32[]{:S(2)}) collective-permute-start(f32[4,64,256]{2,1,0:T(8,128)} %bitcast.262), channel_id=1, source_target_pairs={{0,16},{8,24},{16,0},{24,8},{1,17},{9,25},{17,1},{25,9},{2,18},{10... | collective-permute-start | bytes 786440 | tf_op jit(solution)/shard_map/ppermute | solution.py:150
  632.1 14.9 %collective-permute-start.27 = (f32[4,64,256]{2,1,0:T(8,128)}, f32[4,64,256]{2,1,0:T(8,128)}, u32[]{:S(2)}, u32[]{:S(2)}) collective-permute-start(f32[4,64,256]{2,1,0:T(8,128)} %bitcast.261), channel_id=1, source_target_pairs={{0,8},{8,16},{16,24},{24,0},{1,9},{9,17},{17,25},{25,1},{2,10},{10... | collective-permute-start | bytes 786440 | tf_op jit(solution)/shard_map/ppermute | solution.py:150
  (51 other events, 608.1 us)

commit v9 on v2

--- a/solution.py
+++ b/solution.py
@@ -73,21 +73,23 @@
         got = lax.all_to_all(blocks, "rad", 0, 0, tiled=True).reshape(n, kl, rl, mb)
         return jnp.transpose(got, (1, 0, 2, 3)).reshape(kl, radial, mb)
 
-    def to_radial_rows(y):
+    def to_radial_rows(y, companion=None):
         blocks = jnp.transpose(y.reshape(kl, n, rl, mb), (1, 0, 2, 3))
         got = lax.all_to_all(blocks, "rad", 0, 0, tiled=True).reshape(n, kl, rl, mb)
-        return jnp.transpose(got, (1, 2, 0, 3)).reshape(kl, rl, vc, cc)
+        if companion is not None:
+            companion, got = lax.optimization_barrier((companion, got))
+        return jnp.transpose(got, (1, 2, 0, 3)).reshape(kl, rl, vc, cc), companion
 
-    def hamiltonian(current):
-        columns = to_radial_columns(current)
-        applied = jnp.einsum(
+    def kinetic(columns):
+        return jnp.einsum(
             "krs,ksm->krm",
             kinetic_batched,
             columns,
             precision=PRECISE,
             preferred_element_type=jnp.float32,
         )
-        kinetic_image = to_radial_rows(applied)
+
+    def local_part(current):
         angles = jnp.dot(
             current.reshape(-1, cc), transform.T, precision=PRECISE,
             preferred_element_type=jnp.float32,
@@ -112,47 +114,48 @@
         upper_side = jnp.concatenate([current[1:], from_above], axis=0)
         lower_side = jnp.concatenate([from_below, weighted[:-1]], axis=0)
         return (
-            kinetic_image
-            + (angular.reshape(current.shape) + vib_energy[None, None, :, None] * current)
-            + radial_local[None, :, None, None]
-            * (coriolis[:, None, None, :] * upper_side + lower_side)
+            angular.reshape(current.shape) + vib_energy[None, None, :, None] * current
+        ) + radial_local[None, :, None, None] * (
+            coriolis[:, None, None, :] * upper_side + lower_side
         )
 
+    damp_columns = damping[None, :, None]
     earlier = prev_vector
     current = curr_vector
-    for iteration in range(STEPS):
-        image = hamiltonian(current)
-        following = damp_full * (2.0 * image - damp_full * earlier)
+    columns = to_radial_columns(current)
+    for iteration in range(STEPS - 1):
+        rest = damp_full * (2.0 * local_part(current) - damp_full * earlier)
+        following_columns = damp_columns * (2.0 * kinetic(columns)) + to_radial_columns(rest)
         earlier = current
-        current = following
+        current, _ = to_radial_rows(following_columns)
+        columns = following_columns
+    kinetic_image, local_image = to_radial_rows(kinetic(columns), local_part(current))
+    image = kinetic_image + local_image
+    current = damp_full * (2.0 * image - damp_full * earlier)
 
-    width = vc * cb
-    chans = jnp.transpose(current.reshape(kl, rl, vc, n, cb), (3, 0, 1, 2, 4))
-    got = lax.all_to_all(chans.reshape(n, kl, rl, width), "rad", 0, 0, tiled=True)
-    radial_block = jnp.transpose(got.reshape(n, kl, rl, width), (1, 0, 2, 3)).reshape(
-        kl, radial, width
-    )
     interp = interp_matrix(stencil, interp_weights, radial)
     qq = interp.shape[0]
-    qb = qq // nh
-    placed = jnp.einsum(
-        "kqr,krm->kqm",
-        jnp.broadcast_to(interp, (kl, qq, radial)),
-        radial_block,
+    vb = vc // nh
+    split_v = jnp.transpose(current.reshape(kl, rl, nh, vb, cc), (2, 0, 1, 3, 4))
+    all_k = lax.all_to_all(split_v, "hel", 0, 0, tiled=True)
+    turned = jnp.dot(
+        frame_rotation,
+        all_k.reshape(nh * kl, rl * vb * cc),
         precision=PRECISE,
         preferred_element_type=jnp.float32,
     )
-    pieces = jnp.transpose(placed.reshape(kl, nh, qb, width), (1, 0, 2, 3))
-    gathered = lax.all_to_all(pieces, "hel", 0, 0, tiled=True)
-    turned = jnp.dot(
-        frame_rotation,
-        gathered.reshape(nh * kl, qb * width),
+    outgoing = jnp.transpose(turned.reshape(nh, kl, rl, vb, n, cb), (0, 4, 1, 2, 3, 5))
+    arrived = lax.all_to_all(
+        outgoing.reshape(nh * n, kl, rl, vb * cb), ("hel", "rad"), 0, 0, tiled=True
+    )
+    columns = jnp.transpose(arrived.reshape(nh, n, kl, rl, vb, cb), (2, 1, 3, 0, 4, 5))
+    product_amp = jnp.einsum(
+        "kqr,krm->kqm",
+        jnp.broadcast_to(interp, (kl, qq, radial)),
+        columns.reshape(kl, radial, vc * cb),
         precision=PRECISE,
         preferred_element_type=jnp.float32,
-    )
-    back = lax.all_to_all(turned.reshape(nh, kl, qb, width), "hel", 0, 0, tiled=True)
-    rotated = jnp.transpose(back.reshape(nh, kl, qb, width), (1, 0, 2, 3))
-    product_amp = rotated.reshape(kl, qq, vc, cb)
+    ).reshape(kl, qq, vc, cb)
     return (current, product_amp)
 
 

time: 746 us -> 680 us (0.912)
  blocking collectives: 298 us -> 51.7 us
  waiting for transfers between devices: 209 us -> 324 us
  local copies, waits for them, and re-layouts: 118 us -> 160 us
  starting transfers between devices: 24.8 us -> 36.8 us
  other arithmetic: 3.25 us -> 14.6 us
    all_to_all x4 -> x1, blocking collectives: 298 us -> 51.7 us  [shards(): all_k = lax.all_to_all(split_v, 'hel', 0, 0, tiled=True)]
    all_to_all x1 -> x3, waiting for transfers between devices: 93.6 us -> 210 us  [the longest x2 116 us: to_radial_columns(): got = lax.all_to_all(blocks, 'rad', 0, 0, tiled=True).reshape(n, kl, rl, mb)]
    reshape x6 -> x10, local copies, waits for them, and re-layouts: 33.6 us -> 66.2 us  [the longest x2 15.8 us: shards(): turned.reshape(nh, kl, rl, vb, n, cb)]
    unnamed x38 -> x46, local copies, waits for them, and re-layouts: 22 us -> 1.61 us
    mul x1 -> x4, other arithmetic: 2.9 us -> 14.2 us  [the longest x1 8.77 us: shards(): current = damp_full * (2.0 * image - damp_full * earlier)]
    all_to_all x1 -> x3, starting transfers between devices: 4.69 us -> 15.4 us  [the longest x2 11.5 us: to_radial_columns(): got = lax.all_to_all(blocks, 'rad', 0, 0, tiled=True).reshape(n, kl, rl, mb)]
    slice x8 -> x14, local copies, waits for them, and re-layouts: 14.9 us -> 23.6 us  [the longest x4 15.9 us: local_part(): upper_side = jnp.concatenate([current[1:], from_above], axis=0)]
  transfers between devices with their start and end apart: 7 -> 9, of which waited for: 3 -> 5; matrix products, arithmetic and copies ran while one was open for 12% -> 20% of each run, Pallas kernels for 0% -> 0%
where the time goes in v9:
time: 680 us; the launch traced here: 674 us
  waiting for transfers between devices  324 us (48%)
  local copies, waits for them, and re-layouts  160 us (24%)
  matrix products  85.4 us (13%)
  blocking collectives  51.7 us (8%)
  starting transfers between devices  36.8 us (5%)
  other arithmetic  14.6 us (2%)
    all_to_all x2, waiting for transfers between devices, to_radial_columns(): got = lax.all_to_all(blocks, 'rad', 0, 0, tiled=True).reshape(n, kl, rl, mb)  116 us
    all_to_all x2, waiting for transfers between devices, to_radial_rows(): got = lax.all_to_all(blocks, 'rad', 0, 0, tiled=True).reshape(n, kl, rl, mb)  114 us
    all_to_all x1, waiting for transfers between devices, shards(): lax.all_to_all(outgoing.reshape(nh * n, kl, rl, vb * cb), ('hel', 'rad'),...  94.7 us
    all_to_all x1, blocking collectives, shards(): all_k = lax.all_to_all(split_v, 'hel', 0, 0, tiled=True)  51.7 us
    dot_general x2, matrix products, local_part(): jnp.dot(current.reshape(-1, cc), transform.T, precision=PRECISE, preferre...  25 us
    dot_general x2, matrix products, local_part(): jnp.dot(angles.reshape(-1, angles.shape[3]), transform, precision=PRECISE...  21 us
    reshape x3, local copies, waits for them, and re-layouts, to_radial_columns(): blocks = jnp.transpose(x.reshape(kl, rl, n, mb), (2, 0, 1, 3))  17.1 us
    slice x4, local copies, waits for them, and re-layouts, local_part(): upper_side = jnp.concatenate([current[1:], from_above], axis=0)  15.9 us
  transfers between devices with their start and end apart: 9, of which 5 were waited for; matrix products, arithmetic and copies ran while one was open for 20% of the time, Pallas kernels for 0%

profile of v9, /device:TPU:0, one launch (start us, length us, event | category | flops | bytes accessed | tf_op | source)
XLA Modules:
  0.0 674.4 jit_solution(15094708358980353934)
XLA Ops:
  5.9 6.6 copy.69
  12.6 6.5 all-to-all-start
  35.7 16.4 %convolution_bitcast_fusion.1 = f32[2048,512]{0,1:T(8,128)} fusion(f32[512,512]{1,0:T(8,128)S(1)} %convolution_multiply_fusion, f32[2048,512]{1,0:T(8,128)} %bitcast.81), kind=kOutput, calls=%fused_computation.23 | convolution fusion | flops 6442450944 | bytes 9437184 | tf_op jit(solution)/shard_map/dot_general | solution.py:93
  63.3 11.5 %fusion.5 = f32[4,32,16,512]{3,2,1,0:T(8,128)} fusion(f32[1,32,16,512]{3,2,1,0:T(8,128)S(1)} %collective-permute-done, f32[3,32,16,512]{3,2,1,0:T(8,128)} %slice.30, f32[3,32,16,512]{3,2,1,0:T(8,128)S(1)} %slice-done.1, f32[1,32,16,512]{3,2,1,0:T(8,128)S(1)} %collective-permute-done.1, f32[4,32,16,512]{3,2,1,0:T(8,128)} %param.15, ...), kind=kOutput, calls=%fused_computation.8 | convolution fusion | flops 6456082432 | bytes 26288448 | tf_op jit(solution)/shard_map/dot_general | solution.py:105
  80.0 6.6 copy.96
  86.7 26.5 %all-to-all-done = f32[8,4,32,1024]{3,2,1,0:T(8,128)} async-done(((f32[8,4,32,1024]{3,2,1,0:T(8,128)}), f32[8,4,32,1024]{3,2,1,0:T(8,128)}, u32[]{:S(2)}, u32[]{:S(2)}) %all-to-all-start) | async-done | bytes 4194336 | tf_op jit(solution)/shard_map/all_to_all | solution.py:73
  123.0 89.2 %all-to-all-done.1 = f32[8,4,32,1024]{3,2,1,0:T(8,128)} async-done(((f32[8,4,32,1024]{3,2,1,0:T(8,128)}), f32[8,4,32,1024]{3,2,1,0:T(8,128)}, u32[]{:S(2)}, u32[]{:S(2)}) %all-to-all-start.1) | async-done | bytes 4194336 | tf_op jit(solution)/shard_map/all_to_all | solution.py:73
  235.8 85.7 %all-to-all-done.2 = f32[8,4,32,1024]{3,2,1,0:T(8,128)} async-done(((f32[8,4,32,1024]{3,2,1,0:T(8,128)}), f32[8,4,32,1024]{3,2,1,0:T(8,128)}, u32[]{:S(2)}, u32[]{:S(2)}) %all-to-all-start.2) | async-done | bytes 4194336 | tf_op jit(solution)/shard_map/all_to_all | solution.py:78
  327.4 6.6 copy.75
  369.7 8.6 %fusion.21 = f32[128,16,512]{2,1,0:T(8,128)S(1)} fusion(f32[128,16,512]{2,1,0:T(8,128)} %dot_general.56, f32[512,512]{1,0:T(8,128)S(1)} %convolution_multiply_fusion), kind=kOutput, calls=%fused_computation.31 | convolution fusion | flops 6442450944 | bytes 9437184 | tf_op jit(solution)/shard_map/dot_general | solution.py:93
  382.5 9.5 %fusion.8 = f32[4,32,16,512]{3,2,1,0:T(8,128)} fusion(f32[1,32,16,512]{3,2,1,0:T(8,128)S(1)} %collective-permute-done.2, f32[3,32,16,512]{3,2,1,0:T(8,128)S(1)} %copy-done.9, f32[3,32,16,512]{3,2,1,0:T(8,128)S(1)} %slice-done, f32[1,32,16,512]{3,2,1,0:T(8,128)S(1)} %collective-permute-done.3, f32[4,32,16,512]{3,2,1,0:T(8,128)S(1)} %copy-done.4, ...), kind=kOutput, calls=%fused_computation.12 | convolution fusion | flops 6451888128 | bytes 22094016 | tf_op jit(solution)/shard_map/dot_general | solution.py:105
  391.9 28.2 %all-to-all-done.3 = f32[8,4,32,1024]{3,2,1,0:T(8,128)} async-done(((f32[8,4,32,1024]{3,2,1,0:T(8,128)}), f32[8,4,32,1024]{3,2,1,0:T(8,128)}, u32[]{:S(2)}, u32[]{:S(2)}) %all-to-all-start.3) | async-done | bytes 4194336 | tf_op jit(solution)/shard_map/all_to_all | solution.py:78
  420.1 6.6 copy.80
  431.7 8.8 %subtract_multiply_fusion = f32[4,32,16,512]{3,2,1,0:T(8,128)} fusion(f32[4,32,16,512]{3,2,1,0:T(8,128)} %param.16, f32[4,32,16,512]{3,2,1,0:T(8,128)} %reshape.143, f32[4,32,16,512]{3,2,1,0:T(8,128)} %fusion.8, f32[32]{0:T(128)S(1)} %dynamic_slice.6), kind=kLoop, calls=%fused_computation.18 | loop fusion | flops 5242880 | bytes 16777344 | tf_op jit(solution)/shard_map/mul | solution.py:134
  448.9 51.7 %all_to_all.30 = f32[4,4,32,4,512]{4,3,2,1,0:T(4,128)} all-to-all(f32[4,4,32,4,512]{4,3,2,1,0:T(4,128)S(1)} %bitcast.92), channel_id=1, replica_groups=mesh['hel'=4,'rad'=8] {'hel'}, dimensions={0} | all-to-all | bytes 8388608 | tf_op jit(solution)/shard_map/all_to_all | solution.py:140
  506.5 7.9 %convolution_bitcast_fusion = f32[16,65536]{1,0:T(8,128)} fusion(f32[16,65536]{1,0:T(8,128)} %reshape.145, f32[16,16]{1,0:T(8,128)S(1)} %copy-done.15), kind=kOutput, calls=%fused_computation | convolution fusion | flops 201326592 | bytes 8389632 | tf_op jit(solution)/shard_map/dot_general | solution.py:141
  514.4 7.0 %reshape.146 = f32[4,4,32,4,8,64]{5,4,3,2,1,0:T(8,128)} reshape(f32[16,65536]{1,0:T(8,128)} %convolution_bitcast_fusion) | data formatting | bytes 8388608 | tf_op jit(solution)/shard_map/reshape | solution.py:147
  521.3 8.9 %copy.92 = f32[4,4,32,4,8,64]{5,3,2,1,4,0:T(4,128)} copy(f32[4,4,32,4,8,64]{5,4,3,2,1,0:T(8,128)} %reshape.146) | data formatting | bytes 8388608 | tf_op jit(solution)/shard_map/reshape | solution.py:147
  530.2 8.6 %reshape.147 = f32[32,4,32,256]{3,2,1,0:T(8,128)} reshape(f32[4,8,4,32,4,64]{5,4,3,2,1,0:T(4,128)} %bitcast.83) | data formatting | bytes 8388608 | tf_op jit(solution)/shard_map/reshape | solution.py:149
  543.0 94.7 %all-to-all-done.5 = f32[32,4,32,256]{3,2,1,0:T(8,128)} async-done(((f32[32,4,32,256]{3,2,1,0:T(8,128)}), f32[32,4,32,256]{3,2,1,0:T(8,128)}, u32[]{:S(2)}, u32[]{:S(2)}) %all-to-all-start.5) | async-done | bytes 4194336 | tf_op jit(solution)/shard_map/all_to_all | solution.py:148
  637.7 8.1 %reshape.148 = f32[4,8,4,32,4,64]{5,4,3,2,1,0:T(4,128)} reshape(f32[32,4,32,256]{3,2,1,0:T(8,128)} %all-to-all-done.5) | data formatting | bytes 8388608 | tf_op jit(solution)/shard_map/reshape | solution.py:151
  645.8 8.2 %copy.83 = f32[4,8,32,4,4,64]{5,4,3,2,1,0:T(4,128)} copy(f32[4,8,32,4,4,64]{5,4,2,0,1,3:T(4,128)} %bitcast.84) | data formatting | bytes 8388608 | tf_op jit(solution)/shard_map/transpose | solution.py:151
  654.1 9.3 %reshape.149 = f32[4,256,1024]{2,1,0:T(8,128)} reshape(f32[4,8,32,4,4,64]{5,4,3,2,1,0:T(4,128)} %copy.83) | data formatting | bytes 8388608 | tf_op jit(solution)/shard_map/reshape | solution.py:155
  663.4 10.9 %fusion.23 = f32[4,256,1024]{1,2,0:T(8,128)} fusion(f32[4,256,1024]{2,1,0:T(8,128)} %reshape.149, f32[256,256]{1,0:T(8,128)S(1)} %select_reduce_fusion), kind=kOutput, calls=%fused_computation.35 | convolution fusion | flops 3221225472 | bytes 8650752 | tf_op jit(solution)/shard_map/kqr,krm->kqm/dot_general | solution.py:152
  (99 shorter events, 140.5 us)
Async XLA Ops:
  0.6 214.5 %copy-start = (f32[256,256]{1,0:T(8,128)S(1)}, f32[256,256]{1,0:T(8,128)}, u32[]{:S(2)}) copy-start(f32[256,256]{1,0:T(8,128)} %param.17) | copy-start | bytes 786436
  12.6 10.3 %copy-start.11 = (f32[4,512]{1,0:T(4,128)S(1)}, f32[4,512]{1,0:T(4,128)}, u32[]{:S(2)}) copy-start(f32[4,512]{1,0:T(4,128)} %param.24) | copy-start | bytes 24580
  12.6 100.6 %all-to-all-start = ((f32[8,4,32,1024]{3,2,1,0:T(8,128)}), f32[8,4,32,1024]{3,2,1,0:T(8,128)}, u32[]{:S(2)}, u32[]{:S(2)}) async-start(f32[8,4,32,1024]{3,2,1,0:T(8,128)} %copy.69), calls=%async_computation | async-start | bytes 8388608 | tf_op jit(solution)/shard_map/all_to_all | solution.py:73
  21.3 10.3 %copy-start.2 = (f32[4,32,16,512]{3,2,1,0:T(8,128)S(1)}, f32[4,32,16,512]{3,2,1,0:T(8,128)}, u32[]{:S(2)}) copy-start(f32[4,32,16,512]{3,2,1,0:T(8,128)} %param.16) | copy-start | bytes 12582916
  21.3 41.9 %collective-permute-start = (f32[1,32,16,512]{3,2,1,0:T(8,128)}, f32[1,32,16,512]{3,2,1,0:T(8,128)S(1)}, u32[]{:S(2)}, u32[]{:S(2)}) collective-permute-start(f32[1,32,16,512]{3,2,1,0:T(8,128)} %slice.31), channel_id=1, source_target_pairs={{8,0},{16,8},{24,16},{9,1},{17,9},{25,17},{10,2},{18,10},{26,18},{... | collective-permute-start | bytes 3145736 | tf_op jit(solution)/shard_map/ppermute | solution.py:13
  25.6 7.9 %copy-start.8 = (f32[4,32,16,512]{3,2,1,0:T(8,128)}, f32[4,32,16,512]{3,2,1,0:T(8,128)S(1)}, u32[]{:S(2)}) copy-start(f32[4,32,16,512]{3,2,1,0:T(8,128)S(1)} %broadcast_multiply_fusion.1) | copy-start | bytes 12582916
  26.8 36.4 %collective-permute-start.1 = (f32[1,32,16,512]{3,2,1,0:T(8,128)}, f32[1,32,16,512]{3,2,1,0:T(8,128)S(1)}, u32[]{:S(2)}, u32[]{:S(2)}) collective-permute-start(f32[1,32,16,512]{3,2,1,0:T(8,128)} %slice.40), channel_id=1, source_target_pairs={{0,8},{8,16},{16,24},{1,9},{9,17},{17,25},{2,10},{10,18},{18,26},{... | collective-permute-start | bytes 3145736 | tf_op jit(solution)/shard_map/ppermute | solution.py:13
  52.1 5.4 copy-start.14
  57.5 5.7 copy-start.3
  57.5 5.7 slice-start.1
  57.5 5.8 copy-start.10
  57.5 5.7 copy-start.16
  113.1 5.1 copy-start.21
  113.1 99.1 %all-to-all-start.1 = ((f32[8,4,32,1024]{3,2,1,0:T(8,128)}), f32[8,4,32,1024]{3,2,1,0:T(8,128)}, u32[]{:S(2)}, u32[]{:S(2)}) async-start(f32[8,4,32,1024]{3,2,1,0:T(8,128)} %bitcast.89), calls=%async_computation.1 | async-start | bytes 8388608 | tf_op jit(solution)/shard_map/all_to_all | solution.py:73
  223.0 98.6 %all-to-all-start.2 = ((f32[8,4,32,1024]{3,2,1,0:T(8,128)}), f32[8,4,32,1024]{3,2,1,0:T(8,128)}, u32[]{:S(2)}, u32[]{:S(2)}) async-start(f32[8,4,32,1024]{3,2,1,0:T(8,128)} %bitcast.90), calls=%async_computation.2 | async-start | bytes 8388608 | tf_op jit(solution)/shard_map/all_to_all | solution.py:78
  321.6 98.6 %all-to-all-start.3 = ((f32[8,4,32,1024]{3,2,1,0:T(8,128)}), f32[8,4,32,1024]{3,2,1,0:T(8,128)}, u32[]{:S(2)}, u32[]{:S(2)}) async-start(f32[8,4,32,1024]{3,2,1,0:T(8,128)} %bitcast.88), calls=%async_computation.3 | async-start | bytes 8388608 | tf_op jit(solution)/shard_map/all_to_all | solution.py:78
  335.8 46.6 %collective-permute-start.2 = (f32[1,32,16,512]{3,2,1,0:T(8,128)}, f32[1,32,16,512]{3,2,1,0:T(8,128)S(1)}, u32[]{:S(2)}, u32[]{:S(2)}) collective-permute-start(f32[1,32,16,512]{3,2,1,0:T(8,128)} %slice.37), channel_id=1, source_target_pairs={{8,0},{16,8},{24,16},{9,1},{17,9},{25,17},{10,2},{18,10},{26,18},{... | collective-permute-start | bytes 3145736 | tf_op jit(solution)/shard_map/ppermute | solution.py:13
  345.1 9.8 %copy-start.7 = (f32[4,32,16,512]{3,2,1,0:T(8,128)}, f32[4,32,16,512]{3,2,1,0:T(8,128)S(1)}, u32[]{:S(2)}) copy-start(f32[4,32,16,512]{3,2,1,0:T(8,128)S(1)} %broadcast_multiply_fusion) | copy-start | bytes 12582916
  346.3 36.2 %collective-permute-start.3 = (f32[1,32,16,512]{3,2,1,0:T(8,128)}, f32[1,32,16,512]{3,2,1,0:T(8,128)S(1)}, u32[]{:S(2)}, u32[]{:S(2)}) collective-permute-start(f32[1,32,16,512]{3,2,1,0:T(8,128)} %slice.44), channel_id=1, source_target_pairs={{0,8},{8,16},{16,24},{1,9},{9,17},{17,25},{2,10},{10,18},{18,26},{... | collective-permute-start | bytes 3145736 | tf_op jit(solution)/shard_map/ppermute | solution.py:13
  369.7 12.7 %copy-start.9 = (f32[3,32,16,512]{3,2,1,0:T(8,128)S(1)}, f32[3,32,16,512]{3,2,1,0:T(8,128)}, u32[]{:S(2)}) copy-start(f32[3,32,16,512]{3,2,1,0:T(8,128)} %slice.35) | copy-start | bytes 9437188
  378.3 4.1 copy-start.4
  500.6 5.8 copy-start.15
  538.8 98.9 %all-to-all-start.5 = ((f32[32,4,32,256]{3,2,1,0:T(8,128)}), f32[32,4,32,256]{3,2,1,0:T(8,128)}, u32[]{:S(2)}, u32[]{:S(2)}) async-start(f32[32,4,32,256]{3,2,1,0:T(8,128)} %reshape.147), calls=%async_computation.5 | async-start | bytes 8388608 | tf_op jit(solution)/shard_map/all_to_all | solution.py:148
  654.1 20.2 %copy-start.1 = (f32[256,256]{1,0:T(8,128)S(1)}, f32[256,256]{1,0:T(8,128)}, u32[]{:S(2)}) copy-start(f32[256,256]{1,0:T(8,128)} %param.17) | copy-start | bytes 786436
  (10 other events, 23.3 us)

commit v10 on v8

--- a/solution.py
+++ b/solution.py
@@ -149,11 +149,16 @@
             return x
         return lax.ppermute(x, "hel", [(i, (i + d) % nh) for i in range(nh)])
 
-    vchunks = 4 if vc % 4 == 0 else 1
-    vs = vc // vchunks
-    width = vs * cb
+    if vc % 8 == 0:
+        sizes = [vc // 8] + [vc // 4] * 3 + [vc // 8]
+    else:
+        sizes = [vc]
+    bounds = [sum(sizes[:i]) for i in range(len(sizes) + 1)]
     results = []
+
     def finish(placed):
+        vs = placed.shape[2] // cb
+        width = vs * cb
         arrived = [hel_shift(placed[:, d * qb:(d + 1) * qb], d) for d in range(nh)]
         gathered = jnp.stack(arrived, axis=0)
         turned = jnp.dot(
@@ -174,8 +179,10 @@
         results.append(rotated.reshape(kl, qq, vs, cb))
 
     pending = None
-    for i in range(vchunks):
-        part = current[:, :, i * vs:(i + 1) * vs, :]
+    for lo, hi in zip(bounds[:-1], bounds[1:]):
+        part = current[:, :, lo:hi, :]
+        vs = hi - lo
+        width = vs * cb
         if pending is not None:
             pending, part = lax.optimization_barrier((pending, part))
             finish(pending)

time: 660 us -> 657 us (level)
  starting transfers between devices: 77.3 us -> 85 us
  waiting for transfers between devices: 317 us -> 310 us
    ppermute x24 -> x30, waiting for transfers between devices: 59.1 us -> 38.1 us  [hel_shift(): return lax.ppermute(x, 'hel', [(i, (i + d) % nh) for i in range(nh)])]
    all_to_all x4 -> x5, waiting for transfers between devices: 28.7 us -> 45.1 us  [shards(): lax.all_to_all(chans.reshape(n, kl, rl, width), 'rad', 0, 0, tiled=True)]
    unnamed x90 -> x82, local copies, waits for them, and re-layouts: 13 us -> 18.5 us
    ppermute x24 -> x30, starting transfers between devices: 29 us -> 34.4 us  [hel_shift(): return lax.ppermute(x, 'hel', [(i, (i + d) % nh) for i in range(nh)])]
    all_to_all x4 -> x5, starting transfers between devices: 15.6 us -> 17.8 us  [shards(): lax.all_to_all(chans.reshape(n, kl, rl, width), 'rad', 0, 0, tiled=True)]
    reshape x8 -> x10, local copies, waits for them, and re-layouts: 13.6 us -> 13.2 us  [shards(): chans = jnp.transpose(part.reshape(kl, rl, vs, n, cb), (3, 0, 1, 2, 4))]
  transfers between devices with their start and end apart: 36 -> 43, of which waited for: 20 -> 20; matrix products, arithmetic and copies ran while one was open for 26% -> 29% of each run, Pallas kernels for 0% -> 0%
where the time goes in v10:
time: 657 us; the launch traced here: 652 us
  waiting for transfers between devices  310 us (47%)
  local copies, waits for them, and re-layouts  154 us (23%)
  starting transfers between devices  85 us (13%)
  matrix products  77.8 us (12%)
  other arithmetic  22.7 us (3%)
    all_to_all x2, waiting for transfers between devices, to_radial_columns(): got = lax.all_to_all(blocks, 'rad', 0, 0, tiled=True).reshape(n, kl, rl, mb)  115 us
    all_to_all x2, waiting for transfers between devices, to_radial_rows(): got = lax.all_to_all(blocks, 'rad', 0, 0, tiled=True).reshape(n, kl, rl, mb)  112 us
    all_to_all x5, waiting for transfers between devices, shards(): lax.all_to_all(chans.reshape(n, kl, rl, width), 'rad', 0, 0, tiled=True)  45.1 us
    ppermute x30, waiting for transfers between devices, hel_shift(): return lax.ppermute(x, 'hel', [(i, (i + d) % nh) for i in range(nh)])  38.1 us
    ppermute x30, starting transfers between devices, hel_shift(): return lax.ppermute(x, 'hel', [(i, (i + d) % nh) for i in range(nh)])  34.4 us
    dot_general x2, matrix products, local_part(): jnp.dot(current.reshape(-1, cc), transform.T, precision=PRECISE, preferre...  25 us
    dot_general x2, matrix products, local_part(): jnp.dot(angles.reshape(-1, angles.shape[3]), transform, precision=PRECISE...  21.5 us
    unnamed x82, local copies, waits for them, and re-layouts  18.5 us
  transfers between devices with their start and end apart: 43, of which 20 were waited for; matrix products, arithmetic and copies ran while one was open for 29% of the time, Pallas kernels for 0%

profile of v10, /device:TPU:0, one launch (start us, length us, event | category | flops | bytes accessed | tf_op | source)
XLA Modules:
  0.0 651.5 jit_solution(12688627779270563508)
XLA Ops:
  5.9 6.6 %copy.110 = f32[8,4,32,1024]{3,2,1,0:T(8,128)} copy(f32[8,4,32,1024]{3,0,2,1:T(8,128)} %bitcast.343) | data formatting | bytes 8388608 | tf_op jit(solution)/shard_map/transpose | solution.py:72
  12.6 6.5 all-to-all-start
  35.8 16.4 %convolution_bitcast_fusion = f32[2048,512]{0,1:T(8,128)} fusion(f32[512,512]{1,0:T(8,128)S(1)} %convolution_multiply_fusion, f32[2048,512]{1,0:T(8,128)} %bitcast.334), kind=kOutput, calls=%fused_computation.23 | convolution fusion | flops 6442450944 | bytes 9437184 | tf_op jit(solution)/shard_map/dot_general | solution.py:93
  52.2 5.4 copy.112
  57.6 5.7 fusion.41
  63.3 11.8 %fusion.5 = f32[4,32,16,512]{3,2,1,0:T(8,128)} fusion(f32[1,32,16,512]{3,2,1,0:T(8,128)S(1)} %collective-permute-done, f32[3,32,16,512]{3,2,1,0:T(8,128)} %slice.185, f32[3,32,16,512]{3,2,1,0:T(8,128)S(1)} %slice-done.1, f32[1,32,16,512]{3,2,1,0:T(8,128)S(1)} %collective-permute-done.1, f32[4,32,16,512]{3,2,1,0:T(8,128)} %param.15, ...), kind=kOutput, calls=%fused_computation.9 | convolution fusion | flops 6456082432 | bytes 26288448 | tf_op jit(solution)/shard_map/dot_general | solution.py:105
  80.4 6.6 %copy.217 = f32[4,32,8,1024]{3,1,0,2:T(8,128)} copy(f32[4,32,8,1024]{3,2,1,0:T(8,128)} %reshape.355) | data formatting | bytes 8388608 | tf_op jit(solution)/shard_map/reshape | solution.py:72
  87.0 26.1 %all-to-all-done = f32[8,4,32,1024]{3,2,1,0:T(8,128)} async-done(((f32[8,4,32,1024]{3,2,1,0:T(8,128)}), f32[8,4,32,1024]{3,2,1,0:T(8,128)}, u32[]{:S(2)}, u32[]{:S(2)}) %all-to-all-start) | async-done | bytes 4194336 | tf_op jit(solution)/shard_map/all_to_all | solution.py:73
  122.8 89.2 %all-to-all-done.1 = f32[8,4,32,1024]{3,2,1,0:T(8,128)} async-done(((f32[8,4,32,1024]{3,2,1,0:T(8,128)}), f32[8,4,32,1024]{3,2,1,0:T(8,128)}, u32[]{:S(2)}, u32[]{:S(2)}) %all-to-all-start.1) | async-done | bytes 4194336 | tf_op jit(solution)/shard_map/all_to_all | solution.py:73
  227.3 5.6 fusion.43
  235.5 85.7 %all-to-all-done.2 = f32[8,4,32,1024]{3,2,1,0:T(8,128)} async-done(((f32[8,4,32,1024]{3,2,1,0:T(8,128)}), f32[8,4,32,1024]{3,2,1,0:T(8,128)}, u32[]{:S(2)}, u32[]{:S(2)}) %all-to-all-start.2) | async-done | bytes 4194336 | tf_op jit(solution)/shard_map/all_to_all | solution.py:78
  327.2 6.6 %copy.116 = f32[4,32,8,1024]{3,2,1,0:T(8,128)} copy(f32[4,32,8,1024]{3,1,0,2:T(8,128)} %bitcast.15) | data formatting | bytes 8388608 | tf_op jit(solution)/shard_map/transpose | solution.py:81
  361.7 5.4 copy.118
  371.6 8.6 %fusion.21 = f32[128,16,512]{2,1,0:T(8,128)S(1)} fusion(f32[128,16,512]{2,1,0:T(8,128)} %dot_general.78, f32[512,512]{1,0:T(8,128)S(1)} %convolution_multiply_fusion), kind=kOutput, calls=%fused_computation.40 | convolution fusion | flops 6442450944 | bytes 9437184 | tf_op jit(solution)/shard_map/dot_general | solution.py:93
  384.4 9.7 %fusion.8 = f32[4,32,16,512]{3,2,1,0:T(8,128)} fusion(f32[1,32,16,512]{3,2,1,0:T(8,128)S(1)} %collective-permute-done.2, f32[3,32,16,512]{3,2,1,0:T(8,128)S(1)} %copy-done.10, f32[3,32,16,512]{3,2,1,0:T(8,128)S(1)} %slice-done, f32[1,32,16,512]{3,2,1,0:T(8,128)S(1)} %collective-permute-done.3, f32[4,32,16,512]{3,2,1,0:T(8,128)S(1)} %copy-done.4, ...), kind=kOutput, calls=%fused_computation.13 | convolution fusion | flops 6451888128 | bytes 22094016 | tf_op jit(solution)/shard_map/dot_general | solution.py:105
  394.0 25.8 %all-to-all-done.3 = f32[8,4,32,1024]{3,2,1,0:T(8,128)} async-done(((f32[8,4,32,1024]{3,2,1,0:T(8,128)}), f32[8,4,32,1024]{3,2,1,0:T(8,128)}, u32[]{:S(2)}, u32[]{:S(2)}) %all-to-all-start.3) | async-done | bytes 4194336 | tf_op jit(solution)/shard_map/all_to_all | solution.py:78
  419.8 6.6 %copy.121 = f32[4,32,8,1024]{3,2,1,0:T(8,128)} copy(f32[4,32,8,1024]{3,1,0,2:T(8,128)} %bitcast.22) | data formatting | bytes 8388608 | tf_op jit(solution)/shard_map/transpose | solution.py:81
  431.4 6.3 subtract_multiply_fusion
  447.8 5.8 fusion.96
  453.6 8.1 %all-to-all-done.4 = f32[8,4,32,128]{3,2,1,0:T(8,128)S(1)} async-done(((f32[8,4,32,128]{3,2,1,0:T(8,128)}), f32[8,4,32,128]{3,2,1,0:T(8,128)S(1)}, u32[]{:S(2)}, u32[]{:S(2)}) %all-to-all-start.4) | async-done | bytes 524320 | tf_op jit(solution)/shard_map/all_to_all | solution.py:190
  485.4 15.2 %all-to-all-done.5 = f32[8,4,32,256]{3,2,1,0:T(8,128)S(1)} async-done(((f32[8,4,32,256]{3,2,1,0:T(8,128)}), f32[8,4,32,256]{3,2,1,0:T(8,128)S(1)}, u32[]{:S(2)}, u32[]{:S(2)}) %all-to-all-start.5) | async-done | bytes 1048608 | tf_op jit(solution)/shard_map/all_to_all | solution.py:190
  536.4 7.7 %collective-permute-done.14 = f32[4,64,256]{2,1,0:T(8,128)} collective-permute-done((f32[4,64,256]{2,1,0:T(8,128)}, f32[4,64,256]{2,1,0:T(8,128)}, u32[]{:S(2)}, u32[]{:S(2)}) %collective-permute-start.14) | collective-permute-done | bytes 262176 | tf_op jit(solution)/shard_map/ppermute | solution.py:150
  573.6 18.3 %all-to-all-done.7 = f32[8,4,32,256]{3,2,1,0:T(8,128)S(1)} async-done(((f32[8,4,32,256]{3,2,1,0:T(8,128)}), f32[8,4,32,256]{3,2,1,0:T(8,128)S(1)}, u32[]{:S(2)}, u32[]{:S(2)}) %all-to-all-start.7) | async-done | bytes 1048608 | tf_op jit(solution)/shard_map/all_to_all | solution.py:190
  622.0 6.9 %collective-permute-done.26 = f32[4,64,256]{2,1,0:T(8,128)} collective-permute-done((f32[4,64,256]{2,1,0:T(8,128)}, f32[4,64,256]{2,1,0:T(8,128)}, u32[]{:S(2)}, u32[]{:S(2)}) %collective-permute-start.26) | collective-permute-done | bytes 262176 | tf_op jit(solution)/shard_map/ppermute | solution.py:150
  (270 shorter events, 253.0 us)
Async XLA Ops:
  12.6 100.6 %all-to-all-start = ((f32[8,4,32,1024]{3,2,1,0:T(8,128)}), f32[8,4,32,1024]{3,2,1,0:T(8,128)}, u32[]{:S(2)}, u32[]{:S(2)}) async-start(f32[8,4,32,1024]{3,2,1,0:T(8,128)} %copy.110), calls=%async_computation | async-start | bytes 8388608 | tf_op jit(solution)/shard_map/all_to_all | solution.py:73
  21.3 41.9 %collective-permute-start = (f32[1,32,16,512]{3,2,1,0:T(8,128)}, f32[1,32,16,512]{3,2,1,0:T(8,128)S(1)}, u32[]{:S(2)}, u32[]{:S(2)}) collective-permute-start(f32[1,32,16,512]{3,2,1,0:T(8,128)} %slice.186), channel_id=1, source_target_pairs={{8,0},{16,8},{24,16},{9,1},{17,9},{25,17},{10,2},{18,10},{26,18},{... | collective-permute-start | bytes 3145736 | tf_op jit(solution)/shard_map/ppermute | solution.py:13
  26.8 36.5 %collective-permute-start.1 = (f32[1,32,16,512]{3,2,1,0:T(8,128)}, f32[1,32,16,512]{3,2,1,0:T(8,128)S(1)}, u32[]{:S(2)}, u32[]{:S(2)}) collective-permute-start(f32[1,32,16,512]{3,2,1,0:T(8,128)} %slice.246), channel_id=1, source_target_pairs={{0,8},{8,16},{16,24},{1,9},{9,17},{17,25},{2,10},{10,18},{18,26},{... | collective-permute-start | bytes 3145736 | tf_op jit(solution)/shard_map/ppermute | solution.py:13
  113.1 98.9 %all-to-all-start.1 = ((f32[8,4,32,1024]{3,2,1,0:T(8,128)}), f32[8,4,32,1024]{3,2,1,0:T(8,128)}, u32[]{:S(2)}, u32[]{:S(2)}) async-start(f32[8,4,32,1024]{3,2,1,0:T(8,128)} %bitcast.340), calls=%async_computation.1 | async-start | bytes 8388608 | tf_op jit(solution)/shard_map/all_to_all | solution.py:73
  222.7 98.6 %all-to-all-start.2 = ((f32[8,4,32,1024]{3,2,1,0:T(8,128)}), f32[8,4,32,1024]{3,2,1,0:T(8,128)}, u32[]{:S(2)}, u32[]{:S(2)}) async-start(f32[8,4,32,1024]{3,2,1,0:T(8,128)} %bitcast.341), calls=%async_computation.2 | async-start | bytes 8388608 | tf_op jit(solution)/shard_map/all_to_all | solution.py:78
  321.3 98.6 %all-to-all-start.3 = ((f32[8,4,32,1024]{3,2,1,0:T(8,128)}), f32[8,4,32,1024]{3,2,1,0:T(8,128)}, u32[]{:S(2)}, u32[]{:S(2)}) async-start(f32[8,4,32,1024]{3,2,1,0:T(8,128)} %bitcast.339), calls=%async_computation.3 | async-start | bytes 8388608 | tf_op jit(solution)/shard_map/all_to_all | solution.py:78
  335.6 48.7 %collective-permute-start.2 = (f32[1,32,16,512]{3,2,1,0:T(8,128)}, f32[1,32,16,512]{3,2,1,0:T(8,128)S(1)}, u32[]{:S(2)}, u32[]{:S(2)}) collective-permute-start(f32[1,32,16,512]{3,2,1,0:T(8,128)} %slice.192), channel_id=1, source_target_pairs={{8,0},{16,8},{24,16},{9,1},{17,9},{25,17},{10,2},{18,10},{26,18},{... | collective-permute-start | bytes 3145736 | tf_op jit(solution)/shard_map/ppermute | solution.py:13
  348.0 36.3 %collective-permute-start.3 = (f32[1,32,16,512]{3,2,1,0:T(8,128)}, f32[1,32,16,512]{3,2,1,0:T(8,128)S(1)}, u32[]{:S(2)}, u32[]{:S(2)}) collective-permute-start(f32[1,32,16,512]{3,2,1,0:T(8,128)} %slice.250), channel_id=1, source_target_pairs={{0,8},{8,16},{16,24},{1,9},{9,17},{17,25},{2,10},{10,18},{18,26},{... | collective-permute-start | bytes 3145736 | tf_op jit(solution)/shard_map/ppermute | solution.py:13
  442.7 18.9 %all-to-all-start.4 = ((f32[8,4,32,128]{3,2,1,0:T(8,128)}), f32[8,4,32,128]{3,2,1,0:T(8,128)S(1)}, u32[]{:S(2)}, u32[]{:S(2)}) async-start(f32[8,4,32,128]{3,2,1,0:T(8,128)} %reshape.363), calls=%async_computation.4 | async-start | bytes 1048576 | tf_op jit(solution)/shard_map/all_to_all | solution.py:190
  470.5 30.1 %all-to-all-start.5 = ((f32[8,4,32,256]{3,2,1,0:T(8,128)}), f32[8,4,32,256]{3,2,1,0:T(8,128)S(1)}, u32[]{:S(2)}, u32[]{:S(2)}) async-start(f32[8,4,32,256]{3,2,1,0:T(8,128)} %reshape.368), calls=%async_computation.5 | async-start | bytes 2097152 | tf_op jit(solution)/shard_map/all_to_all | solution.py:190
  502.6 19.6 %collective-permute-start.12 = (f32[4,64,256]{2,1,0:T(8,128)}, f32[4,64,256]{2,1,0:T(8,128)}, u32[]{:S(2)}, u32[]{:S(2)}) collective-permute-start(f32[4,64,256]{2,1,0:T(8,128)} %get-tuple-element.60), channel_id=1, source_target_pairs={{0,24},{8,0},{16,8},{24,16},{1,25},{9,1},{17,9},{25,17},{2,26},{10... | collective-permute-start | bytes 786440 | tf_op jit(solution)/shard_map/ppermute | solution.py:150
  505.1 17.5 %collective-permute-start.11 = (f32[4,64,256]{2,1,0:T(8,128)}, f32[4,64,256]{2,1,0:T(8,128)}, u32[]{:S(2)}, u32[]{:S(2)}) collective-permute-start(f32[4,64,256]{2,1,0:T(8,128)} %get-tuple-element.61), channel_id=1, source_target_pairs={{0,16},{8,24},{16,0},{24,8},{1,17},{9,25},{17,1},{25,9},{2,18},{10... | collective-permute-start | bytes 786440 | tf_op jit(solution)/shard_map/ppermute | solution.py:150
  505.6 17.0 %collective-permute-start.10 = (f32[4,64,256]{2,1,0:T(8,128)}, f32[4,64,256]{2,1,0:T(8,128)}, u32[]{:S(2)}, u32[]{:S(2)}) collective-permute-start(f32[4,64,256]{2,1,0:T(8,128)} %get-tuple-element.62), channel_id=1, source_target_pairs={{0,8},{8,16},{16,24},{24,0},{1,9},{9,17},{17,25},{25,1},{2,10},{10... | collective-permute-start | bytes 786440 | tf_op jit(solution)/shard_map/ppermute | solution.py:150
  507.1 24.2 %collective-permute-start.7 = (f32[4,64,128]{2,1,0:T(8,128)S(1)}, f32[4,64,128]{2,1,0:T(8,128)}, u32[]{:S(2)}, u32[]{:S(2)}) collective-permute-start(f32[4,64,128]{2,1,0:T(8,128)S(1)} %bitcast.387), channel_id=1, source_target_pairs={{0,24},{8,0},{16,8},{24,16},{1,25},{9,1},{17,9},{25,17},{2,26},{10... | collective-permute-start | bytes 393224 | tf_op jit(solution)/shard_map/ppermute | solution.py:150
  509.5 21.9 %collective-permute-start.8 = (f32[4,64,128]{2,1,0:T(8,128)S(1)}, f32[4,64,128]{2,1,0:T(8,128)}, u32[]{:S(2)}, u32[]{:S(2)}) collective-permute-start(f32[4,64,128]{2,1,0:T(8,128)S(1)} %bitcast.386), channel_id=1, source_target_pairs={{0,16},{8,24},{16,0},{24,8},{1,17},{9,25},{17,1},{25,9},{2,18},{10... | collective-permute-start | bytes 393224 | tf_op jit(solution)/shard_map/ppermute | solution.py:150
  518.7 30.1 %all-to-all-start.6 = ((f32[8,4,32,256]{3,2,1,0:T(8,128)}), f32[8,4,32,256]{3,2,1,0:T(8,128)S(1)}, u32[]{:S(2)}, u32[]{:S(2)}) async-start(f32[8,4,32,256]{3,2,1,0:T(8,128)} %reshape.373), calls=%async_computation.6 | async-start | bytes 2097152 | tf_op jit(solution)/shard_map/all_to_all | solution.py:190
  550.9 14.5 %collective-permute-start.18 = (f32[4,64,256]{2,1,0:T(8,128)}, f32[4,64,256]{2,1,0:T(8,128)}, u32[]{:S(2)}, u32[]{:S(2)}) collective-permute-start(f32[4,64,256]{2,1,0:T(8,128)} %get-tuple-element.48), channel_id=1, source_target_pairs={{0,24},{8,0},{16,8},{24,16},{1,25},{9,1},{17,9},{25,17},{2,26},{10... | collective-permute-start | bytes 786440 | tf_op jit(solution)/shard_map/ppermute | solution.py:150
  550.9 14.5 %collective-permute-start.17 = (f32[4,64,256]{2,1,0:T(8,128)}, f32[4,64,256]{2,1,0:T(8,128)}, u32[]{:S(2)}, u32[]{:S(2)}) collective-permute-start(f32[4,64,256]{2,1,0:T(8,128)} %get-tuple-element.49), channel_id=1, source_target_pairs={{0,16},{8,24},{16,0},{24,8},{1,17},{9,25},{17,1},{25,9},{2,18},{10... | collective-permute-start | bytes 786440 | tf_op jit(solution)/shard_map/ppermute | solution.py:150
  551.4 14.0 %collective-permute-start.16 = (f32[4,64,256]{2,1,0:T(8,128)S(1)}, f32[4,64,256]{2,1,0:T(8,128)}, u32[]{:S(2)}, u32[]{:S(2)}) collective-permute-start(f32[4,64,256]{2,1,0:T(8,128)S(1)} %get-tuple-element.50), channel_id=1, source_target_pairs={{0,8},{8,16},{16,24},{24,0},{1,9},{9,17},{17,25},{25,1},{2,10},{10... | collective-permute-start | bytes 786440 | tf_op jit(solution)/shard_map/ppermute | solution.py:150
  561.8 30.1 %all-to-all-start.7 = ((f32[8,4,32,256]{3,2,1,0:T(8,128)}), f32[8,4,32,256]{3,2,1,0:T(8,128)S(1)}, u32[]{:S(2)}, u32[]{:S(2)}) async-start(f32[8,4,32,256]{3,2,1,0:T(8,128)} %reshape.378), calls=%async_computation.7 | async-start | bytes 2097152 | tf_op jit(solution)/shard_map/all_to_all | solution.py:190
  569.2 27.3 %collective-permute-start.19 = (f32[4,64,256]{2,1,0:T(8,128)}, f32[4,64,256]{2,1,0:T(8,128)S(1)}, u32[]{:S(2)}, u32[]{:S(2)}) collective-permute-start(f32[4,64,256]{2,1,0:T(8,128)} %bitcast.324), channel_id=1, source_target_pairs={{0,24},{8,0},{16,8},{24,16},{1,25},{9,1},{17,9},{25,17},{2,26},{10... | collective-permute-start | bytes 786440 | tf_op jit(solution)/shard_map/ppermute | solution.py:150
  570.2 27.6 %collective-permute-start.20 = (f32[4,64,256]{2,1,0:T(8,128)S(1)}, f32[4,64,256]{2,1,0:T(8,128)S(1)}, u32[]{:S(2)}, u32[]{:S(2)}) collective-permute-start(f32[4,64,256]{2,1,0:T(8,128)S(1)} %bitcast.385), channel_id=1, source_target_pairs={{0,16},{8,24},{16,0},{24,8},{1,17},{9,25},{17,1},{25,9},{2,18},{10... | collective-permute-start | bytes 786440 | tf_op jit(solution)/shard_map/ppermute | solution.py:150
  572.5 25.3 %collective-permute-start.21 = (f32[4,64,256]{2,1,0:T(8,128)}, f32[4,64,256]{2,1,0:T(8,128)S(1)}, u32[]{:S(2)}, u32[]{:S(2)}) collective-permute-start(f32[4,64,256]{2,1,0:T(8,128)} %bitcast.322), channel_id=1, source_target_pairs={{0,8},{8,16},{16,24},{24,0},{1,9},{9,17},{17,25},{25,1},{2,10},{10... | collective-permute-start | bytes 786440 | tf_op jit(solution)/shard_map/ppermute | solution.py:150
  601.3 29.6 %all-to-all-start.8 = ((f32[8,4,32,128]{3,2,1,0:T(8,128)}), f32[8,4,32,128]{3,2,1,0:T(8,128)S(1)}, u32[]{:S(2)}, u32[]{:S(2)}) async-start(f32[8,4,32,128]{3,2,1,0:T(8,128)} %reshape.383), calls=%async_computation.8 | async-start | bytes 1048576 | tf_op jit(solution)/shard_map/all_to_all | solution.py:190
  (50 other events, 566.3 us)

commit v11 on v10

--- a/solution.py
+++ b/solution.py
@@ -143,6 +143,14 @@
     k_cols = (lax.rem(hel_index - turn + nh, nh)[:, None] * kl + jnp.arange(kl)[None, :]).reshape(-1)
     j_rows = (lax.rem(hel_index + turn, nh)[:, None] * kl + jnp.arange(kl)[None, :]).reshape(-1)
     frame_turned = frame_rotation[j_rows][:, k_cols]
+    rad_turn = jnp.arange(n, dtype=jnp.int32)
+    r_cols = (lax.rem(rad_index - rad_turn + n, n)[:, None] * rl + jnp.arange(rl)[None, :]).reshape(-1)
+    interp_turned = interp_turned[:, :, r_cols]
+
+    def rad_shift(x, d):
+        if d == 0:
+            return x
+        return lax.ppermute(x, "rad", [(i, (i + d) % n) for i in range(n)])
 
     def hel_shift(x, d):
         if d == 0:
@@ -187,10 +195,12 @@
             pending, part = lax.optimization_barrier((pending, part))
             finish(pending)
         chans = jnp.transpose(part.reshape(kl, rl, vs, n, cb), (3, 0, 1, 2, 4))
-        got = lax.all_to_all(chans.reshape(n, kl, rl, width), "rad", 0, 0, tiled=True)
-        radial_block = jnp.transpose(got.reshape(n, kl, rl, width), (1, 0, 2, 3)).reshape(
-            kl, radial, width
-        )
+        chans = chans.reshape(n, kl, rl, width)
+        rolled = lax.dynamic_slice_in_dim(
+            jnp.concatenate([chans, chans], axis=0), rad_index, n, axis=0
+        )
+        got = jnp.stack([rad_shift(rolled[d], d) for d in range(n)], axis=0)
+        radial_block = jnp.transpose(got, (1, 0, 2, 3)).reshape(kl, radial, width)
         placed = jnp.einsum(
             "kqr,krm->kqm",
             interp_turned,

time: 657 us -> 703 us (1.070)
  starting transfers between devices: 85 us -> 118 us
  local copies, waits for them, and re-layouts: 154 us -> 164 us
    ppermute x0 -> x35, waiting for transfers between devices: none -> 77.5 us  [rad_shift(): return lax.ppermute(x, 'rad', [(i, (i + d) % n) for i in range(n)])]
    all_to_all x5 -> x0, waiting for transfers between devices: 45.1 us -> none  [shards(): lax.all_to_all(chans.reshape(n, kl, rl, width), 'rad', 0, 0, tiled=True)]
    ppermute x0 -> x35, starting transfers between devices: none -> 41.1 us  [rad_shift(): return lax.ppermute(x, 'rad', [(i, (i + d) % n) for i in range(n)])]
    ppermute x30, waiting for transfers between devices: 38.1 us -> 13.9 us  [hel_shift(): return lax.ppermute(x, 'hel', [(i, (i + d) % nh) for i in range(nh)])]
    all_to_all x5 -> x0, starting transfers between devices: 17.8 us -> none  [shards(): lax.all_to_all(chans.reshape(n, kl, rl, width), 'rad', 0, 0, tiled=True)]
    ppermute x30, starting transfers between devices: 34.4 us -> 42.9 us  [hel_shift(): return lax.ppermute(x, 'hel', [(i, (i + d) % nh) for i in range(nh)])]
    unnamed x82 -> x120, local copies, waits for them, and re-layouts: 18.5 us -> 21.3 us
  transfers between devices with their start and end apart: 43 -> 73, of which waited for: 20 -> 29; matrix products, arithmetic and copies ran while one was open for 29% -> 30% of each run, Pallas kernels for 0% -> 0%
where the time goes in v11:
time: 703 us; the launch traced here: 697 us
  waiting for transfers between devices  310 us (44%)
  local copies, waits for them, and re-layouts  164 us (23%)
  starting transfers between devices  118 us (17%)
  matrix products  79.1 us (11%)
  other arithmetic  23.1 us (3%)
    all_to_all x2, waiting for transfers between devices, to_radial_columns(): got = lax.all_to_all(blocks, 'rad', 0, 0, tiled=True).reshape(n, kl, rl, mb)  115 us
    all_to_all x2, waiting for transfers between devices, to_radial_rows(): got = lax.all_to_all(blocks, 'rad', 0, 0, tiled=True).reshape(n, kl, rl, mb)  105 us
    ppermute x35, waiting for transfers between devices, rad_shift(): return lax.ppermute(x, 'rad', [(i, (i + d) % n) for i in range(n)])  77.5 us
    ppermute x30, starting transfers between devices, hel_shift(): return lax.ppermute(x, 'hel', [(i, (i + d) % nh) for i in range(nh)])  42.9 us
    ppermute x35, starting transfers between devices, rad_shift(): return lax.ppermute(x, 'rad', [(i, (i + d) % n) for i in range(n)])  41.1 us
    dot_general x2, matrix products, local_part(): jnp.dot(current.reshape(-1, cc), transform.T, precision=PRECISE, preferre...  25 us
    dot_general x2, matrix products, local_part(): jnp.dot(angles.reshape(-1, angles.shape[3]), transform, precision=PRECISE...  22.2 us
    unnamed x120, local copies, waits for them, and re-layouts  21.3 us
  transfers between devices with their start and end apart: 73, of which 29 were waited for; matrix products, arithmetic and copies ran while one was open for 30% of the time, Pallas kernels for 0%

profile of v11, /device:TPU:0, one launch (start us, length us, event | category | flops | bytes accessed | tf_op | source)
XLA Modules:
  0.0 697.1 jit_solution(12362849793055505585)
XLA Ops:
  5.9 6.6 copy.163
  12.6 6.5 all-to-all-start
  36.7 16.4 %convolution_bitcast_fusion = f32[2048,512]{0,1:T(8,128)} fusion(f32[512,512]{1,0:T(8,128)S(1)} %convolution_multiply_fusion, f32[2048,512]{1,0:T(8,128)} %bitcast.481), kind=kOutput, calls=%fused_computation.24 | convolution fusion | flops 6442450944 | bytes 9437184 | tf_op jit(solution)/shard_map/dot_general | solution.py:93
  58.5 5.7 fusion.36
  64.3 11.6 %fusion.5 = f32[4,32,16,512]{3,2,1,0:T(8,128)} fusion(f32[1,32,16,512]{3,2,1,0:T(8,128)S(1)} %collective-permute-done, f32[3,32,16,512]{3,2,1,0:T(8,128)} %slice.305, f32[3,32,16,512]{3,2,1,0:T(8,128)S(1)} %slice-done.1, f32[1,32,16,512]{3,2,1,0:T(8,128)S(1)} %collective-permute-done.1, f32[4,32,16,512]{3,2,1,0:T(8,128)} %param.15, ...), kind=kOutput, calls=%fused_computation.10 | convolution fusion | flops 6456082432 | bytes 26288448 | tf_op jit(solution)/shard_map/dot_general | solution.py:105
  81.1 6.6 copy.276
  87.7 25.4 %all-to-all-done = f32[8,4,32,1024]{3,2,1,0:T(8,128)} async-done(((f32[8,4,32,1024]{3,2,1,0:T(8,128)}), f32[8,4,32,1024]{3,2,1,0:T(8,128)}, u32[]{:S(2)}, u32[]{:S(2)}) %all-to-all-start) | async-done | bytes 4194336 | tf_op jit(solution)/shard_map/all_to_all | solution.py:73
  123.1 89.2 %all-to-all-done.1 = f32[8,4,32,1024]{3,2,1,0:T(8,128)} async-done(((f32[8,4,32,1024]{3,2,1,0:T(8,128)}), f32[8,4,32,1024]{3,2,1,0:T(8,128)}, u32[]{:S(2)}, u32[]{:S(2)}) %all-to-all-start.1) | async-done | bytes 4194336 | tf_op jit(solution)/shard_map/all_to_all | solution.py:73
  227.6 5.6 fusion.38
  235.8 85.7 %all-to-all-done.2 = f32[8,4,32,1024]{3,2,1,0:T(8,128)} async-done(((f32[8,4,32,1024]{3,2,1,0:T(8,128)}), f32[8,4,32,1024]{3,2,1,0:T(8,128)}, u32[]{:S(2)}, u32[]{:S(2)}) %all-to-all-start.2) | async-done | bytes 4194336 | tf_op jit(solution)/shard_map/all_to_all | solution.py:78
  328.7 6.6 copy.169
  349.5 5.5 collective-permute-start.3
  378.1 8.6 %fusion.24 = f32[128,16,512]{2,1,0:T(8,128)S(1)} fusion(f32[128,16,512]{2,1,0:T(8,128)} %dot_general.78, f32[512,512]{1,0:T(8,128)S(1)} %convolution_multiply_fusion), kind=kOutput, calls=%fused_computation.54 | convolution fusion | flops 6442450944 | bytes 9437184 | tf_op jit(solution)/shard_map/dot_general | solution.py:93
  390.9 10.6 %fusion.8 = f32[4,32,16,512]{3,2,1,0:T(8,128)} fusion(f32[1,32,16,512]{3,2,1,0:T(8,128)} %collective-permute-done.2, f32[3,32,16,512]{3,2,1,0:T(8,128)S(1)} %copy-done.10, f32[3,32,16,512]{3,2,1,0:T(8,128)S(1)} %slice-done, f32[1,32,16,512]{3,2,1,0:T(8,128)} %collective-permute-done.3, f32[4,32,16,512]{3,2,1,0:T(8,128)S(1)} %copy-done.4, ...), kind=kOutput, calls=%fused_computation.14 | convolution fusion | flops 6451888128 | bytes 22094016 | tf_op jit(solution)/shard_map/dot_general | solution.py:105
  401.5 18.8 %all-to-all-done.3 = f32[8,4,32,1024]{3,2,1,0:T(8,128)} async-done(((f32[8,4,32,1024]{3,2,1,0:T(8,128)}), f32[8,4,32,1024]{3,2,1,0:T(8,128)}, u32[]{:S(2)}, u32[]{:S(2)}) %all-to-all-start.3) | async-done | bytes 4194336 | tf_op jit(solution)/shard_map/all_to_all | solution.py:78
  420.3 6.6 copy.174
  431.8 6.3 subtract_multiply_fusion
  443.8 5.8 fusion.93
  509.6 7.2 %collective-permute-done.30 = f32[4,32,256]{2,1,0:T(8,128)S(1)} collective-permute-done((f32[4,32,256]{2,1,0:T(8,128)S(1)}, f32[4,32,256]{2,1,0:T(8,128)S(1)}, u32[]{:S(2)}, u32[]{:S(2)}) %collective-permute-start.30) | collective-permute-done | bytes 131104 | tf_op jit(solution)/shard_map/ppermute | solution.py:153
  516.8 6.7 collective-permute-done.31
  529.0 7.2 %collective-permute-done.33 = f32[4,32,256]{2,1,0:T(8,128)S(1)} collective-permute-done((f32[4,32,256]{2,1,0:T(8,128)S(1)}, f32[4,32,256]{2,1,0:T(8,128)S(1)}, u32[]{:S(2)}, u32[]{:S(2)}) %collective-permute-start.33) | collective-permute-done | bytes 131104 | tf_op jit(solution)/shard_map/ppermute | solution.py:153
  579.0 6.4 collective-permute-start.47
  606.9 6.1 collective-permute-done.57
  645.8 6.1 collective-permute-done.64
  (391 shorter events, 326.7 us)
Async XLA Ops:
  12.6 100.6 %all-to-all-start = ((f32[8,4,32,1024]{3,2,1,0:T(8,128)}), f32[8,4,32,1024]{3,2,1,0:T(8,128)}, u32[]{:S(2)}, u32[]{:S(2)}) async-start(f32[8,4,32,1024]{3,2,1,0:T(8,128)} %copy.163), calls=%async_computation | async-start | bytes 8388608 | tf_op jit(solution)/shard_map/all_to_all | solution.py:73
  21.4 42.8 %collective-permute-start = (f32[1,32,16,512]{3,2,1,0:T(8,128)}, f32[1,32,16,512]{3,2,1,0:T(8,128)S(1)}, u32[]{:S(2)}, u32[]{:S(2)}) collective-permute-start(f32[1,32,16,512]{3,2,1,0:T(8,128)} %slice.306), channel_id=1, source_target_pairs={{8,0},{16,8},{24,16},{9,1},{17,9},{25,17},{10,2},{18,10},{26,18},{... | collective-permute-start | bytes 3145736 | tf_op jit(solution)/shard_map/ppermute | solution.py:13
  26.8 37.4 %collective-permute-start.1 = (f32[1,32,16,512]{3,2,1,0:T(8,128)}, f32[1,32,16,512]{3,2,1,0:T(8,128)S(1)}, u32[]{:S(2)}, u32[]{:S(2)}) collective-permute-start(f32[1,32,16,512]{3,2,1,0:T(8,128)} %slice.408), channel_id=1, source_target_pairs={{0,8},{8,16},{16,24},{1,9},{9,17},{17,25},{2,10},{10,18},{18,26},{... | collective-permute-start | bytes 3145736 | tf_op jit(solution)/shard_map/ppermute | solution.py:13
  113.1 99.1 %all-to-all-start.1 = ((f32[8,4,32,1024]{3,2,1,0:T(8,128)}), f32[8,4,32,1024]{3,2,1,0:T(8,128)}, u32[]{:S(2)}, u32[]{:S(2)}) async-start(f32[8,4,32,1024]{3,2,1,0:T(8,128)} %bitcast.487), calls=%async_computation.1 | async-start | bytes 8388608 | tf_op jit(solution)/shard_map/all_to_all | solution.py:73
  223.0 98.6 %all-to-all-start.2 = ((f32[8,4,32,1024]{3,2,1,0:T(8,128)}), f32[8,4,32,1024]{3,2,1,0:T(8,128)}, u32[]{:S(2)}, u32[]{:S(2)}) async-start(f32[8,4,32,1024]{3,2,1,0:T(8,128)} %bitcast.488), calls=%async_computation.2 | async-start | bytes 8388608 | tf_op jit(solution)/shard_map/all_to_all | solution.py:78
  321.6 98.7 %all-to-all-start.3 = ((f32[8,4,32,1024]{3,2,1,0:T(8,128)}), f32[8,4,32,1024]{3,2,1,0:T(8,128)}, u32[]{:S(2)}, u32[]{:S(2)}) async-start(f32[8,4,32,1024]{3,2,1,0:T(8,128)} %bitcast.486), calls=%async_computation.3 | async-start | bytes 8388608 | tf_op jit(solution)/shard_map/all_to_all | solution.py:78
  337.1 53.7 %collective-permute-start.2 = (f32[1,32,16,512]{3,2,1,0:T(8,128)}, f32[1,32,16,512]{3,2,1,0:T(8,128)}, u32[]{:S(2)}, u32[]{:S(2)}) collective-permute-start(f32[1,32,16,512]{3,2,1,0:T(8,128)} %slice.312), channel_id=1, source_target_pairs={{8,0},{16,8},{24,16},{9,1},{17,9},{25,17},{10,2},{18,10},{26,18},{... | collective-permute-start | bytes 3145736 | tf_op jit(solution)/shard_map/ppermute | solution.py:13
  349.5 41.3 %collective-permute-start.3 = (f32[1,32,16,512]{3,2,1,0:T(8,128)}, f32[1,32,16,512]{3,2,1,0:T(8,128)}, u32[]{:S(2)}, u32[]{:S(2)}) collective-permute-start(f32[1,32,16,512]{3,2,1,0:T(8,128)} %slice.412), channel_id=1, source_target_pairs={{0,8},{8,16},{16,24},{1,9},{9,17},{17,25},{2,10},{10,18},{18,26},{... | collective-permute-start | bytes 3145736 | tf_op jit(solution)/shard_map/ppermute | solution.py:13
  477.7 16.4 %collective-permute-start.20 = (f32[4,32,256]{2,1,0:T(8,128)S(1)}, f32[4,32,256]{2,1,0:T(8,128)S(1)}, u32[]{:S(2)}, u32[]{:S(2)}) collective-permute-start(f32[4,32,256]{2,1,0:T(8,128)S(1)} %get-tuple-element.82), channel_id=1, source_target_pairs={{0,4},{1,5},{2,6},{3,7},{4,0},{5,1},{6,2},{7,3},{8,12},{9,13},{10,... | collective-permute-start | bytes 393224 | tf_op jit(solution)/shard_map/ppermute | solution.py:153
  491.8 56.6 %collective-permute-start.14 = (f32[4,64,128]{2,1,0:T(8,128)}, f32[4,64,128]{2,1,0:T(8,128)}, u32[]{:S(2)}, u32[]{:S(2)}) collective-permute-start(f32[4,64,128]{2,1,0:T(8,128)} %bitcast.480), channel_id=1, source_target_pairs={{0,24},{8,0},{16,8},{24,16},{1,25},{9,1},{17,9},{25,17},{2,26},{10... | collective-permute-start | bytes 393224 | tf_op jit(solution)/shard_map/ppermute | solution.py:158
  494.1 55.2 %collective-permute-start.15 = (f32[4,64,128]{2,1,0:T(8,128)}, f32[4,64,128]{2,1,0:T(8,128)}, u32[]{:S(2)}, u32[]{:S(2)}) collective-permute-start(f32[4,64,128]{2,1,0:T(8,128)} %bitcast.479), channel_id=1, source_target_pairs={{0,16},{8,24},{16,0},{24,8},{1,17},{9,25},{17,1},{25,9},{2,18},{10... | collective-permute-start | bytes 393224 | tf_op jit(solution)/shard_map/ppermute | solution.py:158
  495.7 53.6 %collective-permute-start.16 = (f32[4,64,128]{2,1,0:T(8,128)}, f32[4,64,128]{2,1,0:T(8,128)}, u32[]{:S(2)}, u32[]{:S(2)}) collective-permute-start(f32[4,64,128]{2,1,0:T(8,128)} %bitcast.478), channel_id=1, source_target_pairs={{0,8},{8,16},{16,24},{24,0},{1,9},{9,17},{17,25},{25,1},{2,10},{10... | collective-permute-start | bytes 393224 | tf_op jit(solution)/shard_map/ppermute | solution.py:158
  507.4 58.5 %collective-permute-start.26 = (f32[4,64,256]{2,1,0:T(8,128)}, f32[4,64,256]{2,1,0:T(8,128)}, u32[]{:S(2)}, u32[]{:S(2)}) collective-permute-start(f32[4,64,256]{2,1,0:T(8,128)} %get-tuple-element.76), channel_id=1, source_target_pairs={{0,24},{8,0},{16,8},{24,16},{1,25},{9,1},{17,9},{25,17},{2,26},{10... | collective-permute-start | bytes 786440 | tf_op jit(solution)/shard_map/ppermute | solution.py:158
  547.4 18.6 %collective-permute-start.25 = (f32[4,64,256]{2,1,0:T(8,128)}, f32[4,64,256]{2,1,0:T(8,128)}, u32[]{:S(2)}, u32[]{:S(2)}) collective-permute-start(f32[4,64,256]{2,1,0:T(8,128)} %get-tuple-element.77), channel_id=1, source_target_pairs={{0,16},{8,24},{16,0},{24,8},{1,17},{9,25},{17,1},{25,9},{2,18},{10... | collective-permute-start | bytes 786440 | tf_op jit(solution)/shard_map/ppermute | solution.py:158
  548.4 18.7 %collective-permute-start.24 = (f32[4,64,256]{2,1,0:T(8,128)}, f32[4,64,256]{2,1,0:T(8,128)}, u32[]{:S(2)}, u32[]{:S(2)}) collective-permute-start(f32[4,64,256]{2,1,0:T(8,128)} %get-tuple-element.78), channel_id=1, source_target_pairs={{0,8},{8,16},{16,24},{24,0},{1,9},{9,17},{17,25},{25,1},{2,10},{10... | collective-permute-start | bytes 786440 | tf_op jit(solution)/shard_map/ppermute | solution.py:158
  556.3 79.4 %collective-permute-start.39 = (f32[4,64,256]{2,1,0:T(8,128)}, f32[4,64,256]{2,1,0:T(8,128)}, u32[]{:S(2)}, u32[]{:S(2)}) collective-permute-start(f32[4,64,256]{2,1,0:T(8,128)} %get-tuple-element.56), channel_id=1, source_target_pairs={{0,24},{8,0},{16,8},{24,16},{1,25},{9,1},{17,9},{25,17},{2,26},{10... | collective-permute-start | bytes 786440 | tf_op jit(solution)/shard_map/ppermute | solution.py:158
  558.3 78.7 %collective-permute-start.38 = (f32[4,64,256]{2,1,0:T(8,128)}, f32[4,64,256]{2,1,0:T(8,128)}, u32[]{:S(2)}, u32[]{:S(2)}) collective-permute-start(f32[4,64,256]{2,1,0:T(8,128)} %get-tuple-element.57), channel_id=1, source_target_pairs={{0,16},{8,24},{16,0},{24,8},{1,17},{9,25},{17,1},{25,9},{2,18},{10... | collective-permute-start | bytes 786440 | tf_op jit(solution)/shard_map/ppermute | solution.py:158
  565.9 72.2 %collective-permute-start.37 = (f32[4,64,256]{2,1,0:T(8,128)}, f32[4,64,256]{2,1,0:T(8,128)}, u32[]{:S(2)}, u32[]{:S(2)}) collective-permute-start(f32[4,64,256]{2,1,0:T(8,128)} %get-tuple-element.58), channel_id=1, source_target_pairs={{0,8},{8,16},{16,24},{24,0},{1,9},{9,17},{17,25},{25,1},{2,10},{10... | collective-permute-start | bytes 786440 | tf_op jit(solution)/shard_map/ppermute | solution.py:158
  592.4 64.2 %collective-permute-start.27 = (f32[4,64,256]{2,1,0:T(8,128)}, f32[4,64,256]{2,1,0:T(8,128)}, u32[]{:S(2)}, u32[]{:S(2)}) collective-permute-start(f32[4,64,256]{2,1,0:T(8,128)} %bitcast.474), channel_id=1, source_target_pairs={{0,24},{8,0},{16,8},{24,16},{1,25},{9,1},{17,9},{25,17},{2,26},{10... | collective-permute-start | bytes 786440 | tf_op jit(solution)/shard_map/ppermute | solution.py:158
  633.4 25.2 %collective-permute-start.28 = (f32[4,64,256]{2,1,0:T(8,128)S(1)}, f32[4,64,256]{2,1,0:T(8,128)S(1)}, u32[]{:S(2)}, u32[]{:S(2)}) collective-permute-start(f32[4,64,256]{2,1,0:T(8,128)S(1)} %bitcast.535), channel_id=1, source_target_pairs={{0,16},{8,24},{16,0},{24,8},{1,17},{9,25},{17,1},{25,9},{2,18},{10... | collective-permute-start | bytes 786440 | tf_op jit(solution)/shard_map/ppermute | solution.py:158
  658.7 26.3 %collective-permute-start.40 = (f32[4,64,256]{2,1,0:T(8,128)}, f32[4,64,256]{2,1,0:T(8,128)}, u32[]{:S(2)}, u32[]{:S(2)}) collective-permute-start(f32[4,64,256]{2,1,0:T(8,128)} %bitcast.471), channel_id=1, source_target_pairs={{0,24},{8,0},{16,8},{24,16},{1,25},{9,1},{17,9},{25,17},{2,26},{10... | collective-permute-start | bytes 786440 | tf_op jit(solution)/shard_map/ppermute | solution.py:158
  659.8 25.3 %collective-permute-start.41 = (f32[4,64,256]{2,1,0:T(8,128)}, f32[4,64,256]{2,1,0:T(8,128)}, u32[]{:S(2)}, u32[]{:S(2)}) collective-permute-start(f32[4,64,256]{2,1,0:T(8,128)} %bitcast.470), channel_id=1, source_target_pairs={{0,16},{8,24},{16,0},{24,8},{1,17},{9,25},{17,1},{25,9},{2,18},{10... | collective-permute-start | bytes 786440 | tf_op jit(solution)/shard_map/ppermute | solution.py:158
  662.0 18.2 %collective-permute-start.66 = (f32[4,64,128]{2,1,0:T(8,128)}, f32[4,64,128]{2,1,0:T(8,128)S(1)}, u32[]{:S(2)}, u32[]{:S(2)}) collective-permute-start(f32[4,64,128]{2,1,0:T(8,128)} %bitcast.477), channel_id=1, source_target_pairs={{0,24},{8,0},{16,8},{24,16},{1,25},{9,1},{17,9},{25,17},{2,26},{10... | collective-permute-start | bytes 393224 | tf_op jit(solution)/shard_map/ppermute | solution.py:158
  664.0 16.2 %collective-permute-start.67 = (f32[4,64,128]{2,1,0:T(8,128)}, f32[4,64,128]{2,1,0:T(8,128)S(1)}, u32[]{:S(2)}, u32[]{:S(2)}) collective-permute-start(f32[4,64,128]{2,1,0:T(8,128)} %bitcast.476), channel_id=1, source_target_pairs={{0,16},{8,24},{16,0},{24,8},{1,17},{9,25},{17,1},{25,9},{2,18},{10... | collective-permute-start | bytes 393224 | tf_op jit(solution)/shard_map/ppermute | solution.py:158
  (84 other events, 867.5 us)

commit v12 on v10

--- a/solution.py
+++ b/solution.py
@@ -156,17 +156,19 @@
     bounds = [sum(sizes[:i]) for i in range(len(sizes) + 1)]
     results = []
 
-    def finish(placed):
-        vs = placed.shape[2] // cb
-        width = vs * cb
+    def forward(placed):
+        width = placed.shape[2]
         arrived = [hel_shift(placed[:, d * qb:(d + 1) * qb], d) for d in range(nh)]
         gathered = jnp.stack(arrived, axis=0)
-        turned = jnp.dot(
+        return jnp.dot(
             frame_turned,
             gathered.reshape(nh * kl, qb * width),
             precision=PRECISE,
             preferred_element_type=jnp.float32,
         ).reshape(nh, kl, qb, width)
+
+    def backward(turned):
+        vs = turned.shape[3] // cb
         back = [hel_shift(turned[e], e) for e in range(nh)]
         blocks = []
         for block in range(nh):
@@ -179,27 +181,33 @@
         results.append(rotated.reshape(kl, qq, vs, cb))
 
     pending = None
+    turning = None
     for lo, hi in zip(bounds[:-1], bounds[1:]):
         part = current[:, :, lo:hi, :]
         vs = hi - lo
         width = vs * cb
         if pending is not None:
-            pending, part = lax.optimization_barrier((pending, part))
-            finish(pending)
+            if turning is not None:
+                pending, turning, part = lax.optimization_barrier((pending, turning, part))
+                backward(turning)
+            else:
+                pending, part = lax.optimization_barrier((pending, part))
+            turning = forward(pending)
         chans = jnp.transpose(part.reshape(kl, rl, vs, n, cb), (3, 0, 1, 2, 4))
         got = lax.all_to_all(chans.reshape(n, kl, rl, width), "rad", 0, 0, tiled=True)
         radial_block = jnp.transpose(got.reshape(n, kl, rl, width), (1, 0, 2, 3)).reshape(
             kl, radial, width
         )
-        placed = jnp.einsum(
+        pending = jnp.einsum(
             "kqr,krm->kqm",
             interp_turned,
             radial_block,
             precision=PRECISE,
             preferred_element_type=jnp.float32,
         )
-        pending = placed
-    finish(pending)
+    if turning is not None:
+        backward(turning)
+    backward(forward(pending))
     product_amp = jnp.concatenate(results, axis=2)
     return (current, product_amp)
 

time: 657 us -> 658 us (level)
  waiting for transfers between devices: 310 us -> 299 us
    all_to_all x5, waiting for transfers between devices: 45.1 us -> 27.8 us  [shards(): lax.all_to_all(chans.reshape(n, kl, rl, width), 'rad', 0, 0, tiled=True)]
    ppermute x30, waiting for transfers between devices: 38.1 us -> 44.8 us  [hel_shift(): return lax.ppermute(x, 'hel', [(i, (i + d) % nh) for i in range(nh)])]
    unnamed x82 -> x59, local copies, waits for them, and re-layouts: 18.5 us -> 12.6 us
  transfers between devices with their start and end apart: 43 -> 43, of which waited for: 20 -> 23; matrix products, arithmetic and copies ran while one was open for 29% -> 29% of each run, Pallas kernels for 0% -> 0%
where the time goes in v12:
time: 658 us; the launch traced here: 652 us
  waiting for transfers between devices  299 us (45%)
  local copies, waits for them, and re-layouts  156 us (24%)
  starting transfers between devices  89.4 us (14%)
  matrix products  83.2 us (13%)
  other arithmetic  22.3 us (3%)
    all_to_all x2, waiting for transfers between devices, to_radial_columns(): got = lax.all_to_all(blocks, 'rad', 0, 0, tiled=True).reshape(n, kl, rl, mb)  115 us
    all_to_all x2, waiting for transfers between devices, to_radial_rows(): got = lax.all_to_all(blocks, 'rad', 0, 0, tiled=True).reshape(n, kl, rl, mb)  112 us
    ppermute x30, waiting for transfers between devices, hel_shift(): return lax.ppermute(x, 'hel', [(i, (i + d) % nh) for i in range(nh)])  44.8 us
    ppermute x30, starting transfers between devices, hel_shift(): return lax.ppermute(x, 'hel', [(i, (i + d) % nh) for i in range(nh)])  37.6 us
    all_to_all x5, waiting for transfers between devices, shards(): lax.all_to_all(chans.reshape(n, kl, rl, width), 'rad', 0, 0, tiled=True)  27.8 us
    dot_general x2, matrix products, local_part(): jnp.dot(current.reshape(-1, cc), transform.T, precision=PRECISE, preferre...  25 us
    dot_general x2, matrix products, local_part(): jnp.dot(angles.reshape(-1, angles.shape[3]), transform, precision=PRECISE...  21.5 us
    all_to_all x5, starting transfers between devices, shards(): lax.all_to_all(chans.reshape(n, kl, rl, width), 'rad', 0, 0, tiled=True)  19.1 us
  transfers between devices with their start and end apart: 43, of which 23 were waited for; matrix products, arithmetic and copies ran while one was open for 29% of the time, Pallas kernels for 0%

profile of v12, /device:TPU:0, one launch (start us, length us, event | category | flops | bytes accessed | tf_op | source)
XLA Modules:
  0.0 652.1 jit_solution(13090167250620876677)
XLA Ops:
  5.9 6.7 %copy.125 = f32[8,4,32,1024]{3,2,1,0:T(8,128)} copy(f32[8,4,32,1024]{3,0,2,1:T(8,128)} %bitcast.314) | data formatting | bytes 8388608 | tf_op jit(solution)/shard_map/transpose | solution.py:72
  12.6 6.5 all-to-all-start
  35.8 16.4 %convolution_bitcast_fusion = f32[2048,512]{0,1:T(8,128)} fusion(f32[512,512]{1,0:T(8,128)S(1)} %convolution_multiply_fusion, f32[2048,512]{1,0:T(8,128)} %bitcast.305), kind=kOutput, calls=%fused_computation.23 | convolution fusion | flops 6442450944 | bytes 9437184 | tf_op jit(solution)/shard_map/dot_general | solution.py:93
  52.2 5.4 copy.127
  57.6 5.7 fusion.44
  63.4 11.8 %fusion.5 = f32[4,32,16,512]{3,2,1,0:T(8,128)} fusion(f32[1,32,16,512]{3,2,1,0:T(8,128)S(1)} %collective-permute-done, f32[3,32,16,512]{3,2,1,0:T(8,128)} %slice.173, f32[3,32,16,512]{3,2,1,0:T(8,128)S(1)} %slice-done.1, f32[1,32,16,512]{3,2,1,0:T(8,128)S(1)} %collective-permute-done.1, f32[4,32,16,512]{3,2,1,0:T(8,128)} %param.15, ...), kind=kOutput, calls=%fused_computation.9 | convolution fusion | flops 6456082432 | bytes 26288448 | tf_op jit(solution)/shard_map/dot_general | solution.py:105
  80.4 6.6 %copy.202 = f32[4,32,8,1024]{3,1,0,2:T(8,128)} copy(f32[4,32,8,1024]{3,2,1,0:T(8,128)} %reshape.337) | data formatting | bytes 8388608 | tf_op jit(solution)/shard_map/reshape | solution.py:72
  87.0 26.1 %all-to-all-done = f32[8,4,32,1024]{3,2,1,0:T(8,128)} async-done(((f32[8,4,32,1024]{3,2,1,0:T(8,128)}), f32[8,4,32,1024]{3,2,1,0:T(8,128)}, u32[]{:S(2)}, u32[]{:S(2)}) %all-to-all-start) | async-done | bytes 4194336 | tf_op jit(solution)/shard_map/all_to_all | solution.py:73
  122.8 89.2 %all-to-all-done.1 = f32[8,4,32,1024]{3,2,1,0:T(8,128)} async-done(((f32[8,4,32,1024]{3,2,1,0:T(8,128)}), f32[8,4,32,1024]{3,2,1,0:T(8,128)}, u32[]{:S(2)}, u32[]{:S(2)}) %all-to-all-start.1) | async-done | bytes 4194336 | tf_op jit(solution)/shard_map/all_to_all | solution.py:73
  227.3 5.6 fusion.46
  235.5 85.7 %all-to-all-done.2 = f32[8,4,32,1024]{3,2,1,0:T(8,128)} async-done(((f32[8,4,32,1024]{3,2,1,0:T(8,128)}), f32[8,4,32,1024]{3,2,1,0:T(8,128)}, u32[]{:S(2)}, u32[]{:S(2)}) %all-to-all-start.2) | async-done | bytes 4194336 | tf_op jit(solution)/shard_map/all_to_all | solution.py:78
  327.2 6.6 %copy.131 = f32[4,32,8,1024]{3,2,1,0:T(8,128)} copy(f32[4,32,8,1024]{3,1,0,2:T(8,128)} %bitcast.15) | data formatting | bytes 8388608 | tf_op jit(solution)/shard_map/transpose | solution.py:81
  371.6 8.6 %fusion.25 = f32[128,16,512]{2,1,0:T(8,128)S(1)} fusion(f32[128,16,512]{2,1,0:T(8,128)} %dot_general.92, f32[512,512]{1,0:T(8,128)S(1)} %convolution_multiply_fusion), kind=kOutput, calls=%fused_computation.46 | convolution fusion | flops 6442450944 | bytes 9437184 | tf_op jit(solution)/shard_map/dot_general | solution.py:93
  384.4 9.7 %fusion.8 = f32[4,32,16,512]{3,2,1,0:T(8,128)} fusion(f32[1,32,16,512]{3,2,1,0:T(8,128)S(1)} %collective-permute-done.2, f32[3,32,16,512]{3,2,1,0:T(8,128)S(1)} %copy-done.10, f32[3,32,16,512]{3,2,1,0:T(8,128)S(1)} %slice-done, f32[1,32,16,512]{3,2,1,0:T(8,128)S(1)} %collective-permute-done.3, f32[4,32,16,512]{3,2,1,0:T(8,128)S(1)} %copy-done.4, ...), kind=kOutput, calls=%fused_computation.13 | convolution fusion | flops 6451888128 | bytes 22094016 | tf_op jit(solution)/shard_map/dot_general | solution.py:105
  394.1 25.8 %all-to-all-done.3 = f32[8,4,32,1024]{3,2,1,0:T(8,128)} async-done(((f32[8,4,32,1024]{3,2,1,0:T(8,128)}), f32[8,4,32,1024]{3,2,1,0:T(8,128)}, u32[]{:S(2)}, u32[]{:S(2)}) %all-to-all-start.3) | async-done | bytes 4194336 | tf_op jit(solution)/shard_map/all_to_all | solution.py:78
  419.8 6.6 %copy.136 = f32[4,32,8,1024]{3,2,1,0:T(8,128)} copy(f32[4,32,8,1024]{3,1,0,2:T(8,128)} %bitcast.22) | data formatting | bytes 8388608 | tf_op jit(solution)/shard_map/transpose | solution.py:81
  431.4 6.3 subtract_multiply_fusion
  447.8 5.8 fusion.83
  453.6 8.1 %all-to-all-done.4 = f32[8,4,32,128]{3,2,1,0:T(8,128)S(1)} async-done(((f32[8,4,32,128]{3,2,1,0:T(8,128)}), f32[8,4,32,128]{3,2,1,0:T(8,128)S(1)}, u32[]{:S(2)}, u32[]{:S(2)}) %all-to-all-start.4) | async-done | bytes 524320 | tf_op jit(solution)/shard_map/all_to_all | solution.py:197
  487.1 13.5 %all-to-all-done.5 = f32[8,4,32,256]{3,2,1,0:T(8,128)S(1)} async-done(((f32[8,4,32,256]{3,2,1,0:T(8,128)}), f32[8,4,32,256]{3,2,1,0:T(8,128)S(1)}, u32[]{:S(2)}, u32[]{:S(2)}) %all-to-all-start.5) | async-done | bytes 1048608 | tf_op jit(solution)/shard_map/all_to_all | solution.py:197
  525.2 5.5 collective-permute-done.11
  533.5 6.2 all-to-all-done.6
  568.4 5.7 collective-permute-done.14
  577.4 7.2 %collective-permute-done.17 = f32[4,64,256]{2,1,0:T(8,128)} collective-permute-done((f32[4,64,256]{2,1,0:T(8,128)}, f32[4,64,256]{2,1,0:T(8,128)}, u32[]{:S(2)}, u32[]{:S(2)}) %collective-permute-start.17) | collective-permute-done | bytes 262176 | tf_op jit(solution)/shard_map/ppermute | solution.py:150
  (250 shorter events, 268.9 us)
Async XLA Ops:
  12.6 100.6 %all-to-all-start = ((f32[8,4,32,1024]{3,2,1,0:T(8,128)}), f32[8,4,32,1024]{3,2,1,0:T(8,128)}, u32[]{:S(2)}, u32[]{:S(2)}) async-start(f32[8,4,32,1024]{3,2,1,0:T(8,128)} %copy.125), calls=%async_computation | async-start | bytes 8388608 | tf_op jit(solution)/shard_map/all_to_all | solution.py:73
  21.3 42.0 %collective-permute-start = (f32[1,32,16,512]{3,2,1,0:T(8,128)}, f32[1,32,16,512]{3,2,1,0:T(8,128)S(1)}, u32[]{:S(2)}, u32[]{:S(2)}) collective-permute-start(f32[1,32,16,512]{3,2,1,0:T(8,128)} %slice.174), channel_id=1, source_target_pairs={{8,0},{16,8},{24,16},{9,1},{17,9},{25,17},{10,2},{18,10},{26,18},{... | collective-permute-start | bytes 3145736 | tf_op jit(solution)/shard_map/ppermute | solution.py:13
  26.8 36.5 %collective-permute-start.1 = (f32[1,32,16,512]{3,2,1,0:T(8,128)}, f32[1,32,16,512]{3,2,1,0:T(8,128)S(1)}, u32[]{:S(2)}, u32[]{:S(2)}) collective-permute-start(f32[1,32,16,512]{3,2,1,0:T(8,128)} %slice.234), channel_id=1, source_target_pairs={{0,8},{8,16},{16,24},{1,9},{9,17},{17,25},{2,10},{10,18},{18,26},{... | collective-permute-start | bytes 3145736 | tf_op jit(solution)/shard_map/ppermute | solution.py:13
  113.1 98.9 %all-to-all-start.1 = ((f32[8,4,32,1024]{3,2,1,0:T(8,128)}), f32[8,4,32,1024]{3,2,1,0:T(8,128)}, u32[]{:S(2)}, u32[]{:S(2)}) async-start(f32[8,4,32,1024]{3,2,1,0:T(8,128)} %bitcast.311), calls=%async_computation.1 | async-start | bytes 8388608 | tf_op jit(solution)/shard_map/all_to_all | solution.py:73
  222.7 98.5 %all-to-all-start.2 = ((f32[8,4,32,1024]{3,2,1,0:T(8,128)}), f32[8,4,32,1024]{3,2,1,0:T(8,128)}, u32[]{:S(2)}, u32[]{:S(2)}) async-start(f32[8,4,32,1024]{3,2,1,0:T(8,128)} %bitcast.312), calls=%async_computation.2 | async-start | bytes 8388608 | tf_op jit(solution)/shard_map/all_to_all | solution.py:78
  321.3 98.6 %all-to-all-start.3 = ((f32[8,4,32,1024]{3,2,1,0:T(8,128)}), f32[8,4,32,1024]{3,2,1,0:T(8,128)}, u32[]{:S(2)}, u32[]{:S(2)}) async-start(f32[8,4,32,1024]{3,2,1,0:T(8,128)} %bitcast.310), calls=%async_computation.3 | async-start | bytes 8388608 | tf_op jit(solution)/shard_map/all_to_all | solution.py:78
  335.6 48.7 %collective-permute-start.2 = (f32[1,32,16,512]{3,2,1,0:T(8,128)}, f32[1,32,16,512]{3,2,1,0:T(8,128)S(1)}, u32[]{:S(2)}, u32[]{:S(2)}) collective-permute-start(f32[1,32,16,512]{3,2,1,0:T(8,128)} %slice.180), channel_id=1, source_target_pairs={{8,0},{16,8},{24,16},{9,1},{17,9},{25,17},{10,2},{18,10},{26,18},{... | collective-permute-start | bytes 3145736 | tf_op jit(solution)/shard_map/ppermute | solution.py:13
  348.0 36.3 %collective-permute-start.3 = (f32[1,32,16,512]{3,2,1,0:T(8,128)}, f32[1,32,16,512]{3,2,1,0:T(8,128)S(1)}, u32[]{:S(2)}, u32[]{:S(2)}) collective-permute-start(f32[1,32,16,512]{3,2,1,0:T(8,128)} %slice.238), channel_id=1, source_target_pairs={{0,8},{8,16},{16,24},{1,9},{9,17},{17,25},{2,10},{10,18},{18,26},{... | collective-permute-start | bytes 3145736 | tf_op jit(solution)/shard_map/ppermute | solution.py:13
  442.7 18.9 %all-to-all-start.4 = ((f32[8,4,32,128]{3,2,1,0:T(8,128)}), f32[8,4,32,128]{3,2,1,0:T(8,128)S(1)}, u32[]{:S(2)}, u32[]{:S(2)}) async-start(f32[8,4,32,128]{3,2,1,0:T(8,128)} %reshape.345), calls=%async_computation.4 | async-start | bytes 1048576 | tf_op jit(solution)/shard_map/all_to_all | solution.py:197
  470.5 30.1 %all-to-all-start.5 = ((f32[8,4,32,256]{3,2,1,0:T(8,128)}), f32[8,4,32,256]{3,2,1,0:T(8,128)S(1)}, u32[]{:S(2)}, u32[]{:S(2)}) async-start(f32[8,4,32,256]{3,2,1,0:T(8,128)} %reshape.348), calls=%async_computation.5 | async-start | bytes 2097152 | tf_op jit(solution)/shard_map/all_to_all | solution.py:197
  509.7 30.1 %all-to-all-start.6 = ((f32[8,4,32,256]{3,2,1,0:T(8,128)}), f32[8,4,32,256]{3,2,1,0:T(8,128)S(1)}, u32[]{:S(2)}, u32[]{:S(2)}) async-start(f32[8,4,32,256]{3,2,1,0:T(8,128)} %reshape.353), calls=%async_computation.6 | async-start | bytes 2097152 | tf_op jit(solution)/shard_map/all_to_all | solution.py:197
  515.9 14.8 %collective-permute-start.11 = (f32[4,64,256]{2,1,0:T(8,128)S(1)}, f32[4,64,256]{2,1,0:T(8,128)S(1)}, u32[]{:S(2)}, u32[]{:S(2)}) collective-permute-start(f32[4,64,256]{2,1,0:T(8,128)S(1)} %get-tuple-element.65), channel_id=1, source_target_pairs={{0,16},{8,24},{16,0},{24,8},{1,17},{9,25},{17,1},{25,9},{2,18},{10... | collective-permute-start | bytes 786440 | tf_op jit(solution)/shard_map/ppermute | solution.py:150
  518.0 34.4 %collective-permute-start.7 = (f32[4,64,128]{2,0,1:T(4,128)S(1)}, f32[4,64,128]{2,0,1:T(4,128)}, u32[]{:S(2)}, u32[]{:S(2)}) collective-permute-start(f32[4,64,128]{2,0,1:T(4,128)S(1)} %get-tuple-element.84), channel_id=1, source_target_pairs={{0,24},{8,0},{16,8},{24,16},{1,25},{9,1},{17,9},{25,17},{2,26},{10... | collective-permute-start | bytes 393224 | tf_op jit(solution)/shard_map/ppermute | solution.py:150
  520.4 32.0 %collective-permute-start.8 = (f32[4,64,128]{2,0,1:T(4,128)S(1)}, f32[4,64,128]{2,0,1:T(4,128)}, u32[]{:S(2)}, u32[]{:S(2)}) collective-permute-start(f32[4,64,128]{2,0,1:T(4,128)S(1)} %get-tuple-element.83), channel_id=1, source_target_pairs={{0,16},{8,24},{16,0},{24,8},{1,17},{9,25},{17,1},{25,9},{2,18},{10... | collective-permute-start | bytes 393224 | tf_op jit(solution)/shard_map/ppermute | solution.py:150
  522.6 29.9 %collective-permute-start.9 = (f32[4,64,128]{2,0,1:T(4,128)S(1)}, f32[4,64,128]{2,0,1:T(4,128)}, u32[]{:S(2)}, u32[]{:S(2)}) collective-permute-start(f32[4,64,128]{2,0,1:T(4,128)S(1)} %get-tuple-element.82), channel_id=1, source_target_pairs={{0,8},{8,16},{16,24},{24,0},{1,9},{9,17},{17,25},{25,1},{2,10},{10... | collective-permute-start | bytes 393224 | tf_op jit(solution)/shard_map/ppermute | solution.py:150
  548.8 38.7 %all-to-all-start.7 = ((f32[8,4,32,256]{3,2,1,0:T(8,128)}), f32[8,4,32,256]{3,2,1,0:T(8,128)S(1)}, u32[]{:S(2)}, u32[]{:S(2)}) async-start(f32[8,4,32,256]{3,2,1,0:T(8,128)} %reshape.358), calls=%async_computation.7 | async-start | bytes 2097152 | tf_op jit(solution)/shard_map/all_to_all | solution.py:197
  566.7 17.9 %collective-permute-start.17 = (f32[4,64,256]{2,1,0:T(8,128)}, f32[4,64,256]{2,1,0:T(8,128)}, u32[]{:S(2)}, u32[]{:S(2)}) collective-permute-start(f32[4,64,256]{2,1,0:T(8,128)} %get-tuple-element.58), channel_id=1, source_target_pairs={{0,16},{8,24},{16,0},{24,8},{1,17},{9,25},{17,1},{25,9},{2,18},{10... | collective-permute-start | bytes 786440 | tf_op jit(solution)/shard_map/ppermute | solution.py:150
  568.2 16.3 %collective-permute-start.16 = (f32[4,64,256]{2,1,0:T(8,128)}, f32[4,64,256]{2,1,0:T(8,128)}, u32[]{:S(2)}, u32[]{:S(2)}) collective-permute-start(f32[4,64,256]{2,1,0:T(8,128)} %get-tuple-element.59), channel_id=1, source_target_pairs={{0,8},{8,16},{16,24},{24,0},{1,9},{9,17},{17,25},{25,1},{2,10},{10... | collective-permute-start | bytes 786440 | tf_op jit(solution)/shard_map/ppermute | solution.py:150
  589.6 18.4 %collective-permute-start.24 = (f32[4,64,256]{2,1,0:T(8,128)}, f32[4,64,256]{2,1,0:T(8,128)}, u32[]{:S(2)}, u32[]{:S(2)}) collective-permute-start(f32[4,64,256]{2,1,0:T(8,128)} %get-tuple-element.50), channel_id=1, source_target_pairs={{0,24},{8,0},{16,8},{24,16},{1,25},{9,1},{17,9},{25,17},{2,26},{10... | collective-permute-start | bytes 786440 | tf_op jit(solution)/shard_map/ppermute | solution.py:150
  590.1 18.6 %collective-permute-start.23 = (f32[4,64,256]{2,1,0:T(8,128)}, f32[4,64,256]{2,1,0:T(8,128)}, u32[]{:S(2)}, u32[]{:S(2)}) collective-permute-start(f32[4,64,256]{2,1,0:T(8,128)} %get-tuple-element.51), channel_id=1, source_target_pairs={{0,16},{8,24},{16,0},{24,8},{1,17},{9,25},{17,1},{25,9},{2,18},{10... | collective-permute-start | bytes 786440 | tf_op jit(solution)/shard_map/ppermute | solution.py:150
  591.4 17.3 %collective-permute-start.22 = (f32[4,64,256]{2,1,0:T(8,128)}, f32[4,64,256]{2,1,0:T(8,128)}, u32[]{:S(2)}, u32[]{:S(2)}) collective-permute-start(f32[4,64,256]{2,1,0:T(8,128)} %get-tuple-element.52), channel_id=1, source_target_pairs={{0,8},{8,16},{16,24},{24,0},{1,9},{9,17},{17,25},{25,1},{2,10},{10... | collective-permute-start | bytes 786440 | tf_op jit(solution)/shard_map/ppermute | solution.py:150
  595.4 20.8 %collective-permute-start.19 = (f32[4,64,256]{2,0,1:T(4,128)}, f32[4,64,256]{2,0,1:T(4,128)S(1)}, u32[]{:S(2)}, u32[]{:S(2)}) collective-permute-start(f32[4,64,256]{2,0,1:T(4,128)} %get-tuple-element.55), channel_id=1, source_target_pairs={{0,24},{8,0},{16,8},{24,16},{1,25},{9,1},{17,9},{25,17},{2,26},{10... | collective-permute-start | bytes 786440 | tf_op jit(solution)/shard_map/ppermute | solution.py:150
  597.8 18.3 %collective-permute-start.20 = (f32[4,64,256]{2,0,1:T(4,128)}, f32[4,64,256]{2,0,1:T(4,128)}, u32[]{:S(2)}, u32[]{:S(2)}) collective-permute-start(f32[4,64,256]{2,0,1:T(4,128)} %get-tuple-element.54), channel_id=1, source_target_pairs={{0,16},{8,24},{16,0},{24,8},{1,17},{9,25},{17,1},{25,9},{2,18},{10... | collective-permute-start | bytes 786440 | tf_op jit(solution)/shard_map/ppermute | solution.py:150
  603.3 28.0 %all-to-all-start.8 = ((f32[8,4,32,128]{3,2,1,0:T(8,128)}), f32[8,4,32,128]{3,2,1,0:T(8,128)S(1)}, u32[]{:S(2)}, u32[]{:S(2)}) async-start(f32[8,4,32,128]{3,2,1,0:T(8,128)} %reshape.365), calls=%async_computation.8 | async-start | bytes 1048576 | tf_op jit(solution)/shard_map/all_to_all | solution.py:197
  (48 other events, 557.0 us)

commit v13 on v12

--- a/solution.py
+++ b/solution.py
@@ -150,7 +150,7 @@
         return lax.ppermute(x, "hel", [(i, (i + d) % nh) for i in range(nh)])
 
     if vc % 8 == 0:
-        sizes = [vc // 8] + [vc // 4] * 3 + [vc // 8]
+        sizes = [vc // 8, 3 * vc // 8, 3 * vc // 8, vc // 8]
     else:
         sizes = [vc]
     bounds = [sum(sizes[:i]) for i in range(len(sizes) + 1)]

time: 658 us -> 667 us (1.014)
  waiting for transfers between devices: 299 us -> 310 us
    all_to_all x5 -> x4, waiting for transfers between devices: 27.8 us -> 44.2 us  [shards(): lax.all_to_all(chans.reshape(n, kl, rl, width), 'rad', 0, 0, tiled=True)]
    transpose x0 -> x2, local copies, waits for them, and re-layouts: none -> 7.81 us  [shards(): chans = jnp.transpose(part.reshape(kl, rl, vs, n, cb), (3, 0, 1, 2, 4))]
    ppermute x30 -> x24, waiting for transfers between devices: 44.8 us -> 38.7 us  [hel_shift(): return lax.ppermute(x, 'hel', [(i, (i + d) % nh) for i in range(nh)])]
    reshape x10 -> x6, local copies, waits for them, and re-layouts: 14.2 us -> 8.25 us  [shards(): chans = jnp.transpose(part.reshape(kl, rl, vs, n, cb), (3, 0, 1, 2, 4))]
    all_to_all x5 -> x4, starting transfers between devices: 19.1 us -> 15.8 us  [shards(): lax.all_to_all(chans.reshape(n, kl, rl, width), 'rad', 0, 0, tiled=True)]
    ppermute x30 -> x24, starting transfers between devices: 37.6 us -> 36.3 us  [hel_shift(): return lax.ppermute(x, 'hel', [(i, (i + d) % nh) for i in range(nh)])]
    reshape x5 -> x4, local copies, waits for them, and re-layouts: 13.9 us -> 13.1 us  [shards(): chans.reshape(n, kl, rl, width)]
  transfers between devices with their start and end apart: 43 -> 36, of which waited for: 23 -> 18; matrix products, arithmetic and copies ran while one was open for 29% -> 26% of each run, Pallas kernels for 0% -> 0%
where the time goes in v13:
time: 667 us; the launch traced here: 661 us
  waiting for transfers between devices  310 us (46%)
  local copies, waits for them, and re-layouts  157 us (24%)
  starting transfers between devices  84.9 us (13%)
  matrix products  81.5 us (12%)
  other arithmetic  25.7 us (4%)
    all_to_all x2, waiting for transfers between devices, to_radial_columns(): got = lax.all_to_all(blocks, 'rad', 0, 0, tiled=True).reshape(n, kl, rl, mb)  115 us
    all_to_all x2, waiting for transfers between devices, to_radial_rows(): got = lax.all_to_all(blocks, 'rad', 0, 0, tiled=True).reshape(n, kl, rl, mb)  112 us
    all_to_all x4, waiting for transfers between devices, shards(): lax.all_to_all(chans.reshape(n, kl, rl, width), 'rad', 0, 0, tiled=True)  44.2 us
    ppermute x24, waiting for transfers between devices, hel_shift(): return lax.ppermute(x, 'hel', [(i, (i + d) % nh) for i in range(nh)])  38.7 us
    ppermute x24, starting transfers between devices, hel_shift(): return lax.ppermute(x, 'hel', [(i, (i + d) % nh) for i in range(nh)])  36.3 us
    dot_general x2, matrix products, local_part(): jnp.dot(current.reshape(-1, cc), transform.T, precision=PRECISE, preferre...  25 us
    dot_general x2, matrix products, local_part(): jnp.dot(angles.reshape(-1, angles.shape[3]), transform, precision=PRECISE...  21.5 us
    reshape x3, local copies, waits for them, and re-layouts, to_radial_columns(): blocks = jnp.transpose(x.reshape(kl, rl, n, mb), (2, 0, 1, 3))  17.1 us
  transfers between devices with their start and end apart: 36, of which 18 were waited for; matrix products, arithmetic and copies ran while one was open for 26% of the time, Pallas kernels for 0%

profile of v13, /device:TPU:0, one launch (start us, length us, event | category | flops | bytes accessed | tf_op | source)
XLA Modules:
  0.0 660.7 jit_solution(2455280399080485428)
XLA Ops:
  5.9 6.6 %copy.117 = f32[8,4,32,1024]{3,2,1,0:T(8,128)} copy(f32[8,4,32,1024]{3,0,2,1:T(8,128)} %bitcast.263) | data formatting | bytes 8388608 | tf_op jit(solution)/shard_map/transpose | solution.py:72
  12.6 6.5 all-to-all-start
  35.8 16.4 %convolution_bitcast_fusion = f32[2048,512]{0,1:T(8,128)} fusion(f32[512,512]{1,0:T(8,128)S(1)} %convolution_multiply_fusion, f32[2048,512]{1,0:T(8,128)} %bitcast.254), kind=kOutput, calls=%fused_computation.24 | convolution fusion | flops 6442450944 | bytes 9437184 | tf_op jit(solution)/shard_map/dot_general | solution.py:93
  52.2 5.4 copy.119
  57.6 5.7 fusion.40
  63.4 11.8 %fusion.5 = f32[4,32,16,512]{3,2,1,0:T(8,128)} fusion(f32[1,32,16,512]{3,2,1,0:T(8,128)S(1)} %collective-permute-done, f32[3,32,16,512]{3,2,1,0:T(8,128)} %slice.146, f32[3,32,16,512]{3,2,1,0:T(8,128)S(1)} %slice-done.1, f32[1,32,16,512]{3,2,1,0:T(8,128)S(1)} %collective-permute-done.1, f32[4,32,16,512]{3,2,1,0:T(8,128)} %param.15, ...), kind=kOutput, calls=%fused_computation.9 | convolution fusion | flops 6456082432 | bytes 26288448 | tf_op jit(solution)/shard_map/dot_general | solution.py:105
  80.4 6.6 %copy.180 = f32[4,32,8,1024]{3,1,0,2:T(8,128)} copy(f32[4,32,8,1024]{3,2,1,0:T(8,128)} %reshape.319) | data formatting | bytes 8388608 | tf_op jit(solution)/shard_map/reshape | solution.py:72
  87.1 26.1 %all-to-all-done = f32[8,4,32,1024]{3,2,1,0:T(8,128)} async-done(((f32[8,4,32,1024]{3,2,1,0:T(8,128)}), f32[8,4,32,1024]{3,2,1,0:T(8,128)}, u32[]{:S(2)}, u32[]{:S(2)}) %all-to-all-start) | async-done | bytes 4194336 | tf_op jit(solution)/shard_map/all_to_all | solution.py:73
  122.8 89.2 %all-to-all-done.1 = f32[8,4,32,1024]{3,2,1,0:T(8,128)} async-done(((f32[8,4,32,1024]{3,2,1,0:T(8,128)}), f32[8,4,32,1024]{3,2,1,0:T(8,128)}, u32[]{:S(2)}, u32[]{:S(2)}) %all-to-all-start.1) | async-done | bytes 4194336 | tf_op jit(solution)/shard_map/all_to_all | solution.py:73
  227.3 5.6 fusion.42
  235.6 85.7 %all-to-all-done.2 = f32[8,4,32,1024]{3,2,1,0:T(8,128)} async-done(((f32[8,4,32,1024]{3,2,1,0:T(8,128)}), f32[8,4,32,1024]{3,2,1,0:T(8,128)}, u32[]{:S(2)}, u32[]{:S(2)}) %all-to-all-start.2) | async-done | bytes 4194336 | tf_op jit(solution)/shard_map/all_to_all | solution.py:78
  327.2 6.6 %copy.123 = f32[4,32,8,1024]{3,2,1,0:T(8,128)} copy(f32[4,32,8,1024]{3,1,0,2:T(8,128)} %bitcast.15) | data formatting | bytes 8388608 | tf_op jit(solution)/shard_map/transpose | solution.py:81
  361.6 5.4 copy.125
  371.6 8.6 %fusion.23 = f32[128,16,512]{2,1,0:T(8,128)S(1)} fusion(f32[128,16,512]{2,1,0:T(8,128)} %dot_general.82, f32[512,512]{1,0:T(8,128)S(1)} %convolution_multiply_fusion), kind=kOutput, calls=%fused_computation.39 | convolution fusion | flops 6442450944 | bytes 9437184 | tf_op jit(solution)/shard_map/dot_general | solution.py:93
  384.4 9.7 %fusion.8 = f32[4,32,16,512]{3,2,1,0:T(8,128)} fusion(f32[1,32,16,512]{3,2,1,0:T(8,128)S(1)} %collective-permute-done.2, f32[3,32,16,512]{3,2,1,0:T(8,128)S(1)} %copy-done.10, f32[3,32,16,512]{3,2,1,0:T(8,128)S(1)} %slice-done, f32[1,32,16,512]{3,2,1,0:T(8,128)S(1)} %collective-permute-done.3, f32[4,32,16,512]{3,2,1,0:T(8,128)S(1)} %copy-done.4, ...), kind=kOutput, calls=%fused_computation.13 | convolution fusion | flops 6451888128 | bytes 22094016 | tf_op jit(solution)/shard_map/dot_general | solution.py:105
  394.0 25.9 %all-to-all-done.3 = f32[8,4,32,1024]{3,2,1,0:T(8,128)} async-done(((f32[8,4,32,1024]{3,2,1,0:T(8,128)}), f32[8,4,32,1024]{3,2,1,0:T(8,128)}, u32[]{:S(2)}, u32[]{:S(2)}) %all-to-all-start.3) | async-done | bytes 4194336 | tf_op jit(solution)/shard_map/all_to_all | solution.py:78
  419.9 6.6 %copy.128 = f32[4,32,8,1024]{3,2,1,0:T(8,128)} copy(f32[4,32,8,1024]{3,1,0,2:T(8,128)} %bitcast.22) | data formatting | bytes 8388608 | tf_op jit(solution)/shard_map/transpose | solution.py:81
  431.4 6.3 subtract_multiply_fusion
  452.9 9.7 %all-to-all-done.4 = f32[8,4,32,128]{3,2,1,0:T(8,128)S(1)} async-done(((f32[8,4,32,128]{3,2,1,0:T(8,128)}), f32[8,4,32,128]{3,2,1,0:T(8,128)S(1)}, u32[]{:S(2)}, u32[]{:S(2)}) %all-to-all-start.4) | async-done | bytes 524320 | tf_op jit(solution)/shard_map/all_to_all | solution.py:197
  494.7 24.8 %all-to-all-done.5 = f32[8,4,32,384]{3,2,1,0:T(8,128)} async-done(((f32[8,4,32,384]{3,2,1,0:T(8,128)}), f32[8,4,32,384]{3,2,1,0:T(8,128)}, u32[]{:S(2)}, u32[]{:S(2)}) %all-to-all-start.5) | async-done | bytes 1572896 | tf_op jit(solution)/shard_map/all_to_all | solution.py:197
  556.7 8.5 %collective-permute-done.11 = f32[4,64,384]{2,1,0:T(8,128)S(1)} collective-permute-done((f32[4,64,384]{2,1,0:T(8,128)}, f32[4,64,384]{2,1,0:T(8,128)S(1)}, u32[]{:S(2)}, u32[]{:S(2)}) %collective-permute-start.11) | collective-permute-done | bytes 393248 | tf_op jit(solution)/shard_map/ppermute | solution.py:150
  569.0 9.7 %all-to-all-done.6 = f32[8,4,32,384]{3,2,1,0:T(8,128)S(1)} async-done(((f32[8,4,32,384]{3,2,1,0:T(8,128)}), f32[8,4,32,384]{3,2,1,0:T(8,128)S(1)}, u32[]{:S(2)}, u32[]{:S(2)}) %all-to-all-start.6) | async-done | bytes 1572896 | tf_op jit(solution)/shard_map/all_to_all | solution.py:197
  609.0 8.0 %collective-permute-start.19 = (f32[4,64,384]{2,0,1:T(4,128)}, f32[4,64,384]{2,0,1:T(4,128)}, u32[]{:S(2)}, u32[]{:S(2)}) collective-permute-start(f32[4,64,384]{2,0,1:T(4,128)} %bitcast.67), channel_id=1, source_target_pairs={{0,24},{8,0},{16,8},{24,16},{1,25},{9,1},{17,9},{25,17},{2,26},{10... | collective-permute-start | bytes 1179656 | tf_op jit(solution)/shard_map/ppermute | solution.py:150
  629.4 8.6 %collective-permute-done.20 = f32[4,64,384]{2,0,1:T(4,128)} collective-permute-done((f32[4,64,384]{2,0,1:T(4,128)}, f32[4,64,384]{2,0,1:T(4,128)}, u32[]{:S(2)}, u32[]{:S(2)}) %collective-permute-start.20) | collective-permute-done | bytes 393248 | tf_op jit(solution)/shard_map/ppermute | solution.py:150
  (232 shorter events, 255.0 us)
Async XLA Ops:
  12.6 100.6 %all-to-all-start = ((f32[8,4,32,1024]{3,2,1,0:T(8,128)}), f32[8,4,32,1024]{3,2,1,0:T(8,128)}, u32[]{:S(2)}, u32[]{:S(2)}) async-start(f32[8,4,32,1024]{3,2,1,0:T(8,128)} %copy.117), calls=%async_computation | async-start | bytes 8388608 | tf_op jit(solution)/shard_map/all_to_all | solution.py:73
  21.3 42.0 %collective-permute-start = (f32[1,32,16,512]{3,2,1,0:T(8,128)}, f32[1,32,16,512]{3,2,1,0:T(8,128)S(1)}, u32[]{:S(2)}, u32[]{:S(2)}) collective-permute-start(f32[1,32,16,512]{3,2,1,0:T(8,128)} %slice.147), channel_id=1, source_target_pairs={{8,0},{16,8},{24,16},{9,1},{17,9},{25,17},{10,2},{18,10},{26,18},{... | collective-permute-start | bytes 3145736 | tf_op jit(solution)/shard_map/ppermute | solution.py:13
  26.8 36.5 %collective-permute-start.1 = (f32[1,32,16,512]{3,2,1,0:T(8,128)}, f32[1,32,16,512]{3,2,1,0:T(8,128)S(1)}, u32[]{:S(2)}, u32[]{:S(2)}) collective-permute-start(f32[1,32,16,512]{3,2,1,0:T(8,128)} %slice.198), channel_id=1, source_target_pairs={{0,8},{8,16},{16,24},{1,9},{9,17},{17,25},{2,10},{10,18},{18,26},{... | collective-permute-start | bytes 3145736 | tf_op jit(solution)/shard_map/ppermute | solution.py:13
  113.1 98.9 %all-to-all-start.1 = ((f32[8,4,32,1024]{3,2,1,0:T(8,128)}), f32[8,4,32,1024]{3,2,1,0:T(8,128)}, u32[]{:S(2)}, u32[]{:S(2)}) async-start(f32[8,4,32,1024]{3,2,1,0:T(8,128)} %bitcast.260), calls=%async_computation.1 | async-start | bytes 8388608 | tf_op jit(solution)/shard_map/all_to_all | solution.py:73
  222.7 98.6 %all-to-all-start.2 = ((f32[8,4,32,1024]{3,2,1,0:T(8,128)}), f32[8,4,32,1024]{3,2,1,0:T(8,128)}, u32[]{:S(2)}, u32[]{:S(2)}) async-start(f32[8,4,32,1024]{3,2,1,0:T(8,128)} %bitcast.261), calls=%async_computation.2 | async-start | bytes 8388608 | tf_op jit(solution)/shard_map/all_to_all | solution.py:78
  321.3 98.6 %all-to-all-start.3 = ((f32[8,4,32,1024]{3,2,1,0:T(8,128)}), f32[8,4,32,1024]{3,2,1,0:T(8,128)}, u32[]{:S(2)}, u32[]{:S(2)}) async-start(f32[8,4,32,1024]{3,2,1,0:T(8,128)} %bitcast.259), calls=%async_computation.3 | async-start | bytes 8388608 | tf_op jit(solution)/shard_map/all_to_all | solution.py:78
  335.6 48.7 %collective-permute-start.2 = (f32[1,32,16,512]{3,2,1,0:T(8,128)}, f32[1,32,16,512]{3,2,1,0:T(8,128)S(1)}, u32[]{:S(2)}, u32[]{:S(2)}) collective-permute-start(f32[1,32,16,512]{3,2,1,0:T(8,128)} %slice.153), channel_id=1, source_target_pairs={{8,0},{16,8},{24,16},{9,1},{17,9},{25,17},{10,2},{18,10},{26,18},{... | collective-permute-start | bytes 3145736 | tf_op jit(solution)/shard_map/ppermute | solution.py:13
  348.0 36.3 %collective-permute-start.3 = (f32[1,32,16,512]{3,2,1,0:T(8,128)}, f32[1,32,16,512]{3,2,1,0:T(8,128)S(1)}, u32[]{:S(2)}, u32[]{:S(2)}) collective-permute-start(f32[1,32,16,512]{3,2,1,0:T(8,128)} %slice.202), channel_id=1, source_target_pairs={{0,8},{8,16},{16,24},{1,9},{9,17},{17,25},{2,10},{10,18},{18,26},{... | collective-permute-start | bytes 3145736 | tf_op jit(solution)/shard_map/ppermute | solution.py:13
  477.3 42.3 %all-to-all-start.5 = ((f32[8,4,32,384]{3,2,1,0:T(8,128)}), f32[8,4,32,384]{3,2,1,0:T(8,128)}, u32[]{:S(2)}, u32[]{:S(2)}) async-start(f32[8,4,32,384]{3,2,1,0:T(8,128)} %reshape.330), calls=%async_computation.5 | async-start | bytes 3145728 | tf_op jit(solution)/shard_map/all_to_all | solution.py:197
  537.3 41.3 %all-to-all-start.6 = ((f32[8,4,32,384]{3,2,1,0:T(8,128)}), f32[8,4,32,384]{3,2,1,0:T(8,128)S(1)}, u32[]{:S(2)}, u32[]{:S(2)}) async-start(f32[8,4,32,384]{3,2,1,0:T(8,128)} %reshape.335), calls=%async_computation.6 | async-start | bytes 3145728 | tf_op jit(solution)/shard_map/all_to_all | solution.py:197
  544.6 20.6 %collective-permute-start.11 = (f32[4,64,384]{2,1,0:T(8,128)}, f32[4,64,384]{2,1,0:T(8,128)S(1)}, u32[]{:S(2)}, u32[]{:S(2)}) collective-permute-start(f32[4,64,384]{2,1,0:T(8,128)} %get-tuple-element.47), channel_id=1, source_target_pairs={{0,16},{8,24},{16,0},{24,8},{1,17},{9,25},{17,1},{25,9},{2,18},{10... | collective-permute-start | bytes 1179656 | tf_op jit(solution)/shard_map/ppermute | solution.py:150
  545.1 20.1 %collective-permute-start.10 = (f32[4,64,384]{2,1,0:T(8,128)}, f32[4,64,384]{2,1,0:T(8,128)S(1)}, u32[]{:S(2)}, u32[]{:S(2)}) collective-permute-start(f32[4,64,384]{2,1,0:T(8,128)} %get-tuple-element.48), channel_id=1, source_target_pairs={{0,8},{8,16},{16,24},{24,0},{1,9},{9,17},{17,25},{25,1},{2,10},{10... | collective-permute-start | bytes 1179656 | tf_op jit(solution)/shard_map/ppermute | solution.py:150
  547.4 37.4 %collective-permute-start.7 = (f32[4,64,128]{2,0,1:T(4,128)}, f32[4,64,128]{2,0,1:T(4,128)}, u32[]{:S(2)}, u32[]{:S(2)}) collective-permute-start(f32[4,64,128]{2,0,1:T(4,128)} %get-tuple-element.59), channel_id=1, source_target_pairs={{0,24},{8,0},{16,8},{24,16},{1,25},{9,1},{17,9},{25,17},{2,26},{10... | collective-permute-start | bytes 393224 | tf_op jit(solution)/shard_map/ppermute | solution.py:150
  549.8 35.7 %collective-permute-start.8 = (f32[4,64,128]{2,0,1:T(4,128)}, f32[4,64,128]{2,0,1:T(4,128)}, u32[]{:S(2)}, u32[]{:S(2)}) collective-permute-start(f32[4,64,128]{2,0,1:T(4,128)} %get-tuple-element.58), channel_id=1, source_target_pairs={{0,16},{8,24},{16,0},{24,8},{1,17},{9,25},{17,1},{25,9},{2,18},{10... | collective-permute-start | bytes 393224 | tf_op jit(solution)/shard_map/ppermute | solution.py:150
  554.4 31.1 %collective-permute-start.9 = (f32[4,64,128]{2,0,1:T(4,128)S(1)}, f32[4,64,128]{2,0,1:T(4,128)}, u32[]{:S(2)}, u32[]{:S(2)}) collective-permute-start(f32[4,64,128]{2,0,1:T(4,128)S(1)} %get-tuple-element.57), channel_id=1, source_target_pairs={{0,8},{8,16},{16,24},{24,0},{1,9},{9,17},{17,25},{25,1},{2,10},{10... | collective-permute-start | bytes 393224 | tf_op jit(solution)/shard_map/ppermute | solution.py:150
  584.3 19.6 %collective-permute-start.17 = (f32[4,64,384]{2,1,0:T(8,128)}, f32[4,64,384]{2,1,0:T(8,128)}, u32[]{:S(2)}, u32[]{:S(2)}) collective-permute-start(f32[4,64,384]{2,1,0:T(8,128)} %get-tuple-element.43), channel_id=1, source_target_pairs={{0,16},{8,24},{16,0},{24,8},{1,17},{9,25},{17,1},{25,9},{2,18},{10... | collective-permute-start | bytes 1179656 | tf_op jit(solution)/shard_map/ppermute | solution.py:150
  584.8 19.1 %collective-permute-start.16 = (f32[4,64,384]{2,1,0:T(8,128)}, f32[4,64,384]{2,1,0:T(8,128)}, u32[]{:S(2)}, u32[]{:S(2)}) collective-permute-start(f32[4,64,384]{2,1,0:T(8,128)} %get-tuple-element.44), channel_id=1, source_target_pairs={{0,8},{8,16},{16,24},{24,0},{1,9},{9,17},{17,25},{25,1},{2,10},{10... | collective-permute-start | bytes 1179656 | tf_op jit(solution)/shard_map/ppermute | solution.py:150
  592.5 29.6 %all-to-all-start.7 = ((f32[8,4,32,128]{3,2,1,0:T(8,128)}), f32[8,4,32,128]{3,2,1,0:T(8,128)}, u32[]{:S(2)}, u32[]{:S(2)}) async-start(f32[8,4,32,128]{3,2,1,0:T(8,128)} %reshape.342), calls=%async_computation.7 | async-start | bytes 1048576 | tf_op jit(solution)/shard_map/all_to_all | solution.py:197
  596.9 20.1 %collective-permute-start.13 = (f32[4,64,384]{2,0,1:T(4,128)S(1)}, f32[4,64,384]{2,0,1:T(4,128)S(1)}, u32[]{:S(2)}, u32[]{:S(2)}) collective-permute-start(f32[4,64,384]{2,0,1:T(4,128)S(1)} %get-tuple-element.32), channel_id=1, source_target_pairs={{0,24},{8,0},{16,8},{24,16},{1,25},{9,1},{17,9},{25,17},{2,26},{10... | collective-permute-start | bytes 1179656 | tf_op jit(solution)/shard_map/ppermute | solution.py:150
  599.3 21.4 %collective-permute-start.14 = (f32[4,64,384]{2,0,1:T(4,128)S(1)}, f32[4,64,384]{2,0,1:T(4,128)S(1)}, u32[]{:S(2)}, u32[]{:S(2)}) collective-permute-start(f32[4,64,384]{2,0,1:T(4,128)S(1)} %get-tuple-element.31), channel_id=1, source_target_pairs={{0,16},{8,24},{16,0},{24,8},{1,17},{9,25},{17,1},{25,9},{2,18},{10... | collective-permute-start | bytes 1179656 | tf_op jit(solution)/shard_map/ppermute | solution.py:150
  600.8 19.9 %collective-permute-start.15 = (f32[4,64,384]{2,0,1:T(4,128)S(1)}, f32[4,64,384]{2,0,1:T(4,128)S(1)}, u32[]{:S(2)}, u32[]{:S(2)}) collective-permute-start(f32[4,64,384]{2,0,1:T(4,128)S(1)} %get-tuple-element.30), channel_id=1, source_target_pairs={{0,8},{8,16},{16,24},{24,0},{1,9},{9,17},{17,25},{25,1},{2,10},{10... | collective-permute-start | bytes 1179656 | tf_op jit(solution)/shard_map/ppermute | solution.py:150
  609.0 19.0 %collective-permute-start.19 = (f32[4,64,384]{2,0,1:T(4,128)}, f32[4,64,384]{2,0,1:T(4,128)}, u32[]{:S(2)}, u32[]{:S(2)}) collective-permute-start(f32[4,64,384]{2,0,1:T(4,128)} %bitcast.67), channel_id=1, source_target_pairs={{0,24},{8,0},{16,8},{24,16},{1,25},{9,1},{17,9},{25,17},{2,26},{10... | collective-permute-start | bytes 1179656 | tf_op jit(solution)/shard_map/ppermute | solution.py:150
  617.0 21.1 %collective-permute-start.20 = (f32[4,64,384]{2,0,1:T(4,128)}, f32[4,64,384]{2,0,1:T(4,128)}, u32[]{:S(2)}, u32[]{:S(2)}) collective-permute-start(f32[4,64,384]{2,0,1:T(4,128)} %bitcast.68), channel_id=1, source_target_pairs={{0,16},{8,24},{16,0},{24,8},{1,17},{9,25},{17,1},{25,9},{2,18},{10... | collective-permute-start | bytes 1179656 | tf_op jit(solution)/shard_map/ppermute | solution.py:150
  617.0 21.1 %collective-permute-start.21 = (f32[4,64,384]{2,0,1:T(4,128)}, f32[4,64,384]{2,0,1:T(4,128)}, u32[]{:S(2)}, u32[]{:S(2)}) collective-permute-start(f32[4,64,384]{2,0,1:T(4,128)} %bitcast.69), channel_id=1, source_target_pairs={{0,8},{8,16},{16,24},{24,0},{1,9},{9,17},{17,25},{25,1},{2,10},{10... | collective-permute-start | bytes 1179656 | tf_op jit(solution)/shard_map/ppermute | solution.py:150
  (46 other events, 615.2 us)

commit v14 on v10

--- a/solution.py
+++ b/solution.py
@@ -150,7 +150,7 @@
         return lax.ppermute(x, "hel", [(i, (i + d) % nh) for i in range(nh)])
 
     if vc % 8 == 0:
-        sizes = [vc // 8] + [vc // 4] * 3 + [vc // 8]
+        sizes = [vc // 8] * 2 + [vc // 4] * 2 + [vc // 8] * 2
     else:
         sizes = [vc]
     bounds = [sum(sizes[:i]) for i in range(len(sizes) + 1)]

time: 657 us -> 662 us (level)
  starting transfers between devices: 85 us -> 97.4 us
    all_to_all x5 -> x6, waiting for transfers between devices: 45.1 us -> 36.6 us  [shards(): lax.all_to_all(chans.reshape(n, kl, rl, width), 'rad', 0, 0, tiled=True)]
    ppermute x30 -> x36, starting transfers between devices: 34.4 us -> 42.6 us  [hel_shift(): return lax.ppermute(x, 'hel', [(i, (i + d) % nh) for i in range(nh)])]
    ppermute x30 -> x36, waiting for transfers between devices: 38.1 us -> 43.7 us  [hel_shift(): return lax.ppermute(x, 'hel', [(i, (i + d) % nh) for i in range(nh)])]
    all_to_all x5 -> x6, starting transfers between devices: 17.8 us -> 21.7 us  [shards(): lax.all_to_all(chans.reshape(n, kl, rl, width), 'rad', 0, 0, tiled=True)]
    unnamed x82 -> x91, local copies, waits for them, and re-layouts: 18.5 us -> 15.9 us
    reshape x10 -> x12, local copies, waits for them, and re-layouts: 13.2 us -> 14.9 us  [shards(): chans = jnp.transpose(part.reshape(kl, rl, vs, n, cb), (3, 0, 1, 2, 4))]
    reshape x5 -> x6, local copies, waits for them, and re-layouts: 12.5 us -> 13.3 us  [shards(): chans.reshape(n, kl, rl, width)]
  transfers between devices with their start and end apart: 43 -> 50, of which waited for: 20 -> 26; matrix products, arithmetic and copies ran while one was open for 29% -> 27% of each run, Pallas kernels for 0% -> 0%
where the time goes in v14:
time: 662 us; the launch traced here: 656 us
  waiting for transfers between devices  306 us (46%)
  local copies, waits for them, and re-layouts  154 us (23%)
  starting transfers between devices  97.4 us (15%)
  matrix products  78.2 us (12%)
  other arithmetic  18.5 us (3%)
    all_to_all x2, waiting for transfers between devices, to_radial_columns(): got = lax.all_to_all(blocks, 'rad', 0, 0, tiled=True).reshape(n, kl, rl, mb)  115 us
    all_to_all x2, waiting for transfers between devices, to_radial_rows(): got = lax.all_to_all(blocks, 'rad', 0, 0, tiled=True).reshape(n, kl, rl, mb)  111 us
    ppermute x36, waiting for transfers between devices, hel_shift(): return lax.ppermute(x, 'hel', [(i, (i + d) % nh) for i in range(nh)])  43.7 us
    ppermute x36, starting transfers between devices, hel_shift(): return lax.ppermute(x, 'hel', [(i, (i + d) % nh) for i in range(nh)])  42.6 us
    all_to_all x6, waiting for transfers between devices, shards(): lax.all_to_all(chans.reshape(n, kl, rl, width), 'rad', 0, 0, tiled=True)  36.6 us
    dot_general x2, matrix products, local_part(): jnp.dot(current.reshape(-1, cc), transform.T, precision=PRECISE, preferre...  25 us
    all_to_all x6, starting transfers between devices, shards(): lax.all_to_all(chans.reshape(n, kl, rl, width), 'rad', 0, 0, tiled=True)  21.7 us
    dot_general x2, matrix products, local_part(): jnp.dot(angles.reshape(-1, angles.shape[3]), transform, precision=PRECISE...  21.1 us
  transfers between devices with their start and end apart: 50, of which 26 were waited for; matrix products, arithmetic and copies ran while one was open for 27% of the time, Pallas kernels for 0%

profile of v14, /device:TPU:0, one launch (start us, length us, event | category | flops | bytes accessed | tf_op | source)
XLA Modules:
  0.0 655.8 jit_solution(7311390012980515289)
XLA Ops:
  0.6 5.3 reshape.374
  5.9 6.6 %copy.120 = f32[8,4,32,1024]{3,2,1,0:T(8,128)} copy(f32[8,4,32,1024]{3,0,2,1:T(8,128)} %bitcast.404) | data formatting | bytes 8388608 | tf_op jit(solution)/shard_map/transpose | solution.py:72
  12.6 6.5 all-to-all-start
  36.7 16.4 %convolution_bitcast_fusion = f32[2048,512]{0,1:T(8,128)} fusion(f32[512,512]{1,0:T(8,128)S(1)} %convolution_multiply_fusion, f32[2048,512]{1,0:T(8,128)} %bitcast.395), kind=kOutput, calls=%fused_computation.23 | convolution fusion | flops 6442450944 | bytes 9437184 | tf_op jit(solution)/shard_map/dot_general | solution.py:93
  53.1 5.4 copy.122
  58.5 5.7 fusion.49
  64.3 11.6 %fusion.5 = f32[4,32,16,512]{3,2,1,0:T(8,128)} fusion(f32[1,32,16,512]{3,2,1,0:T(8,128)S(1)} %collective-permute-done, f32[3,32,16,512]{3,2,1,0:T(8,128)} %slice.216, f32[3,32,16,512]{3,2,1,0:T(8,128)S(1)} %slice-done.1, f32[1,32,16,512]{3,2,1,0:T(8,128)S(1)} %collective-permute-done.1, f32[4,32,16,512]{3,2,1,0:T(8,128)} %param.15, ...), kind=kOutput, calls=%fused_computation.9 | convolution fusion | flops 6456082432 | bytes 26288448 | tf_op jit(solution)/shard_map/dot_general | solution.py:105
  75.8 5.2 reshape.379
  81.1 6.6 %copy.251 = f32[4,32,8,1024]{3,1,0,2:T(8,128)} copy(f32[4,32,8,1024]{3,2,1,0:T(8,128)} %reshape.379) | data formatting | bytes 8388608 | tf_op jit(solution)/shard_map/reshape | solution.py:72
  87.7 25.4 %all-to-all-done = f32[8,4,32,1024]{3,2,1,0:T(8,128)} async-done(((f32[8,4,32,1024]{3,2,1,0:T(8,128)}), f32[8,4,32,1024]{3,2,1,0:T(8,128)}, u32[]{:S(2)}, u32[]{:S(2)}) %all-to-all-start) | async-done | bytes 4194336 | tf_op jit(solution)/shard_map/all_to_all | solution.py:73
  123.1 89.2 %all-to-all-done.1 = f32[8,4,32,1024]{3,2,1,0:T(8,128)} async-done(((f32[8,4,32,1024]{3,2,1,0:T(8,128)}), f32[8,4,32,1024]{3,2,1,0:T(8,128)}, u32[]{:S(2)}, u32[]{:S(2)}) %all-to-all-start.1) | async-done | bytes 4194336 | tf_op jit(solution)/shard_map/all_to_all | solution.py:73
  227.6 5.6 fusion.51
  235.8 85.7 %all-to-all-done.2 = f32[8,4,32,1024]{3,2,1,0:T(8,128)} async-done(((f32[8,4,32,1024]{3,2,1,0:T(8,128)}), f32[8,4,32,1024]{3,2,1,0:T(8,128)}, u32[]{:S(2)}, u32[]{:S(2)}) %all-to-all-start.2) | async-done | bytes 4194336 | tf_op jit(solution)/shard_map/all_to_all | solution.py:78
  328.4 6.6 %copy.126 = f32[4,32,8,1024]{3,2,1,0:T(8,128)} copy(f32[4,32,8,1024]{3,1,0,2:T(8,128)} %bitcast.15) | data formatting | bytes 8388608 | tf_op jit(solution)/shard_map/transpose | solution.py:81
  338.1 5.2 reshape.383
  362.9 5.4 copy.128
  372.8 8.6 %fusion.21 = f32[128,16,512]{2,1,0:T(8,128)S(1)} fusion(f32[128,16,512]{2,1,0:T(8,128)} %dot_general.84, f32[512,512]{1,0:T(8,128)S(1)} %convolution_multiply_fusion), kind=kOutput, calls=%fused_computation.37 | convolution fusion | flops 6442450944 | bytes 9437184 | tf_op jit(solution)/shard_map/dot_general | solution.py:93
  385.6 9.5 %fusion.8 = f32[4,32,16,512]{3,2,1,0:T(8,128)} fusion(f32[1,32,16,512]{3,2,1,0:T(8,128)S(1)} %collective-permute-done.2, f32[3,32,16,512]{3,2,1,0:T(8,128)S(1)} %copy-done.10, f32[3,32,16,512]{3,2,1,0:T(8,128)S(1)} %slice-done, f32[1,32,16,512]{3,2,1,0:T(8,128)S(1)} %collective-permute-done.3, f32[4,32,16,512]{3,2,1,0:T(8,128)S(1)} %copy-done.4, ...), kind=kOutput, calls=%fused_computation.13 | convolution fusion | flops 6451888128 | bytes 22094016 | tf_op jit(solution)/shard_map/dot_general | solution.py:105
  395.1 25.2 %all-to-all-done.3 = f32[8,4,32,1024]{3,2,1,0:T(8,128)} async-done(((f32[8,4,32,1024]{3,2,1,0:T(8,128)}), f32[8,4,32,1024]{3,2,1,0:T(8,128)}, u32[]{:S(2)}, u32[]{:S(2)}) %all-to-all-start.3) | async-done | bytes 4194336 | tf_op jit(solution)/shard_map/all_to_all | solution.py:78
  420.3 6.6 %copy.131 = f32[4,32,8,1024]{3,2,1,0:T(8,128)} copy(f32[4,32,8,1024]{3,1,0,2:T(8,128)} %bitcast.22) | data formatting | bytes 8388608 | tf_op jit(solution)/shard_map/transpose | solution.py:81
  431.8 6.3 subtract_multiply_fusion
  449.9 13.8 %all-to-all-done.4 = f32[8,4,32,128]{3,2,1,0:T(8,128)S(1)} async-done(((f32[8,4,32,128]{3,2,1,0:T(8,128)}), f32[8,4,32,128]{3,2,1,0:T(8,128)S(1)}, u32[]{:S(2)}, u32[]{:S(2)}) %all-to-all-start.4) | async-done | bytes 524320 | tf_op jit(solution)/shard_map/all_to_all | solution.py:190
  552.0 16.8 %all-to-all-done.7 = f32[8,4,32,256]{3,2,1,0:T(8,128)S(1)} async-done(((f32[8,4,32,256]{3,2,1,0:T(8,128)}), f32[8,4,32,256]{3,2,1,0:T(8,128)S(1)}, u32[]{:S(2)}, u32[]{:S(2)}) %all-to-all-start.7) | async-done | bytes 1048608 | tf_op jit(solution)/shard_map/all_to_all | solution.py:190
  601.3 6.0 collective-permute-done.26
  (303 shorter events, 268.6 us)
Async XLA Ops:
  12.6 100.6 %all-to-all-start = ((f32[8,4,32,1024]{3,2,1,0:T(8,128)}), f32[8,4,32,1024]{3,2,1,0:T(8,128)}, u32[]{:S(2)}, u32[]{:S(2)}) async-start(f32[8,4,32,1024]{3,2,1,0:T(8,128)} %copy.120), calls=%async_computation | async-start | bytes 8388608 | tf_op jit(solution)/shard_map/all_to_all | solution.py:73
  21.3 42.8 %collective-permute-start = (f32[1,32,16,512]{3,2,1,0:T(8,128)}, f32[1,32,16,512]{3,2,1,0:T(8,128)S(1)}, u32[]{:S(2)}, u32[]{:S(2)}) collective-permute-start(f32[1,32,16,512]{3,2,1,0:T(8,128)} %slice.217), channel_id=1, source_target_pairs={{8,0},{16,8},{24,16},{9,1},{17,9},{25,17},{10,2},{18,10},{26,18},{... | collective-permute-start | bytes 3145736 | tf_op jit(solution)/shard_map/ppermute | solution.py:13
  26.8 37.4 %collective-permute-start.1 = (f32[1,32,16,512]{3,2,1,0:T(8,128)}, f32[1,32,16,512]{3,2,1,0:T(8,128)S(1)}, u32[]{:S(2)}, u32[]{:S(2)}) collective-permute-start(f32[1,32,16,512]{3,2,1,0:T(8,128)} %slice.286), channel_id=1, source_target_pairs={{0,8},{8,16},{16,24},{1,9},{9,17},{17,25},{2,10},{10,18},{18,26},{... | collective-permute-start | bytes 3145736 | tf_op jit(solution)/shard_map/ppermute | solution.py:13
  113.1 99.1 %all-to-all-start.1 = ((f32[8,4,32,1024]{3,2,1,0:T(8,128)}), f32[8,4,32,1024]{3,2,1,0:T(8,128)}, u32[]{:S(2)}, u32[]{:S(2)}) async-start(f32[8,4,32,1024]{3,2,1,0:T(8,128)} %bitcast.401), calls=%async_computation.1 | async-start | bytes 8388608 | tf_op jit(solution)/shard_map/all_to_all | solution.py:73
  223.0 98.6 %all-to-all-start.2 = ((f32[8,4,32,1024]{3,2,1,0:T(8,128)}), f32[8,4,32,1024]{3,2,1,0:T(8,128)}, u32[]{:S(2)}, u32[]{:S(2)}) async-start(f32[8,4,32,1024]{3,2,1,0:T(8,128)} %bitcast.402), calls=%async_computation.2 | async-start | bytes 8388608 | tf_op jit(solution)/shard_map/all_to_all | solution.py:78
  321.6 98.7 %all-to-all-start.3 = ((f32[8,4,32,1024]{3,2,1,0:T(8,128)}), f32[8,4,32,1024]{3,2,1,0:T(8,128)}, u32[]{:S(2)}, u32[]{:S(2)}) async-start(f32[8,4,32,1024]{3,2,1,0:T(8,128)} %bitcast.400), calls=%async_computation.3 | async-start | bytes 8388608 | tf_op jit(solution)/shard_map/all_to_all | solution.py:78
  336.8 48.7 %collective-permute-start.2 = (f32[1,32,16,512]{3,2,1,0:T(8,128)}, f32[1,32,16,512]{3,2,1,0:T(8,128)S(1)}, u32[]{:S(2)}, u32[]{:S(2)}) collective-permute-start(f32[1,32,16,512]{3,2,1,0:T(8,128)} %slice.223), channel_id=1, source_target_pairs={{8,0},{16,8},{24,16},{9,1},{17,9},{25,17},{10,2},{18,10},{26,18},{... | collective-permute-start | bytes 3145736 | tf_op jit(solution)/shard_map/ppermute | solution.py:13
  349.2 36.4 %collective-permute-start.3 = (f32[1,32,16,512]{3,2,1,0:T(8,128)}, f32[1,32,16,512]{3,2,1,0:T(8,128)S(1)}, u32[]{:S(2)}, u32[]{:S(2)}) collective-permute-start(f32[1,32,16,512]{3,2,1,0:T(8,128)} %slice.290), channel_id=1, source_target_pairs={{0,8},{8,16},{16,24},{1,9},{9,17},{17,25},{2,10},{10,18},{18,26},{... | collective-permute-start | bytes 3145736 | tf_op jit(solution)/shard_map/ppermute | solution.py:13
  444.5 19.2 %all-to-all-start.4 = ((f32[8,4,32,128]{3,2,1,0:T(8,128)}), f32[8,4,32,128]{3,2,1,0:T(8,128)S(1)}, u32[]{:S(2)}, u32[]{:S(2)}) async-start(f32[8,4,32,128]{3,2,1,0:T(8,128)} %reshape.387), calls=%async_computation.4 | async-start | bytes 1048576 | tf_op jit(solution)/shard_map/all_to_all | solution.py:190
  468.3 18.8 %all-to-all-start.5 = ((f32[8,4,32,128]{3,2,1,0:T(8,128)}), f32[8,4,32,128]{3,2,1,0:T(8,128)S(1)}, u32[]{:S(2)}, u32[]{:S(2)}) async-start(f32[8,4,32,128]{3,2,1,0:T(8,128)} %reshape.392), calls=%async_computation.5 | async-start | bytes 1048576 | tf_op jit(solution)/shard_map/all_to_all | solution.py:190
  495.0 30.1 %all-to-all-start.6 = ((f32[8,4,32,256]{3,2,1,0:T(8,128)}), f32[8,4,32,256]{3,2,1,0:T(8,128)S(1)}, u32[]{:S(2)}, u32[]{:S(2)}) async-start(f32[8,4,32,256]{3,2,1,0:T(8,128)} %reshape.397), calls=%async_computation.6 | async-start | bytes 2097152 | tf_op jit(solution)/shard_map/all_to_all | solution.py:190
  527.1 15.2 %collective-permute-start.18 = (f32[4,64,256]{2,1,0:T(8,128)}, f32[4,64,256]{2,1,0:T(8,128)S(1)}, u32[]{:S(2)}, u32[]{:S(2)}) collective-permute-start(f32[4,64,256]{2,1,0:T(8,128)} %get-tuple-element.53), channel_id=1, source_target_pairs={{0,24},{8,0},{16,8},{24,16},{1,25},{9,1},{17,9},{25,17},{2,26},{10... | collective-permute-start | bytes 786440 | tf_op jit(solution)/shard_map/ppermute | solution.py:150
  529.5 13.3 %collective-permute-start.17 = (f32[4,64,256]{2,1,0:T(8,128)S(1)}, f32[4,64,256]{2,1,0:T(8,128)}, u32[]{:S(2)}, u32[]{:S(2)}) collective-permute-start(f32[4,64,256]{2,1,0:T(8,128)S(1)} %get-tuple-element.54), channel_id=1, source_target_pairs={{0,16},{8,24},{16,0},{24,8},{1,17},{9,25},{17,1},{25,9},{2,18},{10... | collective-permute-start | bytes 786440 | tf_op jit(solution)/shard_map/ppermute | solution.py:150
  530.1 12.8 %collective-permute-start.16 = (f32[4,64,256]{2,1,0:T(8,128)S(1)}, f32[4,64,256]{2,1,0:T(8,128)}, u32[]{:S(2)}, u32[]{:S(2)}) collective-permute-start(f32[4,64,256]{2,1,0:T(8,128)S(1)} %get-tuple-element.55), channel_id=1, source_target_pairs={{0,8},{8,16},{16,24},{24,0},{1,9},{9,17},{17,25},{25,1},{2,10},{10... | collective-permute-start | bytes 786440 | tf_op jit(solution)/shard_map/ppermute | solution.py:150
  538.7 30.1 %all-to-all-start.7 = ((f32[8,4,32,256]{3,2,1,0:T(8,128)}), f32[8,4,32,256]{3,2,1,0:T(8,128)S(1)}, u32[]{:S(2)}, u32[]{:S(2)}) async-start(f32[8,4,32,256]{3,2,1,0:T(8,128)} %reshape.402), calls=%async_computation.7 | async-start | bytes 2097152 | tf_op jit(solution)/shard_map/all_to_all | solution.py:190
  546.6 29.5 %collective-permute-start.19 = (f32[4,64,256]{2,1,0:T(8,128)}, f32[4,64,256]{2,1,0:T(8,128)S(1)}, u32[]{:S(2)}, u32[]{:S(2)}) collective-permute-start(f32[4,64,256]{2,1,0:T(8,128)} %bitcast.382), channel_id=1, source_target_pairs={{0,24},{8,0},{16,8},{24,16},{1,25},{9,1},{17,9},{25,17},{2,26},{10... | collective-permute-start | bytes 786440 | tf_op jit(solution)/shard_map/ppermute | solution.py:150
  548.4 27.7 %collective-permute-start.20 = (f32[4,64,256]{2,1,0:T(8,128)S(1)}, f32[4,64,256]{2,1,0:T(8,128)S(1)}, u32[]{:S(2)}, u32[]{:S(2)}) collective-permute-start(f32[4,64,256]{2,1,0:T(8,128)S(1)} %bitcast.446), channel_id=1, source_target_pairs={{0,16},{8,24},{16,0},{24,8},{1,17},{9,25},{17,1},{25,9},{2,18},{10... | collective-permute-start | bytes 786440 | tf_op jit(solution)/shard_map/ppermute | solution.py:150
  552.0 24.1 %collective-permute-start.21 = (f32[4,64,256]{2,1,0:T(8,128)}, f32[4,64,256]{2,1,0:T(8,128)S(1)}, u32[]{:S(2)}, u32[]{:S(2)}) collective-permute-start(f32[4,64,256]{2,1,0:T(8,128)} %bitcast.380), channel_id=1, source_target_pairs={{0,8},{8,16},{16,24},{24,0},{1,9},{9,17},{17,25},{25,1},{2,10},{10... | collective-permute-start | bytes 786440 | tf_op jit(solution)/shard_map/ppermute | solution.py:150
  570.9 12.4 %collective-permute-start.24 = (f32[4,64,256]{2,1,0:T(8,128)}, f32[4,64,256]{2,1,0:T(8,128)}, u32[]{:S(2)}, u32[]{:S(2)}) collective-permute-start(f32[4,64,256]{2,1,0:T(8,128)} %get-tuple-element.41), channel_id=1, source_target_pairs={{0,24},{8,0},{16,8},{24,16},{1,25},{9,1},{17,9},{25,17},{2,26},{10... | collective-permute-start | bytes 786440 | tf_op jit(solution)/shard_map/ppermute | solution.py:150
  573.2 14.6 %collective-permute-start.23 = (f32[4,64,256]{2,1,0:T(8,128)}, f32[4,64,256]{2,1,0:T(8,128)}, u32[]{:S(2)}, u32[]{:S(2)}) collective-permute-start(f32[4,64,256]{2,1,0:T(8,128)} %get-tuple-element.42), channel_id=1, source_target_pairs={{0,16},{8,24},{16,0},{24,8},{1,17},{9,25},{17,1},{25,9},{2,18},{10... | collective-permute-start | bytes 786440 | tf_op jit(solution)/shard_map/ppermute | solution.py:150
  576.1 11.8 %collective-permute-start.22 = (f32[4,64,256]{2,1,0:T(8,128)}, f32[4,64,256]{2,1,0:T(8,128)}, u32[]{:S(2)}, u32[]{:S(2)}) collective-permute-start(f32[4,64,256]{2,1,0:T(8,128)} %get-tuple-element.43), channel_id=1, source_target_pairs={{0,8},{8,16},{16,24},{24,0},{1,9},{9,17},{17,25},{25,1},{2,10},{10... | collective-permute-start | bytes 786440 | tf_op jit(solution)/shard_map/ppermute | solution.py:150
  579.6 29.4 %all-to-all-start.8 = ((f32[8,4,32,128]{3,2,1,0:T(8,128)}), f32[8,4,32,128]{3,2,1,0:T(8,128)S(1)}, u32[]{:S(2)}, u32[]{:S(2)}) async-start(f32[8,4,32,128]{3,2,1,0:T(8,128)} %reshape.407), calls=%async_computation.8 | async-start | bytes 1048576 | tf_op jit(solution)/shard_map/all_to_all | solution.py:190
  594.7 12.6 %collective-permute-start.26 = (f32[4,64,256]{2,1,0:T(8,128)}, f32[4,64,256]{2,1,0:T(8,128)}, u32[]{:S(2)}, u32[]{:S(2)}) collective-permute-start(f32[4,64,256]{2,1,0:T(8,128)} %bitcast.378), channel_id=1, source_target_pairs={{0,16},{8,24},{16,0},{24,8},{1,17},{9,25},{17,1},{25,9},{2,18},{10... | collective-permute-start | bytes 786440 | tf_op jit(solution)/shard_map/ppermute | solution.py:150
  615.9 18.8 %all-to-all-start.9 = ((f32[8,4,32,128]{3,2,1,0:T(8,128)}), f32[8,4,32,128]{3,2,1,0:T(8,128)S(1)}, u32[]{:S(2)}, u32[]{:S(2)}) async-start(f32[8,4,32,128]{3,2,1,0:T(8,128)} %reshape.412), calls=%async_computation.9 | async-start | bytes 1048576 | tf_op jit(solution)/shard_map/all_to_all | solution.py:190
  (59 other events, 597.2 us)
